TPU v7x, 512 devices: a whole 4x4x16 slice. The times are simulated.
512 devices in a mesh: wide: 128 (over y, z, core), narrow: 4 (over x).
Axes of the slice: x: 4, y: 4, z: 16, core: 2. Of those that a mesh axis runs over, the one named last changes fastest.
Arguments:
- raw_echo: bfloat16 [2, 4, 1024, 16384], P(None, 'narrow', 'wide'), may hold values from -6 to 6
- range_replica: bfloat16 [2, 4096], replicated, may hold values from -0.0625 to 0.0625
- interp_weight: float32 [8, 1024], replicated, may hold values from -2.5 to 2.5
- band_offset: int32 [16384], P('wide'), may hold values from 0 to 24, as said below
- azimuth_rate: float32 [16384], P('wide'), may hold values from 0.01 to 0.1
- tile_owner: int32 [4, 16], replicated, may hold values from 0 to 3, as said below
Outputs:
- tile_mean: float32 [4, 64, 16384], P('narrow', None, 'wide')
Inputs may be any that keep to these rules, and one draw needn't show every extreme that they name: band_offset reaches 24 in every draw. `tile_owner`: every tile owns at least one block of every group. One tile, the same for every group, owns exactly 8 blocks of every group; no tile owns more than 8 blocks of one group.
All inputs are finite; a program needn't handle non-finite values.
Results may differ from a plain program's by a relative error of at most 0.011.
Values may be sent and summed in bfloat16 or wider, within the bound.
No kernel may reach another device: no remote copies, remote signals or barrier semaphores. Data moves between devices by JAX's collectives and lax.ppermute only.
A program may use at most 64 MiB of HBM per device.

v0:
```python
import math

import jax
import jax.numpy as jnp
from jax import lax
from jax.sharding import PartitionSpec as P

RSPLIT = 128
PUL_DEV = 8
CAP = 8
HALO = 31


def passed_along(shard, axis, by):
    devices = lax.axis_size(axis)
    pairs = [(i, i + by) for i in range(devices) if 0 <= i + by < devices]
    return lax.ppermute(shard, axis, pairs)


def make_table(size, sign):
    index = jnp.arange(size, dtype=jnp.int32)
    product = index[:, None] * index[None, :] % size
    angle = sign * 2.0 * math.pi / size * product.astype(jnp.float32)
    norm = 1.0 / math.sqrt(size)
    return (
        (jnp.cos(angle) * norm).astype(jnp.bfloat16),
        (jnp.sin(angle) * norm).astype(jnp.bfloat16),
    )


def make_twiddle(first, second, sign):
    heads = jnp.arange(first, dtype=jnp.int32)
    tails = jnp.arange(second, dtype=jnp.int32)
    product = heads[:, None] * tails[None, :] % (first * second)
    angle = sign * 2.0 * math.pi / (first * second) * product.astype(jnp.float32)
    return (jnp.cos(angle), jnp.sin(angle))


def range_transform(real_part, imag_part, first, sign):
    count = real_part.shape[0]
    length = real_part.shape[1]
    second = length // first
    head_cos, head_sin = make_table(first, sign)
    tail_cos, tail_sin = make_table(second, sign)
    twist_cos, twist_sin = make_twiddle(first, second, sign)
    split_real = real_part.reshape(count, first, second)
    split_imag = imag_part.reshape(count, first, second)

    def section_one(table, values):
        return jnp.einsum("kn,pnm->pkm", table, values, preferred_element_type=jnp.float32)

    mid_real = section_one(head_cos, split_real) - section_one(head_sin, split_imag)
    mid_imag = section_one(head_cos, split_imag) + section_one(head_sin, split_real)
    turn_real = (mid_real * twist_cos - mid_imag * twist_sin).astype(jnp.bfloat16)
    turn_imag = (mid_real * twist_sin + mid_imag * twist_cos).astype(jnp.bfloat16)

    def section_two(table, values):
        return jnp.einsum("pam,km->pka", values, table, preferred_element_type=jnp.float32)

    out_real = section_two(tail_cos, turn_real) - section_two(tail_sin, turn_imag)
    out_imag = section_two(tail_cos, turn_imag) + section_two(tail_sin, turn_real)
    return (out_real.reshape(count, length), out_imag.reshape(count, length))


def pulse_transform(real_part, imag_part, first, sign):
    length = real_part.shape[0]
    width = real_part.shape[1]
    second = length // first
    head_cos, head_sin = make_table(first, sign)
    tail_cos, tail_sin = make_table(second, sign)
    twist_cos, twist_sin = make_twiddle(first, second, sign)
    twist_cos = twist_cos[:, :, None]
    twist_sin = twist_sin[:, :, None]
    split_real = real_part.reshape(first, second, width)
    split_imag = imag_part.reshape(first, second, width)

    def section_one(table, values):
        return jnp.einsum("kn,nmc->kmc", table, values, preferred_element_type=jnp.float32)

    mid_real = section_one(head_cos, split_real) - section_one(head_sin, split_imag)
    mid_imag = section_one(head_cos, split_imag) + section_one(head_sin, split_real)
    turn_real = (mid_real * twist_cos - mid_imag * twist_sin).astype(jnp.bfloat16)
    turn_imag = (mid_real * twist_sin + mid_imag * twist_cos).astype(jnp.bfloat16)

    def section_two(table, values):
        return jnp.einsum("kmc,jm->jkc", values, table, preferred_element_type=jnp.float32)

    out_real = section_two(tail_cos, turn_real) - section_two(tail_sin, turn_imag)
    out_imag = section_two(tail_cos, turn_imag) + section_two(tail_sin, turn_real)
    return (out_real.reshape(length, width), out_imag.reshape(length, width))


def azimuth_spectra(values):
    first_real, first_imag = pulse_transform(values[0, :, 0], values[1, :, 0], PUL_DEV, -1)
    return jnp.stack([first_real.astype(jnp.bfloat16), first_imag.astype(jnp.bfloat16)])[
        :, :, None, :
    ]


def per_device(raw_echo, range_replica, interp_weight, band_offset, azimuth_rate, tile_owner):
    echo = raw_echo[:, 0]
    length = echo.shape[2]
    padded = jnp.pad(range_replica, ((0, 0), (0, length - range_replica.shape[1])))
    replica_real, replica_imag = range_transform(padded[0:1], padded[1:2], RSPLIT, -1)
    scale = math.sqrt(length)
    replica_real = replica_real[0] * scale
    replica_imag = replica_imag[0] * scale
    spec_real, spec_imag = range_transform(echo[0], echo[1], RSPLIT, -1)
    match_real = (spec_real * replica_real + spec_imag * replica_imag).astype(jnp.bfloat16)
    match_imag = (spec_imag * replica_real - spec_real * replica_imag).astype(jnp.bfloat16)
    comp_real, comp_imag = range_transform(match_real, match_imag, RSPLIT, 1)
    compressed = jnp.stack([comp_real.astype(jnp.bfloat16), comp_imag.astype(jnp.bfloat16)])
    devices = lax.axis_size("wide")
    width = length // devices
    local_pulses = compressed.shape[1]
    split_bins = compressed.reshape(2, local_pulses, devices, width)
    doppler = azimuth_spectra(
        lax.all_to_all(split_bins, "wide", split_axis=2, concat_axis=1, tiled=True)
    )[:, :, 0]
    rim = passed_along(doppler[:, :, :HALO], "wide", -1)
    extended = jnp.concatenate([doppler, rim], axis=2)
    pulses = extended.shape[1]
    columns = jnp.arange(width + HALO, dtype=jnp.int32)
    bins = jnp.arange(width, dtype=jnp.int32) + band_offset
    moved_real = jnp.zeros((pulses, width), jnp.float32)
    moved_imag = jnp.zeros((pulses, width), jnp.float32)
    for tap_index in range(interp_weight.shape[0]):
        select = (columns[:, None] == (bins + tap_index)[None, :]).astype(jnp.bfloat16)
        picked = jnp.einsum("xpc,cr->xpr", extended, select, preferred_element_type=jnp.float32)
        weight = interp_weight[tap_index][:, None]
        moved_real = moved_real + weight * picked[0]
        moved_imag = moved_imag + weight * picked[1]
    freq = jnp.arange(pulses, dtype=jnp.int32)
    shifted = ((freq + pulses // 2) % pulses - pulses // 2).astype(jnp.float32) / pulses
    phase = math.pi * (shifted * shifted)[:, None] / azimuth_rate[None, :]
    phase_cos = jnp.cos(phase)
    phase_sin = jnp.sin(phase)
    focus_real = (moved_real * phase_cos - moved_imag * phase_sin).astype(jnp.bfloat16)
    focus_imag = (moved_real * phase_sin + moved_imag * phase_cos).astype(jnp.bfloat16)
    image_real, image_imag = pulse_transform(focus_real, focus_imag, PUL_DEV, 1)
    intensity = (image_real * image_real + image_imag * image_imag).astype(jnp.bfloat16)
    block_count = tile_owner.shape[1]
    block_rows = pulses // block_count
    blocks = intensity.reshape(block_count, block_rows, width)
    tiles = lax.axis_size("narrow")
    group = lax.axis_index("narrow")
    tile_ids = jnp.arange(tiles, dtype=jnp.int32)
    own_row = lax.dynamic_slice_in_dim(tile_owner, group, 1, 0)[0]
    member = (own_row[None, :] == tile_ids[:, None]).astype(jnp.int32)
    counts = jnp.sum(
        (tile_owner[:, :, None] == tile_ids[None, None, :]).astype(jnp.int32), axis=(0, 1)
    )
    own_count = jnp.sum(jnp.where(tile_ids == group, counts, 0)).astype(jnp.float32)
    rank = jnp.cumsum(member, axis=1) - 1
    slots = jnp.arange(CAP, dtype=jnp.int32)
    select_slots = ((member[:, None, :] == 1) & (rank[:, None, :] == slots[None, :, None])).astype(
        jnp.bfloat16
    )
    outgoing = jnp.einsum(
        "tsb,bir->tsir", select_slots, blocks, preferred_element_type=jnp.float32
    ).astype(jnp.bfloat16)
    incoming = lax.all_to_all(outgoing, "narrow", split_axis=0, concat_axis=0, tiled=True)
    summed = jnp.sum(incoming, axis=(0, 1), dtype=jnp.float32)[None]
    return summed / own_count


def solution(mesh):
    return jax.shard_map(
        per_device,
        mesh=mesh,
        in_specs=(P(None, "narrow", "wide", None), P(), P(), P("wide"), P("wide"), P()),
        out_specs=P("narrow", None, "wide"),
        check_vma=False,
    )
```

profile of v0, /device:TPU:1, one launch (start us, length us, event | category | flops | bytes accessed | tf_op | source)
XLA Modules:
  0.0 111.3 jit_solution(6334069500444813462)
XLA Ops:
  0.0 0.3 multiply_sine_fusion.1
  0.5 0.3 multiply_sine_fusion
  0.8 1.1 slice_bitcast_fusion.1
  1.9 0.4 fusion.34
  2.3 0.4 fusion.38
  2.8 0.5 convolution_add_fusion.7
  3.2 0.5 fusion.31
  3.8 0.4 fusion.129
  4.2 0.4 fusion.131
  4.6 0.4 convolution_add_fusion.6
  5.2 0.4 fusion.115
  5.6 0.4 fusion.119
  6.0 0.4 fusion.14
  6.4 0.6 fusion.112
  7.0 0.4 fusion.137
  7.4 0.4 fusion.138
  7.8 0.4 fusion.12
  8.1 0.4 fusion.13
  8.5 0.5 fusion.32
  9.0 0.5 fusion.153
  9.5 0.5 fusion.151
  10.0 0.5 fusion.3
  10.6 0.6 subtract_convert_fusion.3
  11.2 0.4 fusion.149
  11.6 0.4 fusion.147
  12.1 0.4 fusion.11
  12.5 0.4 fusion.10
  13.0 1.1 %copy.222 = bf16[2,8,128,128]{3,1,0,2:T(8,128)(2,1)} copy(bf16[2,8,128,128]{3,2,1,0:T(8,128)(2,1)S(1)} %pad_maximum_fusion.1) | data formatting | bytes 1048576 | tf_op jit(solution)/shard_map/stack | solution.py:112
  14.2 20.7 %all-to-all-start = ((bf16[2,8,128,128]{3,1,0,2:T(8,128)(2,1)}), bf16[2,8,128,128]{3,1,0,2:T(8,128)(2,1)S(1)}, u32[]{:S(2)}, u32[]{:S(2)}) async-start(bf16[2,8,128,128]{3,1,0,2:T(8,128)(2,1)} %copy.222), calls=%async_computation | async-start | bytes 1048576 | tf_op jit(solution)/shard_map/all_to_all | solution.py:118
  36.7 31.4 %all-to-all-done = bf16[2,8,128,128]{3,1,0,2:T(8,128)(2,1)S(1)} async-done(((bf16[2,8,128,128]{3,1,0,2:T(8,128)(2,1)}), bf16[2,8,128,128]{3,1,0,2:T(8,128)(2,1)S(1)}, u32[]{:S(2)}, u32[]{:S(2)}) %all-to-all-start) | async-done | bytes 524320 | tf_op jit(solution)/shard_map/all_to_all | solution.py:118
  68.1 0.3 fusion.62
  68.4 0.3 fusion.58
  68.7 0.3 convolution_subtract_fusion.1
  69.0 0.5 subtract_convert_fusion.2
  69.5 0.4 fusion.56
  69.9 0.4 fusion.52
  70.4 0.5 fusion.8
  71.2 0.5 fusion.9
  72.0 3.1 %collective-permute-start = (bf16[2,1024,31]{1,2,0:T(8,128)(2,1)S(1)}, bf16[2,1024,31]{1,2,0:T(8,128)(2,1)S(1)}, u32[]{:S(2)}, u32[]{:S(2)}) collective-permute-start(bf16[2,1024,31]{1,2,0:T(8,128)(2,1)S(1)} %pad_maximum_fusion.2), channel_id=1, source_target_pairs={{4,0},{8,4},{12,8},{16,12},{20,16},{24,20},{28,24},{32,28},{36,32}... | collective-permute-start | bytes 380936 | tf_op jit(solution)/shard_map/ppermute | solution.py:17
  75.1 4.3 %collective-permute-done = bf16[2,1024,31]{1,2,0:T(8,128)(2,1)S(1)} collective-permute-done((bf16[2,1024,31]{1,2,0:T(8,128)(2,1)S(1)}, bf16[2,1024,31]{1,2,0:T(8,128)(2,1)S(1)}, u32[]{:S(2)}, u32[]{:S(2)}) %collective-permute-start) | collective-permute-done | bytes 127008 | tf_op jit(solution)/shard_map/ppermute | solution.py:17
  79.5 0.5 fusion.65
  80.0 0.5 fusion.68
  80.6 0.5 fusion.71
  81.1 0.5 fusion.74
  81.7 0.5 fusion.77
  82.3 0.5 fusion.80
  82.8 0.5 fusion.83
  83.4 0.5 fusion.86
  84.0 0.6 copy-done.2
  84.6 7.7 %subtract_convert_fusion.1 = (bf16[8,128,128]{2,0,1:T(8,128)(2,1)S(1)}, f32[8,128,128]{2,0,1:T(8,128)S(1)}, f32[8,128,128]{2,0,1:T(8,128)S(1)}) fusion(f32[128]{0:T(128)S(1)} %copy-done.2, f32[8,128]{0,1:T(8,128)S(1)} %copy.253, f32[8,128,128]{2,1,0:T(8,128)S(1)} %bitcast.245, f32[8,128]{0,1:T(8,128)S(1)} %copy.251, f32[8,128,128]{2,1,0:T(8,128)S(1)} %bitcast.243, ...), kind=kLoop, calls=%fused_computation.74 | loop fusion | flops 4587520 | bytes 9736704 | tf_op jit(solution)/shard_map/convert_element_type | solution.py:138
  92.3 0.3 fusion.188
  92.5 2.5 %add_convert_fusion.1 = bf16[8,128,128]{2,0,1:T(8,128)(2,1)S(1)} fusion(f32[8,128,128]{2,0,1:T(8,128)S(1)} %get-tuple-element.9, f32[8,128,128]{2,0,1:T(8,128)S(1)} %get-tuple-element.8, f32[128]{0:T(128)S(1)} %copy-done.2, f32[8,128]{0,1:T(8,128)S(1)} %copy.253), kind=kLoop, calls=%fused_computation.73 | loop fusion | flops 655360 | bytes 1315328 | tf_op jit(solution)/shard_map/convert_element_type | solution.py:139
  95.0 0.3 fusion.186
  95.3 0.3 convolution_subtract_fusion
  95.5 0.4 subtract_convert_fusion
  95.9 0.4 fusion.46
  96.4 0.4 fusion.50
  96.9 0.5 fusion
  97.3 0.5 fusion.5
  98.0 1.1 convolution_convert_fusion
  99.1 4.0 %all-to-all-start.1 = ((bf16[4,8,64,128]{3,1,2,0:T(8,128)(2,1)}), bf16[4,8,64,128]{3,1,2,0:T(8,128)(2,1)S(1)}, u32[]{:S(2)}, u32[]{:S(2)}) async-start(bf16[4,8,64,128]{3,1,2,0:T(8,128)(2,1)} %convolution_convert_fusion), calls=%async_computation.1 | async-start | bytes 1048576 | tf_op jit(solution)/shard_map/all_to_all | solution.py:162
  103.2 0.6 fusion.191
  104.5 6.1 %all-to-all-done.1 = bf16[4,8,64,128]{3,1,2,0:T(8,128)(2,1)S(1)} async-done(((bf16[4,8,64,128]{3,1,2,0:T(8,128)(2,1)}), bf16[4,8,64,128]{3,1,2,0:T(8,128)(2,1)S(1)}, u32[]{:S(2)}, u32[]{:S(2)}) %all-to-all-start.1) | async-done | bytes 524320 | tf_op jit(solution)/shard_map/all_to_all | solution.py:162
  110.7 0.6 divide_bitcast_fusion
  (56 shorter events, 4.2 us)
Async XLA Ops:
  4.2 0.9 copy-start.1
  13.0 22.2 %copy-start = (f32[8,1024]{1,0:T(8,128)S(1)}, f32[8,1024]{1,0:T(8,128)}, u32[]{:S(2)}) copy-start(f32[8,1024]{1,0:T(8,128)} %param.8) | copy-start | bytes 98308
  14.1 22.3 %copy-start.3 = (s32[4,16]{1,0:T(4,128)S(1)}, s32[4,16]{1,0:T(4,128)}, u32[]{:S(2)}) copy-start(s32[4,16]{1,0:T(4,128)} %param.11) | copy-start | bytes 772
  14.1 22.5 %copy-start.4 = (s32[128]{0:T(128)S(1)}, s32[128]{0:T(128)}, u32[]{:S(2)}) copy-start(s32[128]{0:T(128)} %param.9) | copy-start | bytes 1540
  14.2 53.9 %all-to-all-start = ((bf16[2,8,128,128]{3,1,0,2:T(8,128)(2,1)}), bf16[2,8,128,128]{3,1,0,2:T(8,128)(2,1)S(1)}, u32[]{:S(2)}, u32[]{:S(2)}) async-start(bf16[2,8,128,128]{3,1,0,2:T(8,128)(2,1)} %copy.222), calls=%async_computation | async-start | bytes 1048576 | tf_op jit(solution)/shard_map/all_to_all | solution.py:118
  72.0 7.4 %collective-permute-start = (bf16[2,1024,31]{1,2,0:T(8,128)(2,1)S(1)}, bf16[2,1024,31]{1,2,0:T(8,128)(2,1)S(1)}, u32[]{:S(2)}, u32[]{:S(2)}) collective-permute-start(bf16[2,1024,31]{1,2,0:T(8,128)(2,1)S(1)} %pad_maximum_fusion.2), channel_id=1, source_target_pairs={{4,0},{8,4},{12,8},{16,12},{20,16},{24,20},{28,24},{32,28},{36,32}... | collective-permute-start | bytes 380936 | tf_op jit(solution)/shard_map/ppermute | solution.py:17
  83.9 0.7 copy-start.2
  99.1 11.5 %all-to-all-start.1 = ((bf16[4,8,64,128]{3,1,2,0:T(8,128)(2,1)}), bf16[4,8,64,128]{3,1,2,0:T(8,128)(2,1)S(1)}, u32[]{:S(2)}, u32[]{:S(2)}) async-start(bf16[4,8,64,128]{3,1,2,0:T(8,128)(2,1)} %convolution_convert_fusion), calls=%async_computation.1 | async-start | bytes 1048576 | tf_op jit(solution)/shard_map/all_to_all | solution.py:162
where the time goes:
time: 112 us; the launch traced here: 111 us
  waiting for transfers between devices  41.8 us (37%)
  starting transfers between devices  27.8 us (25%)
  matrix products  21.6 us (19%)
  other arithmetic  13 us (12%)
  local copies, waits for them, and re-layouts  5.95 us (5%)
  between operations  1.22 us (1%)
    all_to_all x1, waiting for transfers between devices, per_device(): lax.all_to_all(split_bins, 'wide', split_axis=2, concat_axis=1, tiled=True)  31.4 us
    all_to_all x1, starting transfers between devices, per_device(): lax.all_to_all(split_bins, 'wide', split_axis=2, concat_axis=1, tiled=True)  20.7 us
    convert_element_type x1, other arithmetic, per_device(): (moved_real * phase_cos - moved_imag * phase_sin).astype(jnp.bfloat16)  7.7 us
    all_to_all x1, waiting for transfers between devices, per_device(): lax.all_to_all(outgoing, 'narrow', split_axis=0, concat_axis=0, tiled=True)  6.08 us
    dot_general x12, matrix products, section_one(): jnp.einsum('kn,pnm->pkm', table, values, preferred_element_type=jnp.float32)  5.55 us
    dot_general x12, matrix products, section_two(): jnp.einsum('pam,km->pka', values, table, preferred_element_type=jnp.float32)  5.02 us
    ppermute x1, waiting for transfers between devices, passed_along(): return lax.ppermute(shard, axis, pairs)  4.31 us
    all_to_all x1, starting transfers between devices, per_device(): lax.all_to_all(outgoing, 'narrow', split_axis=0, concat_axis=0, tiled=True)  4 us
  transfers between devices with their start and end apart: 3, of which 3 were waited for; matrix products, arithmetic and copies ran while one was open for 2% of the time, Pallas kernels for 0%

commit v1 on v0

--- a/solution.py
+++ b/solution.py
@@ -2,7 +2,11 @@
 
 import jax
 import jax.numpy as jnp
+import ml_dtypes
+import numpy as np
 from jax import lax
+from jax.experimental import pallas as pl
+from jax.experimental.pallas import tpu as pltpu
 from jax.sharding import PartitionSpec as P
 
 RSPLIT = 128
@@ -36,30 +40,96 @@
     return (jnp.cos(angle), jnp.sin(angle))
 
 
-def range_transform(real_part, imag_part, first, sign):
-    count = real_part.shape[0]
-    length = real_part.shape[1]
-    second = length // first
-    head_cos, head_sin = make_table(first, sign)
-    tail_cos, tail_sin = make_table(second, sign)
-    twist_cos, twist_sin = make_twiddle(first, second, sign)
-    split_real = real_part.reshape(count, first, second)
-    split_imag = imag_part.reshape(count, first, second)
-
-    def section_one(table, values):
-        return jnp.einsum("kn,pnm->pkm", table, values, preferred_element_type=jnp.float32)
-
-    mid_real = section_one(head_cos, split_real) - section_one(head_sin, split_imag)
-    mid_imag = section_one(head_cos, split_imag) + section_one(head_sin, split_real)
+def host_block_table(size, sign):
+    index = np.arange(size, dtype=np.int64)
+    product = (index[:, None] * index[None, :] % size).astype(np.float32)
+    angle = np.float32(sign * 2.0 * math.pi / size) * product
+    norm = np.float32(1.0 / math.sqrt(size))
+    cos = (np.cos(angle) * norm).astype(ml_dtypes.bfloat16)
+    sin = (np.sin(angle) * norm).astype(ml_dtypes.bfloat16)
+    top = np.concatenate([cos, -sin], axis=1)
+    bottom = np.concatenate([sin, cos], axis=1)
+    return np.concatenate([top, bottom], axis=0)
+
+
+def host_twiddle(first, second, sign):
+    heads = np.arange(first, dtype=np.int64)
+    tails = np.arange(second, dtype=np.int64)
+    product = (heads[:, None] * tails[None, :] % (first * second)).astype(np.float32)
+    angle = np.float32(sign * 2.0 * math.pi / (first * second)) * product
+    return np.stack([np.cos(angle), np.sin(angle)]).astype(np.float32)
+
+
+def square_transform(stacked, table, twiddle):
+    half = stacked.shape[0] // 2
+    mid = jnp.dot(table, stacked, preferred_element_type=jnp.float32)
+    mid_real, mid_imag = mid[:half], mid[half:]
+    twist_cos, twist_sin = twiddle[0], twiddle[1]
     turn_real = (mid_real * twist_cos - mid_imag * twist_sin).astype(jnp.bfloat16)
     turn_imag = (mid_real * twist_sin + mid_imag * twist_cos).astype(jnp.bfloat16)
-
-    def section_two(table, values):
-        return jnp.einsum("pam,km->pka", values, table, preferred_element_type=jnp.float32)
-
-    out_real = section_two(tail_cos, turn_real) - section_two(tail_sin, turn_imag)
-    out_imag = section_two(tail_cos, turn_imag) + section_two(tail_sin, turn_real)
-    return (out_real.reshape(count, length), out_imag.reshape(count, length))
+    turned = jnp.concatenate([turn_real, turn_imag], axis=1)
+    out = lax.dot_general(
+        table, turned, (((1,), (1,)), ((), ())), preferred_element_type=jnp.float32
+    )
+    return out[:half], out[half:]
+
+
+def range_kernel(echo_ref, replica_ref, fwd_ref, inv_ref, fwd_tw_ref, inv_tw_ref, out_ref, rep_ref):
+    fwd = fwd_ref[...]
+    fwd_tw = fwd_tw_ref[...]
+
+    @pl.when(pl.program_id(0) == 0)
+    def _():
+        rep_real, rep_imag = square_transform(replica_ref[...], fwd, fwd_tw)
+        rep_ref[0] = rep_real * 128.0
+        rep_ref[1] = rep_imag * 128.0
+
+    pulse = echo_ref[:, 0]
+    stacked = jnp.concatenate([pulse[0], pulse[1]], axis=0)
+    spec_real, spec_imag = square_transform(stacked, fwd, fwd_tw)
+    rep_real = rep_ref[0]
+    rep_imag = rep_ref[1]
+    match_real = (spec_real * rep_real + spec_imag * rep_imag).astype(jnp.bfloat16)
+    match_imag = (spec_imag * rep_real - spec_real * rep_imag).astype(jnp.bfloat16)
+    matched = jnp.concatenate([match_real, match_imag], axis=0)
+    comp_real, comp_imag = square_transform(matched, inv_ref[...], inv_tw_ref[...])
+    out_ref[0, 0] = comp_real.astype(jnp.bfloat16)
+    out_ref[1, 0] = comp_imag.astype(jnp.bfloat16)
+
+
+def range_compress(echo, range_replica):
+    pulses, length = echo.shape[1], echo.shape[2]
+    side = RSPLIT
+    assert length == side * side
+    padded = jnp.pad(range_replica, ((0, 0), (0, length - range_replica.shape[1])))
+    replica = padded.reshape(2 * side, side)
+    fwd = jnp.asarray(host_block_table(side, -1))
+    inv = jnp.asarray(host_block_table(side, 1))
+    fwd_tw = jnp.asarray(host_twiddle(side, side, -1))
+    inv_tw = jnp.asarray(host_twiddle(side, side, 1))
+    full = lambda shape: pl.BlockSpec(shape, lambda p: (0,) * len(shape))
+    out = pl.pallas_call(
+        range_kernel,
+        grid=(pulses,),
+        in_specs=[
+            pl.BlockSpec((2, 1, side, side), lambda p: (0, p, 0, 0)),
+            full((2 * side, side)),
+            full((2 * side, 2 * side)),
+            full((2 * side, 2 * side)),
+            full((2, side, side)),
+            full((2, side, side)),
+        ],
+        out_specs=pl.BlockSpec((2, 1, side, side), lambda p: (0, p, 0, 0)),
+        out_shape=jax.ShapeDtypeStruct((2, pulses, side, side), jnp.bfloat16),
+        scratch_shapes=[pltpu.VMEM((2, side, side), jnp.float32)],
+        compiler_params=pltpu.CompilerParams(dimension_semantics=("arbitrary",)),
+        cost_estimate=pl.CostEstimate(
+            flops=pulses * 4 * 2 * (2 * side) ** 2 * side,
+            bytes_accessed=pulses * 2 * 2 * length * 2,
+            transcendentals=0,
+        ),
+    )(echo.reshape(2, pulses, side, side), replica, fwd, inv, fwd_tw, inv_tw)
+    return out.reshape(2, pulses, length)
 
 
 def pulse_transform(real_part, imag_part, first, sign):
@@ -100,16 +170,7 @@
 def per_device(raw_echo, range_replica, interp_weight, band_offset, azimuth_rate, tile_owner):
     echo = raw_echo[:, 0]
     length = echo.shape[2]
-    padded = jnp.pad(range_replica, ((0, 0), (0, length - range_replica.shape[1])))
-    replica_real, replica_imag = range_transform(padded[0:1], padded[1:2], RSPLIT, -1)
-    scale = math.sqrt(length)
-    replica_real = replica_real[0] * scale
-    replica_imag = replica_imag[0] * scale
-    spec_real, spec_imag = range_transform(echo[0], echo[1], RSPLIT, -1)
-    match_real = (spec_real * replica_real + spec_imag * replica_imag).astype(jnp.bfloat16)
-    match_imag = (spec_imag * replica_real - spec_real * replica_imag).astype(jnp.bfloat16)
-    comp_real, comp_imag = range_transform(match_real, match_imag, RSPLIT, 1)
-    compressed = jnp.stack([comp_real.astype(jnp.bfloat16), comp_imag.astype(jnp.bfloat16)])
+    compressed = range_compress(echo, range_replica)
     devices = lax.axis_size("wide")
     width = length // devices
     local_pulses = compressed.shape[1]
@@ -130,37 +191,34 @@
         weight = interp_weight[tap_index][:, None]
         moved_real = moved_real + weight * picked[0]
         moved_imag = moved_imag + weight * picked[1]
-    freq = jnp.arange(pulses, dtype=jnp.int32)
-    shifted = ((freq + pulses // 2) % pulses - pulses // 2).astype(jnp.float32) / pulses
+    half = pulses // 2
+    freq = jnp.arange(half + 1, dtype=jnp.int32)
+    shifted = ((freq + half) % pulses - half).astype(jnp.float32) / pulses
     phase = math.pi * (shifted * shifted)[:, None] / azimuth_rate[None, :]
-    phase_cos = jnp.cos(phase)
-    phase_sin = jnp.sin(phase)
+    half_cos = jnp.cos(phase)
+    half_sin = jnp.sin(phase)
+    phase_cos = jnp.concatenate([half_cos, jnp.flip(half_cos[1:half], 0)], axis=0)
+    phase_sin = jnp.concatenate([half_sin, jnp.flip(half_sin[1:half], 0)], axis=0)
     focus_real = (moved_real * phase_cos - moved_imag * phase_sin).astype(jnp.bfloat16)
     focus_imag = (moved_real * phase_sin + moved_imag * phase_cos).astype(jnp.bfloat16)
     image_real, image_imag = pulse_transform(focus_real, focus_imag, PUL_DEV, 1)
     intensity = (image_real * image_real + image_imag * image_imag).astype(jnp.bfloat16)
     block_count = tile_owner.shape[1]
     block_rows = pulses // block_count
-    blocks = intensity.reshape(block_count, block_rows, width)
+    blocks = intensity.reshape(block_count, block_rows * width)
     tiles = lax.axis_size("narrow")
     group = lax.axis_index("narrow")
     tile_ids = jnp.arange(tiles, dtype=jnp.int32)
     own_row = lax.dynamic_slice_in_dim(tile_owner, group, 1, 0)[0]
-    member = (own_row[None, :] == tile_ids[:, None]).astype(jnp.int32)
+    member = (own_row[None, :] == tile_ids[:, None]).astype(jnp.bfloat16)
     counts = jnp.sum(
         (tile_owner[:, :, None] == tile_ids[None, None, :]).astype(jnp.int32), axis=(0, 1)
     )
     own_count = jnp.sum(jnp.where(tile_ids == group, counts, 0)).astype(jnp.float32)
-    rank = jnp.cumsum(member, axis=1) - 1
-    slots = jnp.arange(CAP, dtype=jnp.int32)
-    select_slots = ((member[:, None, :] == 1) & (rank[:, None, :] == slots[None, :, None])).astype(
-        jnp.bfloat16
-    )
-    outgoing = jnp.einsum(
-        "tsb,bir->tsir", select_slots, blocks, preferred_element_type=jnp.float32
-    ).astype(jnp.bfloat16)
-    incoming = lax.all_to_all(outgoing, "narrow", split_axis=0, concat_axis=0, tiled=True)
-    summed = jnp.sum(incoming, axis=(0, 1), dtype=jnp.float32)[None]
+    partial = jnp.dot(member, blocks, preferred_element_type=jnp.float32)
+    partial = partial.reshape(tiles, block_rows, width)
+    incoming = lax.all_to_all(partial, "narrow", split_axis=0, concat_axis=0, tiled=True)
+    summed = jnp.sum(incoming, axis=0)[None]
     return summed / own_count
 
 

time: 112 us -> 99.5 us (0.89)
  matrix products: 21.6 us -> 10.3 us
  Pallas kernels: 0 us -> 8.74 us
  other arithmetic: 13 us -> 4.34 us
  waiting for transfers between devices: 41.8 us -> 38.1 us
  local copies, waits for them, and re-layouts: 5.95 us -> 8.3 us
    dot_general x25 -> x1, matrix products: 11.7 us -> 0.16 us  [per_device(): partial = jnp.dot(member, blocks, preferred_element_type=jnp.float32)]
    pallas_call x0 -> x1, Pallas kernels: none -> 8.74 us  [range_compress(): pl.pallas_call(range_kernel, grid=(pulses,), in_specs=[pl.BlockSpec((2, 1...]
    convert_element_type x1, other arithmetic: 7.7 us -> 1.51 us  [per_device(): (moved_real * phase_cos - moved_imag * phase_sin).astype(jnp.bfloat16)]
    all_to_all x1, waiting for transfers between devices: 6.08 us -> 3.54 us  [per_device(): lax.all_to_all(partial, 'narrow', split_axis=0, concat_axis=0, tiled=True)]
    convert_element_type x1, other arithmetic: 2.47 us -> 0.11 us  [per_device(): (moved_real * phase_sin + moved_imag * phase_cos).astype(jnp.bfloat16)]
    pallas_call x0 -> x1, local copies, waits for them, and re-layouts: none -> 2.2 us  [range_compress(): pl.pallas_call(range_kernel, grid=(pulses,), in_specs=[pl.BlockSpec((2, 1...]
    another operation x1 -> x0, local copies, waits for them, and re-layouts: 1.13 us -> none  [per_device(): jnp.stack([comp_real.astype(jnp.bfloat16), comp_imag.astype(jnp.bfloat16)])]
  transfers between devices with their start and end apart: 3 -> 3, of which waited for: 3 -> 3; matrix products, arithmetic and copies ran while one was open for 2% -> 3% of each run, Pallas kernels for 0% -> 0%
where the time goes in v1:
time: 99.5 us; the launch traced here: 98.8 us
  waiting for transfers between devices  38.1 us (38%)
  starting transfers between devices  27.9 us (28%)
  matrix products  10.3 us (10%)
  Pallas kernels  8.74 us (9%)
  local copies, waits for them, and re-layouts  8.3 us (8%)
  other arithmetic  4.34 us (4%)
  between operations  1.13 us (1%)
    all_to_all x1, waiting for transfers between devices, per_device(): lax.all_to_all(split_bins, 'wide', split_axis=2, concat_axis=1, tiled=True)  30.6 us
    all_to_all x1, starting transfers between devices, per_device(): lax.all_to_all(split_bins, 'wide', split_axis=2, concat_axis=1, tiled=True)  20.6 us
    pallas_call x1, Pallas kernels, range_compress(): pl.pallas_call(range_kernel, grid=(pulses,), in_specs=[pl.BlockSpec((2, 1...  8.74 us
    ppermute x1, waiting for transfers between devices, passed_along(): return lax.ppermute(shard, axis, pairs)  4.03 us
    all_to_all x1, starting transfers between devices, per_device(): lax.all_to_all(partial, 'narrow', split_axis=0, concat_axis=0, tiled=True)  4.01 us
    dot_general x8, matrix products, per_device(): jnp.einsum('xpc,cr->xpr', extended, select, preferred_element_type=jnp.fl...  3.84 us
    dot_general x8, matrix products, section_two(): jnp.einsum('kmc,jm->jkc', values, table, preferred_element_type=jnp.float32)  3.61 us
    all_to_all x1, waiting for transfers between devices, per_device(): lax.all_to_all(partial, 'narrow', split_axis=0, concat_axis=0, tiled=True)  3.54 us
  transfers between devices with their start and end apart: 3, of which 3 were waited for; matrix products, arithmetic and copies ran while one was open for 3% of the time, Pallas kernels for 0%

profile of v1, /device:TPU:1, one launch (start us, length us, event | category | flops | bytes accessed | tf_op | source)
XLA Modules:
  0.0 98.8 jit_solution(4618021351035181387)
XLA Ops:
  0.0 2.0 %copy.192 = bf16[2,8,128,128]{3,2,1,0:T(8,128)(2,1)} copy(bf16[2,8,128,128]{3,1,2,0:T(8,128)(2,1)} %bitcast.148) | data formatting | bytes 1048576
  2.0 0.7 reshape.346.replica_ref
  2.7 8.7 %shard_map.100 = bf16[2,8,128,128]{3,2,1,0:T(8,128)(2,1)} custom-call(bf16[2,8,128,128]{3,2,1,0:T(8,128)(2,1)} %copy.192, bf16[256,128]{1,0:T(8,128)(2,1)} %reshape.346.replica_ref, bf16[256,256]{1,0:T(8,128)(2,1)} %constant.116.clone.fwd_ref, bf16[256,256]{1,0:T(8,128)(2,1)} %constant.117.clone.inv_ref, f32[2,128,128]{2,1,0:T(8,128)} %constant.118.clone.fwd_tw_ref, ...), custom_call_target="tpu_custom_call" | custom-call | flops 536870912 | bytes 1048576 | tf_op jit(solution)/shard_map/pallas_call | solution.py:111
  11.4 2.2 %copy.117 = bf16[2,8,128,128]{3,1,0,2:T(8,128)(2,1)} copy(bf16[2,8,128,128]{3,2,1,0:T(8,128)(2,1)} %shard_map.100) | data formatting | bytes 1048576 | tf_op jit(solution)/shard_map/pallas_call | solution.py:111
  13.6 20.6 %all-to-all-start = ((bf16[2,8,128,128]{3,1,0,2:T(8,128)(2,1)}), bf16[2,8,128,128]{3,1,0,2:T(8,128)(2,1)S(1)}, u32[]{:S(2)}, u32[]{:S(2)}) async-start(bf16[2,8,128,128]{3,1,0,2:T(8,128)(2,1)} %copy.117), calls=%async_computation | async-start | bytes 1048576 | tf_op jit(solution)/shard_map/all_to_all | solution.py:179
  34.2 0.1 multiply_cosine_fusion.1
  34.3 0.1 copy.121
  34.4 0.1 copy.124
  34.5 1.0 %divide_cosine_fusion = (f32[513,128]{1,0:T(8,128)S(1)}, f32[513,128]{1,0:T(8,128)S(1)}) fusion(f32[128]{0:T(128)S(1)} %copy-done.3, f32[513]{0:T(1024)S(1)} %fusion.91), kind=kLoop, calls=%fused_computation.33 | loop fusion | flops 65664 | bytes 527876 | tf_op jit(solution)/shard_map/cos | solution.py:198
  35.6 0.3 rev.7
  36.0 0.3 rev.8
  36.4 0.1 copy.135
  36.5 0.1 copy.138
  36.7 0.1 convert_reduce_fusion
  36.9 30.6 %all-to-all-done = bf16[2,8,128,128]{3,1,0,2:T(8,128)(2,1)S(1)} async-done(((bf16[2,8,128,128]{3,1,0,2:T(8,128)(2,1)}), bf16[2,8,128,128]{3,1,0,2:T(8,128)(2,1)S(1)}, u32[]{:S(2)}, u32[]{:S(2)}) %all-to-all-start) | async-done | bytes 524320 | tf_op jit(solution)/shard_map/all_to_all | solution.py:179
  67.5 0.3 fusion.31
  67.8 0.3 fusion.27
  68.1 0.3 convolution_subtract_fusion.1
  68.4 0.5 subtract_convert_fusion.2
  68.9 0.4 fusion.25
  69.3 0.4 fusion.21
  69.8 0.5 fusion.4
  70.2 0.2 copy.195
  70.4 0.1 copy.131
  70.6 0.5 fusion.5
  71.0 0.2 copy.194
  71.2 0.1 copy.132
  71.4 3.3 %collective-permute-start = (bf16[2,1024,31]{1,2,0:T(8,128)(2,1)S(1)}, bf16[2,1024,31]{1,2,0:T(8,128)(2,1)S(1)}, u32[]{:S(2)}, u32[]{:S(2)}) collective-permute-start(bf16[2,1024,31]{1,2,0:T(8,128)(2,1)S(1)} %pad_maximum_fusion.3), channel_id=1, source_target_pairs={{4,0},{8,4},{12,8},{16,12},{20,16},{24,20},{28,24},{32,28},{36,32}... | collective-permute-start | bytes 380936 | tf_op jit(solution)/shard_map/ppermute | solution.py:21
  74.7 0.1 pad_maximum_fusion.1
  74.8 4.0 %collective-permute-done = bf16[2,1024,31]{1,2,0:T(8,128)(2,1)S(1)} collective-permute-done((bf16[2,1024,31]{1,2,0:T(8,128)(2,1)S(1)}, bf16[2,1024,31]{1,2,0:T(8,128)(2,1)S(1)}, u32[]{:S(2)}, u32[]{:S(2)}) %collective-permute-start) | collective-permute-done | bytes 127008 | tf_op jit(solution)/shard_map/ppermute | solution.py:21
  78.8 0.5 fusion.34
  79.3 0.1 fusion.197
  79.4 0.5 fusion.37
  79.9 0.1 fusion.198
  80.0 0.5 fusion.40
  80.5 0.1 fusion.199
  80.5 0.5 fusion.43
  81.0 0.1 fusion.200
  81.1 0.5 fusion.46
  81.6 0.1 fusion.201
  81.7 0.5 fusion.49
  82.2 0.1 fusion.202
  82.2 0.5 fusion.52
  82.7 0.1 fusion.203
  82.8 0.5 fusion.55
  83.3 0.1 fusion.204
  83.4 1.5 %subtract_convert_fusion.1 = (bf16[8,128,128]{2,1,0:T(8,128)(2,1)S(1)}, f32[8,128,128]{2,1,0:T(8,128)S(1)}, f32[8,128,128]{2,1,0:T(8,128)S(1)}) fusion(f32[8,128,128]{2,1,0:T(8,128)S(1)} %bitcast.123, f32[8,128,128]{2,1,0:T(8,128)S(1)} %bitcast.121, f32[8,128,128]{2,1,0:T(8,128)S(1)} %bitcast.143, f32[8,128]{1,0:T(8,128)S(1)} %bitcast.155, ...), kind=kLoop, calls=%fused_computation.22 | loop fusion | flops 4456448 | bytes 10780672 | tf_op jit(solution)/shard_map/convert_element_type | solution.py:202
  84.9 0.3 fusion.19
  85.2 0.1 add_convert_fusion.1
  85.3 0.3 fusion.15
  85.6 0.3 convolution_subtract_fusion
  85.9 0.5 subtract_convert_fusion
  86.4 0.4 fusion.9
  86.8 0.4 fusion.13
  87.3 0.5 fusion
  87.7 0.5 fusion.3
  88.2 0.2 copy.143
  88.4 0.1 convert_element_type.207
  88.5 0.2 fusion.6
  88.7 0.7 copy.145
  89.3 4.0 %all-to-all-start.1 = ((f32[4,64,128]{2,1,0:T(8,128)}), f32[4,64,128]{2,1,0:T(8,128)S(1)}, u32[]{:S(2)}, u32[]{:S(2)}) async-start(f32[4,64,128]{2,1,0:T(8,128)} %copy.145), calls=%async_computation.1 | async-start | bytes 262144 | tf_op jit(solution)/shard_map/all_to_all | solution.py:220
  93.3 0.6 fusion.116
  94.6 3.5 %all-to-all-done.1 = f32[4,64,128]{2,1,0:T(8,128)S(1)} async-done(((f32[4,64,128]{2,1,0:T(8,128)}), f32[4,64,128]{2,1,0:T(8,128)S(1)}, u32[]{:S(2)}, u32[]{:S(2)}) %all-to-all-start.1) | async-done | bytes 131104 | tf_op jit(solution)/shard_map/all_to_all | solution.py:220
  98.2 0.6 divide_bitcast_fusion
  (24 shorter events, 0.4 us)
Async XLA Ops:
  0.0 2.0 %copy-start.1 = (bf16[2,4096]{1,0:T(2,128)(2,1)S(1)}, bf16[2,4096]{1,0:T(2,128)(2,1)}, u32[]{:S(2)}) copy-start(bf16[2,4096]{1,0:T(2,128)(2,1)} %param.11) | copy-start | bytes 49156
  11.4 23.1 %copy-start.3 = (f32[128]{0:T(128)S(1)}, f32[128]{0:T(128)}, u32[]{:S(2)}) copy-start(f32[128]{0:T(128)} %param.14) | copy-start | bytes 1540
  13.6 53.8 %all-to-all-start = ((bf16[2,8,128,128]{3,1,0,2:T(8,128)(2,1)}), bf16[2,8,128,128]{3,1,0,2:T(8,128)(2,1)S(1)}, u32[]{:S(2)}, u32[]{:S(2)}) async-start(bf16[2,8,128,128]{3,1,0,2:T(8,128)(2,1)} %copy.117), calls=%async_computation | async-start | bytes 1048576 | tf_op jit(solution)/shard_map/all_to_all | solution.py:179
  35.5 1.1 %copy-start.2 = (s32[4,16]{1,0:T(4,128)S(1)}, s32[4,16]{1,0:T(4,128)}, u32[]{:S(2)}) copy-start(s32[4,16]{1,0:T(4,128)} %param.15) | copy-start | bytes 772
  35.6 1.2 %copy-start.4 = (s32[128]{0:T(128)S(1)}, s32[128]{0:T(128)}, u32[]{:S(2)}) copy-start(s32[128]{0:T(128)} %param.13) | copy-start | bytes 1540
  35.6 1.2 %copy-start = (f32[8,1024]{1,0:T(8,128)S(1)}, f32[8,1024]{1,0:T(8,128)}, u32[]{:S(2)}) copy-start(f32[8,1024]{1,0:T(8,128)} %param.12) | copy-start | bytes 98308
  71.4 7.4 %collective-permute-start = (bf16[2,1024,31]{1,2,0:T(8,128)(2,1)S(1)}, bf16[2,1024,31]{1,2,0:T(8,128)(2,1)S(1)}, u32[]{:S(2)}, u32[]{:S(2)}) collective-permute-start(bf16[2,1024,31]{1,2,0:T(8,128)(2,1)S(1)} %pad_maximum_fusion.3), channel_id=1, source_target_pairs={{4,0},{8,4},{12,8},{16,12},{20,16},{24,20},{28,24},{32,28},{36,32}... | collective-permute-start | bytes 380936 | tf_op jit(solution)/shard_map/ppermute | solution.py:21
  89.3 8.8 %all-to-all-start.1 = ((f32[4,64,128]{2,1,0:T(8,128)}), f32[4,64,128]{2,1,0:T(8,128)S(1)}, u32[]{:S(2)}, u32[]{:S(2)}) async-start(f32[4,64,128]{2,1,0:T(8,128)} %copy.145), calls=%async_computation.1 | async-start | bytes 262144 | tf_op jit(solution)/shard_map/all_to_all | solution.py:220

commit v2 on v1

--- a/solution.py
+++ b/solution.py
@@ -40,61 +40,75 @@
     return (jnp.cos(angle), jnp.sin(angle))
 
 
-def host_block_table(size, sign):
+def host_twiddle(first, second, sign):
+    heads = np.arange(first, dtype=np.int64)
+    tails = np.arange(second, dtype=np.int64)
+    product = (heads[:, None] * tails[None, :] % (first * second)).astype(np.float32)
+    angle = np.float32(sign * 2.0 * math.pi / (first * second)) * product
+    return np.stack([np.cos(angle), np.sin(angle)]).astype(np.float32)
+
+
+def host_tables(size, sign):
     index = np.arange(size, dtype=np.int64)
     product = (index[:, None] * index[None, :] % size).astype(np.float32)
     angle = np.float32(sign * 2.0 * math.pi / size) * product
     norm = np.float32(1.0 / math.sqrt(size))
     cos = (np.cos(angle) * norm).astype(ml_dtypes.bfloat16)
     sin = (np.sin(angle) * norm).astype(ml_dtypes.bfloat16)
-    top = np.concatenate([cos, -sin], axis=1)
-    bottom = np.concatenate([sin, cos], axis=1)
-    return np.concatenate([top, bottom], axis=0)
-
-
-def host_twiddle(first, second, sign):
-    heads = np.arange(first, dtype=np.int64)
-    tails = np.arange(second, dtype=np.int64)
-    product = (heads[:, None] * tails[None, :] % (first * second)).astype(np.float32)
-    angle = np.float32(sign * 2.0 * math.pi / (first * second)) * product
-    return np.stack([np.cos(angle), np.sin(angle)]).astype(np.float32)
-
-
-def square_transform(stacked, table, twiddle):
-    half = stacked.shape[0] // 2
-    mid = jnp.dot(table, stacked, preferred_element_type=jnp.float32)
-    mid_real, mid_imag = mid[:half], mid[half:]
+    table = np.block([[cos, -sin], [sin, cos]])
+    return table, np.ascontiguousarray(table.T)
+
+
+def twist(mid_real, mid_imag, twiddle):
     twist_cos, twist_sin = twiddle[0], twiddle[1]
     turn_real = (mid_real * twist_cos - mid_imag * twist_sin).astype(jnp.bfloat16)
     turn_imag = (mid_real * twist_sin + mid_imag * twist_cos).astype(jnp.bfloat16)
-    turned = jnp.concatenate([turn_real, turn_imag], axis=1)
-    out = lax.dot_general(
-        table, turned, (((1,), (1,)), ((), ())), preferred_element_type=jnp.float32
+    return turn_real, turn_imag
+
+
+def forward_transposed(stacked, table, table_t, twiddle):
+    half = stacked.shape[0] // 2
+    mid = jnp.dot(table, stacked, preferred_element_type=jnp.float32)
+    turn_real, turn_imag = twist(mid[:half], mid[half:], twiddle)
+    spec = jnp.dot(
+        jnp.concatenate([turn_real, turn_imag], axis=1), table_t, preferred_element_type=jnp.float32
+    )
+    return spec[:, :half], spec[:, half:]
+
+
+def inverse_from_transposed(real_t, imag_t, table, table_t, twiddle):
+    half = real_t.shape[0]
+    mid = jnp.dot(
+        jnp.concatenate([real_t, imag_t], axis=1), table_t, preferred_element_type=jnp.float32
+    )
+    turn_real, turn_imag = twist(mid[:, :half], mid[:, half:], twiddle)
+    out = jnp.dot(
+        table, jnp.concatenate([turn_real, turn_imag], axis=0), preferred_element_type=jnp.float32
     )
     return out[:half], out[half:]
 
 
-def range_kernel(echo_ref, replica_ref, fwd_ref, inv_ref, fwd_tw_ref, inv_tw_ref, out_ref, rep_ref):
-    fwd = fwd_ref[...]
-    fwd_tw = fwd_tw_ref[...]
-
-    @pl.when(pl.program_id(0) == 0)
-    def _():
-        rep_real, rep_imag = square_transform(replica_ref[...], fwd, fwd_tw)
-        rep_ref[0] = rep_real * 128.0
-        rep_ref[1] = rep_imag * 128.0
-
-    pulse = echo_ref[:, 0]
-    stacked = jnp.concatenate([pulse[0], pulse[1]], axis=0)
-    spec_real, spec_imag = square_transform(stacked, fwd, fwd_tw)
-    rep_real = rep_ref[0]
-    rep_imag = rep_ref[1]
-    match_real = (spec_real * rep_real + spec_imag * rep_imag).astype(jnp.bfloat16)
-    match_imag = (spec_imag * rep_real - spec_real * rep_imag).astype(jnp.bfloat16)
-    matched = jnp.concatenate([match_real, match_imag], axis=0)
-    comp_real, comp_imag = square_transform(matched, inv_ref[...], inv_tw_ref[...])
-    out_ref[0, 0] = comp_real.astype(jnp.bfloat16)
-    out_ref[1, 0] = comp_imag.astype(jnp.bfloat16)
+def range_kernel(
+    echo_ref, replica_ref, fwd_ref, fwd_t_ref, inv_ref, inv_t_ref, fwd_tw_ref, inv_tw_ref, out_ref, wide_ref
+):
+    pulses = echo_ref.shape[1] // echo_ref.shape[2]
+    side = echo_ref.shape[2]
+    fwd, fwd_t = fwd_ref[...], fwd_t_ref[...]
+    inv, inv_t = inv_ref[...], inv_t_ref[...]
+    fwd_tw, inv_tw = fwd_tw_ref[...], inv_tw_ref[...]
+    rep_real, rep_imag = forward_transposed(replica_ref[...], fwd, fwd_t, fwd_tw)
+    rep_real = rep_real * 128.0
+    rep_imag = rep_imag * 128.0
+    for pulse in range(pulses):
+        rows = pl.ds(pulse, side, stride=pulses)
+        stacked = jnp.concatenate([echo_ref[0, rows, :], echo_ref[1, rows, :]], axis=0)
+        spec_real, spec_imag = forward_transposed(stacked, fwd, fwd_t, fwd_tw)
+        match_real = (spec_real * rep_real + spec_imag * rep_imag).astype(jnp.bfloat16)
+        match_imag = (spec_imag * rep_real - spec_real * rep_imag).astype(jnp.bfloat16)
+        comp_real, comp_imag = inverse_from_transposed(match_real, match_imag, inv, inv_t, inv_tw)
+        wide_ref[pl.ds(pulse, side, stride=2 * pulses), :] = comp_real
+        wide_ref[pl.ds(pulses + pulse, side, stride=2 * pulses), :] = comp_imag
+    out_ref[...] = wide_ref[...].astype(jnp.bfloat16)
 
 
 def range_compress(echo, range_replica):
@@ -103,33 +117,34 @@
     assert length == side * side
     padded = jnp.pad(range_replica, ((0, 0), (0, length - range_replica.shape[1])))
     replica = padded.reshape(2 * side, side)
-    fwd = jnp.asarray(host_block_table(side, -1))
-    inv = jnp.asarray(host_block_table(side, 1))
-    fwd_tw = jnp.asarray(host_twiddle(side, side, -1))
-    inv_tw = jnp.asarray(host_twiddle(side, side, 1))
-    full = lambda shape: pl.BlockSpec(shape, lambda p: (0,) * len(shape))
+    rows = echo.reshape(2, pulses, side, side).transpose(0, 2, 1, 3).reshape(2, side * pulses, side)
+    fwd, fwd_t = host_tables(side, -1)
+    inv, inv_t = host_tables(side, 1)
+    fwd_tw = host_twiddle(side, side, -1)
+    inv_tw = host_twiddle(side, side, 1)
+    whole = pl.BlockSpec(memory_space=pltpu.VMEM)
     out = pl.pallas_call(
         range_kernel,
-        grid=(pulses,),
-        in_specs=[
-            pl.BlockSpec((2, 1, side, side), lambda p: (0, p, 0, 0)),
-            full((2 * side, side)),
-            full((2 * side, 2 * side)),
-            full((2 * side, 2 * side)),
-            full((2, side, side)),
-            full((2, side, side)),
-        ],
-        out_specs=pl.BlockSpec((2, 1, side, side), lambda p: (0, p, 0, 0)),
-        out_shape=jax.ShapeDtypeStruct((2, pulses, side, side), jnp.bfloat16),
-        scratch_shapes=[pltpu.VMEM((2, side, side), jnp.float32)],
-        compiler_params=pltpu.CompilerParams(dimension_semantics=("arbitrary",)),
+        in_specs=[whole] * 8,
+        out_specs=whole,
+        out_shape=jax.ShapeDtypeStruct((side * 2 * pulses, side), jnp.bfloat16),
+        scratch_shapes=[pltpu.VMEM((side * 2 * pulses, side), jnp.float32)],
         cost_estimate=pl.CostEstimate(
-            flops=pulses * 4 * 2 * (2 * side) ** 2 * side,
+            flops=(pulses + 1) * 4 * 2 * (2 * side) ** 2 * side,
             bytes_accessed=pulses * 2 * 2 * length * 2,
             transcendentals=0,
         ),
-    )(echo.reshape(2, pulses, side, side), replica, fwd, inv, fwd_tw, inv_tw)
-    return out.reshape(2, pulses, length)
+    )(
+        rows,
+        replica,
+        jnp.asarray(fwd),
+        jnp.asarray(fwd_t),
+        jnp.asarray(inv),
+        jnp.asarray(inv_t),
+        jnp.asarray(fwd_tw),
+        jnp.asarray(inv_tw),
+    )
+    return out.reshape(side, 2, pulses, side)
 
 
 def pulse_transform(real_part, imag_part, first, sign):
@@ -173,11 +188,9 @@
     compressed = range_compress(echo, range_replica)
     devices = lax.axis_size("wide")
     width = length // devices
-    local_pulses = compressed.shape[1]
-    split_bins = compressed.reshape(2, local_pulses, devices, width)
-    doppler = azimuth_spectra(
-        lax.all_to_all(split_bins, "wide", split_axis=2, concat_axis=1, tiled=True)
-    )[:, :, 0]
+    assert compressed.shape[0] == devices and compressed.shape[3] == width
+    turned = lax.all_to_all(compressed, "wide", split_axis=0, concat_axis=2, tiled=True)[0]
+    doppler = azimuth_spectra(turned[:, :, None, :])[:, :, 0]
     rim = passed_along(doppler[:, :, :HALO], "wide", -1)
     extended = jnp.concatenate([doppler, rim], axis=2)
     pulses = extended.shape[1]

time: 99.5 us -> 92.7 us (0.932)
  local copies, waits for them, and re-layouts: 8.3 us -> 4.87 us
  Pallas kernels: 8.74 us -> 5.6 us
    pallas_call x1, Pallas kernels: 8.74 us -> 5.6 us  [range_compress(): pl.pallas_call(range_kernel, in_specs=[whole] * 8, out_specs=whole, out_s...]
    pallas_call x1 -> x0, local copies, waits for them, and re-layouts: 2.2 us -> none  [range_compress(): pl.pallas_call(range_kernel, grid=(pulses,), in_specs=[pl.BlockSpec((2, 1...]
    unnamed x11 -> x8, local copies, waits for them, and re-layouts: 1.98 us -> 0.02 us
  transfers between devices with their start and end apart: 3 -> 3, of which waited for: 3 -> 3; matrix products, arithmetic and copies ran while one was open for 3% -> 4% of each run, Pallas kernels for 0% -> 0%
where the time goes in v2:
time: 92.7 us; the launch traced here: 92.4 us
  waiting for transfers between devices  38.1 us (41%)
  starting transfers between devices  28 us (30%)
  matrix products  10.3 us (11%)
  Pallas kernels  5.6 us (6%)
  local copies, waits for them, and re-layouts  4.87 us (5%)
  other arithmetic  4.34 us (5%)
  between operations  1.12 us (1%)
    all_to_all x1, waiting for transfers between devices, per_device(): lax.all_to_all(compressed, 'wide', split_axis=0, concat_axis=2, tiled=True)  30.6 us
    all_to_all x1, starting transfers between devices, per_device(): lax.all_to_all(compressed, 'wide', split_axis=0, concat_axis=2, tiled=True)  20.7 us
    pallas_call x1, Pallas kernels, range_compress(): pl.pallas_call(range_kernel, in_specs=[whole] * 8, out_specs=whole, out_s...  5.6 us
    ppermute x1, waiting for transfers between devices, passed_along(): return lax.ppermute(shard, axis, pairs)  4.03 us
    all_to_all x1, starting transfers between devices, per_device(): lax.all_to_all(partial, 'narrow', split_axis=0, concat_axis=0, tiled=True)  4.01 us
    dot_general x8, matrix products, per_device(): jnp.einsum('xpc,cr->xpr', extended, select, preferred_element_type=jnp.fl...  3.85 us
    dot_general x8, matrix products, section_two(): jnp.einsum('kmc,jm->jkc', values, table, preferred_element_type=jnp.float32)  3.61 us
    all_to_all x1, waiting for transfers between devices, per_device(): lax.all_to_all(partial, 'narrow', split_axis=0, concat_axis=0, tiled=True)  3.54 us
  transfers between devices with their start and end apart: 3, of which 3 were waited for; matrix products, arithmetic and copies ran while one was open for 4% of the time, Pallas kernels for 0%

profile of v2, /device:TPU:1, one launch (start us, length us, event | category | flops | bytes accessed | tf_op | source)
XLA Modules:
  0.0 92.4 jit_solution(79654731759422446)
XLA Ops:
  0.0 0.8 pad.4
  0.8 0.7 reshape.354.replica_ref
  1.4 5.6 %shard_map.118 = bf16[2048,128]{1,0:T(8,128)(2,1)} custom-call(bf16[2,1024,128]{2,1,0:T(8,128)(2,1)} %bitcast.156, bf16[256,128]{1,0:T(8,128)(2,1)} %reshape.354.replica_ref, bf16[256,256]{1,0:T(8,128)(2,1)} %constant.116.clone.fwd_ref.inv_t_ref, bf16[256,256]{1,0:T(8,128)(2,1)} %constant.117.clone.fwd_t_ref.inv_ref, ...), custom_call_target="tpu_custom_call" | custom-call | flops 603979776 | bytes 1048576 | tf_op jit(solution)/shard_map/pallas_call | solution.py:126
  7.0 20.7 %all-to-all-start = ((bf16[128,2,8,128]{3,2,1,0:T(8,128)(2,1)}), bf16[128,2,8,128]{3,2,1,0:T(8,128)(2,1)S(1)}, u32[]{:S(2)}, u32[]{:S(2)}) async-start(bf16[128,2,8,128]{3,2,1,0:T(8,128)(2,1)} %bitcast.147), calls=%async_computation | async-start | bytes 1048576 | tf_op jit(solution)/shard_map/all_to_all | solution.py:192
  27.8 0.1 multiply_cosine_fusion.1
  27.8 0.1 copy.119
  28.0 0.1 copy.122
  28.1 1.0 %divide_cosine_fusion = (f32[513,128]{1,0:T(8,128)S(1)}, f32[513,128]{1,0:T(8,128)S(1)}) fusion(f32[128]{0:T(128)S(1)} %copy-done.2, f32[513]{0:T(1024)S(1)} %fusion.91), kind=kLoop, calls=%fused_computation.32 | loop fusion | flops 65664 | bytes 527876 | tf_op jit(solution)/shard_map/cos | solution.py:211
  29.2 0.3 rev.7
  29.5 0.3 rev.8
  29.9 0.1 multiply_cosine_fusion
  29.9 0.1 copy.133
  30.1 0.1 copy.136
  30.2 0.1 convert_reduce_fusion
  30.4 30.6 %all-to-all-done = bf16[128,2,8,128]{3,2,1,0:T(8,128)(2,1)S(1)} async-done(((bf16[128,2,8,128]{3,2,1,0:T(8,128)(2,1)}), bf16[128,2,8,128]{3,2,1,0:T(8,128)(2,1)S(1)}, u32[]{:S(2)}, u32[]{:S(2)}) %all-to-all-start) | async-done | bytes 524320 | tf_op jit(solution)/shard_map/all_to_all | solution.py:192
  61.0 0.3 fusion.31
  61.3 0.3 fusion.27
  61.6 0.3 convolution_subtract_fusion.1
  61.9 0.5 subtract_convert_fusion.2
  62.4 0.4 fusion.25
  62.9 0.4 fusion.21
  63.3 0.5 fusion.4
  63.8 0.2 copy.190
  64.0 0.1 copy.129
  64.1 0.5 fusion.5
  64.6 0.2 copy.189
  64.8 0.1 copy.130
  64.9 3.3 %collective-permute-start = (bf16[2,1024,31]{1,2,0:T(8,128)(2,1)S(1)}, bf16[2,1024,31]{1,2,0:T(8,128)(2,1)S(1)}, u32[]{:S(2)}, u32[]{:S(2)}) collective-permute-start(bf16[2,1024,31]{1,2,0:T(8,128)(2,1)S(1)} %pad_maximum_fusion.3), channel_id=1, source_target_pairs={{4,0},{8,4},{12,8},{16,12},{20,16},{24,20},{28,24},{32,28},{36,32}... | collective-permute-start | bytes 380936 | tf_op jit(solution)/shard_map/ppermute | solution.py:21
  68.2 0.1 pad_maximum_fusion.1
  68.4 4.0 %collective-permute-done = bf16[2,1024,31]{1,2,0:T(8,128)(2,1)S(1)} collective-permute-done((bf16[2,1024,31]{1,2,0:T(8,128)(2,1)S(1)}, bf16[2,1024,31]{1,2,0:T(8,128)(2,1)S(1)}, u32[]{:S(2)}, u32[]{:S(2)}) %collective-permute-start) | collective-permute-done | bytes 127008 | tf_op jit(solution)/shard_map/ppermute | solution.py:21
  72.4 0.5 fusion.34
  72.9 0.1 fusion.197
  73.0 0.5 fusion.37
  73.4 0.1 fusion.198
  73.5 0.5 fusion.40
  74.0 0.1 fusion.199
  74.1 0.5 fusion.43
  74.6 0.1 fusion.200
  74.7 0.5 fusion.46
  75.1 0.1 fusion.201
  75.2 0.5 fusion.49
  75.7 0.1 fusion.202
  75.8 0.5 fusion.52
  76.3 0.1 fusion.203
  76.4 0.5 fusion.55
  76.8 0.1 fusion.204
  76.9 1.5 %subtract_convert_fusion.1 = (bf16[8,128,128]{2,1,0:T(8,128)(2,1)S(1)}, f32[8,128,128]{2,1,0:T(8,128)S(1)}, f32[8,128,128]{2,1,0:T(8,128)S(1)}) fusion(f32[8,128,128]{2,1,0:T(8,128)S(1)} %bitcast.122, f32[8,128,128]{2,1,0:T(8,128)S(1)} %bitcast.120, f32[8,128,128]{2,1,0:T(8,128)S(1)} %bitcast.142, f32[8,128]{1,0:T(8,128)S(1)} %bitcast.154, ...), kind=kLoop, calls=%fused_computation.21 | loop fusion | flops 4456448 | bytes 10780672 | tf_op jit(solution)/shard_map/convert_element_type | solution.py:215
  78.4 0.3 fusion.19
  78.7 0.1 add_convert_fusion.1
  78.9 0.3 fusion.15
  79.1 0.3 convolution_subtract_fusion
  79.4 0.5 subtract_convert_fusion
  79.9 0.4 fusion.9
  80.4 0.4 fusion.13
  80.8 0.5 fusion
  81.3 0.5 fusion.3
  81.8 0.2 copy.141
  81.9 0.1 convert_element_type.207
  82.1 0.2 fusion.6
  82.2 0.7 copy.143
  82.9 4.0 %all-to-all-start.1 = ((f32[4,64,128]{2,1,0:T(8,128)}), f32[4,64,128]{2,1,0:T(8,128)S(1)}, u32[]{:S(2)}, u32[]{:S(2)}) async-start(f32[4,64,128]{2,1,0:T(8,128)} %copy.143), calls=%async_computation.1 | async-start | bytes 262144 | tf_op jit(solution)/shard_map/all_to_all | solution.py:233
  86.9 0.6 fusion.116
  88.2 3.5 %all-to-all-done.1 = f32[4,64,128]{2,1,0:T(8,128)S(1)} async-done(((f32[4,64,128]{2,1,0:T(8,128)}), f32[4,64,128]{2,1,0:T(8,128)S(1)}, u32[]{:S(2)}, u32[]{:S(2)}) %all-to-all-start.1) | async-done | bytes 131104 | tf_op jit(solution)/shard_map/all_to_all | solution.py:233
  91.8 0.6 divide_bitcast_fusion
  (20 shorter events, 0.3 us)
Async XLA Ops:
  7.0 21.0 %copy-start.2 = (f32[128]{0:T(128)S(1)}, f32[128]{0:T(128)}, u32[]{:S(2)}) copy-start(f32[128]{0:T(128)} %param.16) | copy-start | bytes 1540
  7.0 53.9 %all-to-all-start = ((bf16[128,2,8,128]{3,2,1,0:T(8,128)(2,1)}), bf16[128,2,8,128]{3,2,1,0:T(8,128)(2,1)S(1)}, u32[]{:S(2)}, u32[]{:S(2)}) async-start(bf16[128,2,8,128]{3,2,1,0:T(8,128)(2,1)} %bitcast.147), calls=%async_computation | async-start | bytes 1048576 | tf_op jit(solution)/shard_map/all_to_all | solution.py:192
  29.1 1.1 %copy-start.1 = (s32[4,16]{1,0:T(4,128)S(1)}, s32[4,16]{1,0:T(4,128)}, u32[]{:S(2)}) copy-start(s32[4,16]{1,0:T(4,128)} %param.17) | copy-start | bytes 772
  29.1 1.2 %copy-start.3 = (s32[128]{0:T(128)S(1)}, s32[128]{0:T(128)}, u32[]{:S(2)}) copy-start(s32[128]{0:T(128)} %param.15) | copy-start | bytes 1540
  29.1 1.2 %copy-start = (f32[8,1024]{1,0:T(8,128)S(1)}, f32[8,1024]{1,0:T(8,128)}, u32[]{:S(2)}) copy-start(f32[8,1024]{1,0:T(8,128)} %param.14) | copy-start | bytes 98308
  64.9 7.4 %collective-permute-start = (bf16[2,1024,31]{1,2,0:T(8,128)(2,1)S(1)}, bf16[2,1024,31]{1,2,0:T(8,128)(2,1)S(1)}, u32[]{:S(2)}, u32[]{:S(2)}) collective-permute-start(bf16[2,1024,31]{1,2,0:T(8,128)(2,1)S(1)} %pad_maximum_fusion.3), channel_id=1, source_target_pairs={{4,0},{8,4},{12,8},{16,12},{20,16},{24,20},{28,24},{32,28},{36,32}... | collective-permute-start | bytes 380936 | tf_op jit(solution)/shard_map/ppermute | solution.py:21
  82.9 8.8 %all-to-all-start.1 = ((f32[4,64,128]{2,1,0:T(8,128)}), f32[4,64,128]{2,1,0:T(8,128)S(1)}, u32[]{:S(2)}, u32[]{:S(2)}) async-start(f32[4,64,128]{2,1,0:T(8,128)} %copy.143), calls=%async_computation.1 | async-start | bytes 262144 | tf_op jit(solution)/shard_map/all_to_all | solution.py:233

commit v3 on v2

--- a/solution.py
+++ b/solution.py
@@ -230,9 +230,13 @@
     own_count = jnp.sum(jnp.where(tile_ids == group, counts, 0)).astype(jnp.float32)
     partial = jnp.dot(member, blocks, preferred_element_type=jnp.float32)
     partial = partial.reshape(tiles, block_rows, width)
-    incoming = lax.all_to_all(partial, "narrow", split_axis=0, concat_axis=0, tiled=True)
-    summed = jnp.sum(incoming, axis=0)[None]
-    return summed / own_count
+    summed = lax.dynamic_index_in_dim(partial, group, 0, keepdims=False)
+    for shift in range(1, tiles):
+        outgoing = lax.dynamic_index_in_dim(partial, (group + shift) % tiles, 0, keepdims=False)
+        summed = summed + lax.ppermute(
+            outgoing, "narrow", [(i, (i + shift) % tiles) for i in range(tiles)]
+        )
+    return summed[None] / own_count
 
 
 def solution(mesh):

time: 92.7 us -> 95.5 us (1.030)
  starting transfers between devices: 28 us -> 34.5 us
  waiting for transfers between devices: 38.1 us -> 34.8 us
    ppermute x0 -> x3, starting transfers between devices: none -> 10.5 us  [per_device(): lax.ppermute(outgoing, 'narrow', [(i, (i + shift) % tiles) for i in range...]
    all_to_all x1 -> x0, starting transfers between devices: 4.01 us -> none  [per_device(): lax.all_to_all(partial, 'narrow', split_axis=0, concat_axis=0, tiled=True)]
    all_to_all x1 -> x0, waiting for transfers between devices: 3.54 us -> none  [per_device(): lax.all_to_all(partial, 'narrow', split_axis=0, concat_axis=0, tiled=True)]
  transfers between devices with their start and end apart: 3 -> 5, of which waited for: 3 -> 3; matrix products, arithmetic and copies ran while one was open for 4% -> 3% of each run, Pallas kernels for 0% -> 0%
where the time goes in v3:
time: 95.5 us; the launch traced here: 95.1 us
  waiting for transfers between devices  34.8 us (36%)
  starting transfers between devices  34.5 us (36%)
  matrix products  10.3 us (11%)
  Pallas kernels  5.61 us (6%)
  other arithmetic  4.33 us (5%)
  local copies, waits for them, and re-layouts  4.32 us (5%)
  between operations  1.23 us (1%)
    all_to_all x1, waiting for transfers between devices, per_device(): lax.all_to_all(compressed, 'wide', split_axis=0, concat_axis=2, tiled=True)  30.5 us
    all_to_all x1, starting transfers between devices, per_device(): lax.all_to_all(compressed, 'wide', split_axis=0, concat_axis=2, tiled=True)  20.7 us
    ppermute x3, starting transfers between devices, per_device(): lax.ppermute(outgoing, 'narrow', [(i, (i + shift) % tiles) for i in range...  10.5 us
    pallas_call x1, Pallas kernels, range_compress(): pl.pallas_call(range_kernel, in_specs=[whole] * 8, out_specs=whole, out_s...  5.61 us
    ppermute x1, waiting for transfers between devices, passed_along(): return lax.ppermute(shard, axis, pairs)  4.03 us
    dot_general x8, matrix products, per_device(): jnp.einsum('xpc,cr->xpr', extended, select, preferred_element_type=jnp.fl...  3.84 us
    dot_general x8, matrix products, section_two(): jnp.einsum('kmc,jm->jkc', values, table, preferred_element_type=jnp.float32)  3.61 us
    ppermute x1, starting transfers between devices, passed_along(): return lax.ppermute(shard, axis, pairs)  3.28 us
  transfers between devices with their start and end apart: 5, of which 3 were waited for; matrix products, arithmetic and copies ran while one was open for 3% of the time, Pallas kernels for 0%

profile of v3, /device:TPU:1, one launch (start us, length us, event | category | flops | bytes accessed | tf_op | source)
XLA Modules:
  0.0 95.1 jit_solution(6797568844595126716)
XLA Ops:
  0.0 0.8 pad.4
  0.8 0.7 reshape.345.replica_ref
  1.4 5.6 %shard_map.118 = bf16[2048,128]{1,0:T(8,128)(2,1)} custom-call(bf16[2,1024,128]{2,1,0:T(8,128)(2,1)} %bitcast.164, bf16[256,128]{1,0:T(8,128)(2,1)} %reshape.345.replica_ref, bf16[256,256]{1,0:T(8,128)(2,1)} %constant.144.clone.fwd_ref.inv_t_ref, bf16[256,256]{1,0:T(8,128)(2,1)} %constant.145.clone.fwd_t_ref.inv_ref, ...), custom_call_target="tpu_custom_call" | custom-call | flops 603979776 | bytes 1048576 | tf_op jit(solution)/shard_map/pallas_call | solution.py:126
  7.1 20.7 %all-to-all-start = ((bf16[128,2,8,128]{3,2,1,0:T(8,128)(2,1)}), bf16[128,2,8,128]{3,2,1,0:T(8,128)(2,1)S(1)}, u32[]{:S(2)}, u32[]{:S(2)}) async-start(bf16[128,2,8,128]{3,2,1,0:T(8,128)(2,1)} %bitcast.151), calls=%async_computation | async-start | bytes 1048576 | tf_op jit(solution)/shard_map/all_to_all | solution.py:192
  27.9 0.1 copy.117
  28.0 0.1 copy.120
  28.1 1.0 %divide_cosine_fusion = (f32[513,128]{1,0:T(8,128)S(1)}, f32[513,128]{1,0:T(8,128)S(1)}) fusion(f32[128]{0:T(128)S(1)} %copy-done.2, f32[513]{0:T(1024)S(1)} %fusion.91), kind=kLoop, calls=%fused_computation.32 | loop fusion | flops 65664 | bytes 527876 | tf_op jit(solution)/shard_map/cos | solution.py:211
  29.2 0.3 rev.7
  29.6 0.3 rev.8
  30.0 0.1 copy.131
  30.1 0.1 copy.134
  30.3 0.1 convert_reduce_fusion
  30.5 30.5 %all-to-all-done = bf16[128,2,8,128]{3,2,1,0:T(8,128)(2,1)S(1)} async-done(((bf16[128,2,8,128]{3,2,1,0:T(8,128)(2,1)}), bf16[128,2,8,128]{3,2,1,0:T(8,128)(2,1)S(1)}, u32[]{:S(2)}, u32[]{:S(2)}) %all-to-all-start) | async-done | bytes 524320 | tf_op jit(solution)/shard_map/all_to_all | solution.py:192
  61.1 0.3 fusion.31
  61.3 0.3 fusion.27
  61.6 0.3 convolution_subtract_fusion.1
  61.9 0.5 subtract_convert_fusion.2
  62.4 0.4 fusion.25
  62.9 0.4 fusion.21
  63.3 0.5 fusion.4
  63.8 0.2 copy.187
  64.0 0.1 copy.127
  64.1 0.5 fusion.5
  64.6 0.2 copy.186
  64.8 0.1 copy.128
  64.9 3.3 %collective-permute-start = (bf16[2,1024,31]{1,2,0:T(8,128)(2,1)S(1)}, bf16[2,1024,31]{1,2,0:T(8,128)(2,1)S(1)}, u32[]{:S(2)}, u32[]{:S(2)}) collective-permute-start(bf16[2,1024,31]{1,2,0:T(8,128)(2,1)S(1)} %pad_maximum_fusion.3), channel_id=1, source_target_pairs={{4,0},{8,4},{12,8},{16,12},{20,16},{24,20},{28,24},{32,28},{36,32}... | collective-permute-start | bytes 380936 | tf_op jit(solution)/shard_map/ppermute | solution.py:21
  68.2 0.1 pad_maximum_fusion.1
  68.3 4.0 %collective-permute-done = bf16[2,1024,31]{1,2,0:T(8,128)(2,1)S(1)} collective-permute-done((bf16[2,1024,31]{1,2,0:T(8,128)(2,1)S(1)}, bf16[2,1024,31]{1,2,0:T(8,128)(2,1)S(1)}, u32[]{:S(2)}, u32[]{:S(2)}) %collective-permute-start) | collective-permute-done | bytes 127008 | tf_op jit(solution)/shard_map/ppermute | solution.py:21
  72.4 0.5 fusion.34
  72.9 0.1 fusion.198
  72.9 0.5 fusion.37
  73.4 0.1 fusion.199
  73.5 0.5 fusion.40
  74.0 0.1 fusion.200
  74.1 0.5 fusion.43
  74.6 0.1 fusion.201
  74.6 0.5 fusion.46
  75.1 0.1 fusion.202
  75.2 0.5 fusion.49
  75.7 0.1 fusion.203
  75.8 0.5 fusion.52
  76.3 0.1 fusion.204
  76.3 0.5 fusion.55
  76.8 0.1 fusion.205
  76.9 1.5 %subtract_convert_fusion.1 = (bf16[8,128,128]{2,1,0:T(8,128)(2,1)S(1)}, f32[8,128,128]{2,1,0:T(8,128)S(1)}, f32[8,128,128]{2,1,0:T(8,128)S(1)}) fusion(f32[8,128,128]{2,1,0:T(8,128)S(1)} %bitcast.126, f32[8,128,128]{2,1,0:T(8,128)S(1)} %bitcast.124, f32[8,128,128]{2,1,0:T(8,128)S(1)} %bitcast.146, f32[8,128]{1,0:T(8,128)S(1)} %bitcast.162, ...), kind=kLoop, calls=%fused_computation.21 | loop fusion | flops 4456448 | bytes 10780672 | tf_op jit(solution)/shard_map/convert_element_type | solution.py:215
  78.4 0.3 fusion.19
  78.7 0.1 add_convert_fusion.1
  78.8 0.3 fusion.15
  79.1 0.3 convolution_subtract_fusion
  79.4 0.5 subtract_convert_fusion
  79.9 0.4 fusion.9
  80.4 0.4 fusion.13
  80.8 0.5 fusion
  81.3 0.5 fusion.3
  81.7 0.2 copy.139
  81.9 0.1 convert_element_type.207
  82.1 0.2 fusion.6
  82.2 0.1 constant_dynamic-slice_fusion.2
  82.3 3.1 %collective-permute-start.1 = (f32[64,128]{1,0:T(8,128)S(1)}, f32[64,128]{1,0:T(8,128)S(1)}, u32[]{:S(2)}, u32[]{:S(2)}) collective-permute-start(f32[64,128]{1,0:T(8,128)S(1)} %bitcast.155), channel_id=1, source_target_pairs={{0,1},{1,2},{2,3},{3,0},{4,5},{5,6},{6,7},{7,4},{8,9},{9,10},{10,1... | collective-permute-start | bytes 98312 | tf_op jit(solution)/shard_map/ppermute | solution.py:236
  85.5 4.4 %collective-permute-start.2 = (f32[64,128]{1,0:T(8,128)S(1)}, f32[64,128]{1,0:T(8,128)S(1)}, u32[]{:S(2)}, u32[]{:S(2)}) collective-permute-start(f32[64,128]{1,0:T(8,128)S(1)} %bitcast.154), channel_id=1, source_target_pairs={{0,2},{1,3},{2,0},{3,1},{4,6},{5,7},{6,4},{7,5},{8,10},{9,11},{10,... | collective-permute-start | bytes 98312 | tf_op jit(solution)/shard_map/ppermute | solution.py:236
  89.8 3.1 %collective-permute-start.3 = (f32[64,128]{1,0:T(8,128)S(1)}, f32[64,128]{1,0:T(8,128)S(1)}, u32[]{:S(2)}, u32[]{:S(2)}) collective-permute-start(f32[64,128]{1,0:T(8,128)S(1)} %bitcast.153), channel_id=1, source_target_pairs={{0,3},{1,0},{2,1},{3,2},{4,7},{5,4},{6,5},{7,6},{8,11},{9,8},{10,9... | collective-permute-start | bytes 98312 | tf_op jit(solution)/shard_map/ppermute | solution.py:236
  92.9 0.6 fusion.133
  94.2 0.3 collective-permute-done.3
  94.5 0.6 divide_bitcast_fusion
  (23 shorter events, 0.4 us)
Async XLA Ops:
  7.1 21.1 %copy-start.2 = (f32[128]{0:T(128)S(1)}, f32[128]{0:T(128)}, u32[]{:S(2)}) copy-start(f32[128]{0:T(128)} %param.16) | copy-start | bytes 1540
  7.1 53.9 %all-to-all-start = ((bf16[128,2,8,128]{3,2,1,0:T(8,128)(2,1)}), bf16[128,2,8,128]{3,2,1,0:T(8,128)(2,1)S(1)}, u32[]{:S(2)}, u32[]{:S(2)}) async-start(bf16[128,2,8,128]{3,2,1,0:T(8,128)(2,1)} %bitcast.151), calls=%async_computation | async-start | bytes 1048576 | tf_op jit(solution)/shard_map/all_to_all | solution.py:192
  29.1 1.1 %copy-start.1 = (s32[4,16]{1,0:T(4,128)S(1)}, s32[4,16]{1,0:T(4,128)}, u32[]{:S(2)}) copy-start(s32[4,16]{1,0:T(4,128)} %param.17) | copy-start | bytes 772
  29.2 1.3 %copy-start.3 = (s32[128]{0:T(128)S(1)}, s32[128]{0:T(128)}, u32[]{:S(2)}) copy-start(s32[128]{0:T(128)} %param.15) | copy-start | bytes 1540
  29.2 1.3 %copy-start = (f32[8,1024]{1,0:T(8,128)S(1)}, f32[8,1024]{1,0:T(8,128)}, u32[]{:S(2)}) copy-start(f32[8,1024]{1,0:T(8,128)} %param.14) | copy-start | bytes 98308
  64.9 7.4 %collective-permute-start = (bf16[2,1024,31]{1,2,0:T(8,128)(2,1)S(1)}, bf16[2,1024,31]{1,2,0:T(8,128)(2,1)S(1)}, u32[]{:S(2)}, u32[]{:S(2)}) collective-permute-start(bf16[2,1024,31]{1,2,0:T(8,128)(2,1)S(1)} %pad_maximum_fusion.3), channel_id=1, source_target_pairs={{4,0},{8,4},{12,8},{16,12},{20,16},{24,20},{28,24},{32,28},{36,32}... | collective-permute-start | bytes 380936 | tf_op jit(solution)/shard_map/ppermute | solution.py:21
  82.3 11.8 %collective-permute-start.1 = (f32[64,128]{1,0:T(8,128)S(1)}, f32[64,128]{1,0:T(8,128)S(1)}, u32[]{:S(2)}, u32[]{:S(2)}) collective-permute-start(f32[64,128]{1,0:T(8,128)S(1)} %bitcast.155), channel_id=1, source_target_pairs={{0,1},{1,2},{2,3},{3,0},{4,5},{5,6},{6,7},{7,4},{8,9},{9,10},{10,1... | collective-permute-start | bytes 98312 | tf_op jit(solution)/shard_map/ppermute | solution.py:236
  85.5 8.7 %collective-permute-start.2 = (f32[64,128]{1,0:T(8,128)S(1)}, f32[64,128]{1,0:T(8,128)S(1)}, u32[]{:S(2)}, u32[]{:S(2)}) collective-permute-start(f32[64,128]{1,0:T(8,128)S(1)} %bitcast.154), channel_id=1, source_target_pairs={{0,2},{1,3},{2,0},{3,1},{4,6},{5,7},{6,4},{7,5},{8,10},{9,11},{10,... | collective-permute-start | bytes 98312 | tf_op jit(solution)/shard_map/ppermute | solution.py:236
  89.8 4.7 %collective-permute-start.3 = (f32[64,128]{1,0:T(8,128)S(1)}, f32[64,128]{1,0:T(8,128)S(1)}, u32[]{:S(2)}, u32[]{:S(2)}) collective-permute-start(f32[64,128]{1,0:T(8,128)S(1)} %bitcast.153), channel_id=1, source_target_pairs={{0,3},{1,0},{2,1},{3,2},{4,7},{5,4},{6,5},{7,6},{8,11},{9,8},{10,9... | collective-permute-start | bytes 98312 | tf_op jit(solution)/shard_map/ppermute | solution.py:236

commit v4 on v2

--- a/solution.py
+++ b/solution.py
@@ -19,25 +19,6 @@
     devices = lax.axis_size(axis)
     pairs = [(i, i + by) for i in range(devices) if 0 <= i + by < devices]
     return lax.ppermute(shard, axis, pairs)
-
-
-def make_table(size, sign):
-    index = jnp.arange(size, dtype=jnp.int32)
-    product = index[:, None] * index[None, :] % size
-    angle = sign * 2.0 * math.pi / size * product.astype(jnp.float32)
-    norm = 1.0 / math.sqrt(size)
-    return (
-        (jnp.cos(angle) * norm).astype(jnp.bfloat16),
-        (jnp.sin(angle) * norm).astype(jnp.bfloat16),
-    )
-
-
-def make_twiddle(first, second, sign):
-    heads = jnp.arange(first, dtype=jnp.int32)
-    tails = jnp.arange(second, dtype=jnp.int32)
-    product = heads[:, None] * tails[None, :] % (first * second)
-    angle = sign * 2.0 * math.pi / (first * second) * product.astype(jnp.float32)
-    return (jnp.cos(angle), jnp.sin(angle))
 
 
 def host_twiddle(first, second, sign):
@@ -147,39 +128,30 @@
     return out.reshape(side, 2, pulses, side)
 
 
-def pulse_transform(real_part, imag_part, first, sign):
-    length = real_part.shape[0]
-    width = real_part.shape[1]
+def host_block_table4(size, sign):
+    index = np.arange(size, dtype=np.int64)
+    product = (index[:, None] * index[None, :] % size).astype(np.float32)
+    angle = np.float32(sign * 2.0 * math.pi / size) * product
+    norm = np.float32(1.0 / math.sqrt(size))
+    cos = (np.cos(angle) * norm).astype(ml_dtypes.bfloat16)
+    sin = (np.sin(angle) * norm).astype(ml_dtypes.bfloat16)
+    return np.stack([np.stack([cos, -sin], axis=1), np.stack([sin, cos], axis=1)])
+
+
+def pulse_transform(values, first, sign):
+    length, width = values.shape[1], values.shape[2]
     second = length // first
-    head_cos, head_sin = make_table(first, sign)
-    tail_cos, tail_sin = make_table(second, sign)
-    twist_cos, twist_sin = make_twiddle(first, second, sign)
-    twist_cos = twist_cos[:, :, None]
-    twist_sin = twist_sin[:, :, None]
-    split_real = real_part.reshape(first, second, width)
-    split_imag = imag_part.reshape(first, second, width)
-
-    def section_one(table, values):
-        return jnp.einsum("kn,nmc->kmc", table, values, preferred_element_type=jnp.float32)
-
-    mid_real = section_one(head_cos, split_real) - section_one(head_sin, split_imag)
-    mid_imag = section_one(head_cos, split_imag) + section_one(head_sin, split_real)
-    turn_real = (mid_real * twist_cos - mid_imag * twist_sin).astype(jnp.bfloat16)
-    turn_imag = (mid_real * twist_sin + mid_imag * twist_cos).astype(jnp.bfloat16)
-
-    def section_two(table, values):
-        return jnp.einsum("kmc,jm->jkc", values, table, preferred_element_type=jnp.float32)
-
-    out_real = section_two(tail_cos, turn_real) - section_two(tail_sin, turn_imag)
-    out_imag = section_two(tail_cos, turn_imag) + section_two(tail_sin, turn_real)
-    return (out_real.reshape(length, width), out_imag.reshape(length, width))
-
-
-def azimuth_spectra(values):
-    first_real, first_imag = pulse_transform(values[0, :, 0], values[1, :, 0], PUL_DEV, -1)
-    return jnp.stack([first_real.astype(jnp.bfloat16), first_imag.astype(jnp.bfloat16)])[
-        :, :, None, :
-    ]
+    head = jnp.asarray(host_block_table4(first, sign))
+    tail = jnp.asarray(host_block_table4(second, sign))
+    twist_cos, twist_sin = (jnp.asarray(t) for t in host_twiddle(first, second, sign))
+    split = values.reshape(2, first, second, width)
+    mid = jnp.einsum("okrn,rnmc->okmc", head, split, preferred_element_type=jnp.float32)
+    mid_real, mid_imag = mid[0], mid[1]
+    turn_real = mid_real * twist_cos[:, :, None] - mid_imag * twist_sin[:, :, None]
+    turn_imag = mid_real * twist_sin[:, :, None] + mid_imag * twist_cos[:, :, None]
+    turned = jnp.stack([turn_real, turn_imag]).astype(jnp.bfloat16)
+    out = jnp.einsum("ojrm,rkmc->ojkc", tail, turned, preferred_element_type=jnp.float32)
+    return out.reshape(2, length, width)
 
 
 def per_device(raw_echo, range_replica, interp_weight, band_offset, azimuth_rate, tile_owner):
@@ -190,7 +162,7 @@
     width = length // devices
     assert compressed.shape[0] == devices and compressed.shape[3] == width
     turned = lax.all_to_all(compressed, "wide", split_axis=0, concat_axis=2, tiled=True)[0]
-    doppler = azimuth_spectra(turned[:, :, None, :])[:, :, 0]
+    doppler = pulse_transform(turned, PUL_DEV, -1).astype(jnp.bfloat16)
     rim = passed_along(doppler[:, :, :HALO], "wide", -1)
     extended = jnp.concatenate([doppler, rim], axis=2)
     pulses = extended.shape[1]
@@ -214,8 +186,8 @@
     phase_sin = jnp.concatenate([half_sin, jnp.flip(half_sin[1:half], 0)], axis=0)
     focus_real = (moved_real * phase_cos - moved_imag * phase_sin).astype(jnp.bfloat16)
     focus_imag = (moved_real * phase_sin + moved_imag * phase_cos).astype(jnp.bfloat16)
-    image_real, image_imag = pulse_transform(focus_real, focus_imag, PUL_DEV, 1)
-    intensity = (image_real * image_real + image_imag * image_imag).astype(jnp.bfloat16)
+    image = pulse_transform(jnp.stack([focus_real, focus_imag]), PUL_DEV, 1)
+    intensity = (image[0] * image[0] + image[1] * image[1]).astype(jnp.bfloat16)
     block_count = tile_owner.shape[1]
     block_rows = pulses // block_count
     blocks = intensity.reshape(block_count, block_rows * width)

time: 92.7 us -> 91.2 us (0.984)
  matrix products: 10.3 us -> 5.4 us
  local copies, waits for them, and re-layouts: 4.87 us -> 6.8 us
  other arithmetic: 4.34 us -> 6.04 us
    dot_general x16 -> x4, matrix products: 6.31 us -> 1.37 us  [the longest x2 0.77 us: pulse_transform(): jnp.einsum('okrn,rnmc->okmc', head, split, preferred_element_type=jnp.flo...]
    unnamed x8 -> x22, local copies, waits for them, and re-layouts: 0.02 us -> 1.75 us
    convert_element_type x1, other arithmetic: 1.51 us -> 2.49 us  [per_device(): (moved_real * phase_cos - moved_imag * phase_sin).astype(jnp.bfloat16)]
where the time goes in v4:
time: 91.2 us; the launch traced here: 90.7 us
  waiting for transfers between devices  37.8 us (41%)
  starting transfers between devices  28 us (31%)
  local copies, waits for them, and re-layouts  6.8 us (7%)
  other arithmetic  6.04 us (7%)
  Pallas kernels  5.6 us (6%)
  matrix products  5.4 us (6%)
  between operations  1.04 us (1%)
    all_to_all x1, waiting for transfers between devices, per_device(): lax.all_to_all(compressed, 'wide', split_axis=0, concat_axis=2, tiled=True)  31 us
    all_to_all x1, starting transfers between devices, per_device(): lax.all_to_all(compressed, 'wide', split_axis=0, concat_axis=2, tiled=True)  20.7 us
    pallas_call x1, Pallas kernels, range_compress(): pl.pallas_call(range_kernel, in_specs=[whole] * 8, out_specs=whole, out_s...  5.6 us
    all_to_all x1, starting transfers between devices, per_device(): lax.all_to_all(partial, 'narrow', split_axis=0, concat_axis=0, tiled=True)  4 us
    dot_general x8, matrix products, per_device(): jnp.einsum('xpc,cr->xpr', extended, select, preferred_element_type=jnp.fl...  3.87 us
    all_to_all x1, waiting for transfers between devices, per_device(): lax.all_to_all(partial, 'narrow', split_axis=0, concat_axis=0, tiled=True)  3.54 us
    ppermute x1, waiting for transfers between devices, passed_along(): return lax.ppermute(shard, axis, pairs)  3.3 us
    ppermute x1, starting transfers between devices, passed_along(): return lax.ppermute(shard, axis, pairs)  3.29 us
  transfers between devices with their start and end apart: 3, of which 3 were waited for; matrix products, arithmetic and copies ran while one was open for 4% of the time, Pallas kernels for 0%

profile of v4, /device:TPU:1, one launch (start us, length us, event | category | flops | bytes accessed | tf_op | source)
XLA Modules:
  0.0 90.7 jit_solution(1868173963965063494)
XLA Ops:
  0.0 0.8 pad.4
  0.8 0.7 reshape.343.replica_ref
  1.4 5.6 %shard_map.190 = bf16[2048,128]{1,0:T(8,128)(2,1)} custom-call(bf16[2,1024,128]{2,1,0:T(8,128)(2,1)} %bitcast.127, bf16[256,128]{1,0:T(8,128)(2,1)} %reshape.343.replica_ref, bf16[256,256]{1,0:T(8,128)(2,1)} %constant.70.clone.fwd_ref.inv_t_ref, bf16[256,256]{1,0:T(8,128)(2,1)} %constant.71.clone.fwd_t_ref.inv_ref, ...), custom_call_target="tpu_custom_call" | custom-call | flops 603979776 | bytes 1048576 | tf_op jit(solution)/shard_map/pallas_call | solution.py:107
  7.0 0.0 copy-start.10
  7.0 0.0 copy-start.5
  7.0 20.7 %all-to-all-start = ((bf16[128,2,8,128]{3,2,1,0:T(8,128)(2,1)}), bf16[128,2,8,128]{3,2,1,0:T(8,128)(2,1)S(1)}, u32[]{:S(2)}, u32[]{:S(2)}) async-start(bf16[128,2,8,128]{3,2,1,0:T(8,128)(2,1)} %bitcast.118), calls=%async_computation | async-start | bytes 1048576 | tf_op jit(solution)/shard_map/all_to_all | solution.py:164
  27.8 0.0 copy-done.10
  27.8 0.0 copy-done.5
  27.8 0.0 copy-done.8
  27.9 0.1 broadcast_divide_fusion
  28.0 1.0 %divide_cosine_fusion = (f32[1,513,128]{2,1,0:T(8,128)S(1)}, f32[1,513,128]{2,1,0:T(8,128)S(1)}) fusion(f32[128]{0:T(128)S(1)} %copy-done.8, f32[513]{0:T(1024)S(1)} %fusion.65), kind=kLoop, calls=%fused_computation.66 | loop fusion | flops 65664 | bytes 527876 | tf_op jit(solution)/shard_map/cos | solution.py:183
  29.0 0.0 copy-start.7
  29.0 1.0 %slice_cosine_fusion = (f32[511,128]{1,0:T(8,128)S(1)}, f32[511,128]{1,0:T(8,128)S(1)}) fusion(f32[513,128]{1,0:T(8,128)S(1)} %broadcast_divide_fusion), kind=kLoop, calls=%fused_computation.64 | loop fusion | bytes 784896 | tf_op jit(solution)/shard_map/cos | solution.py:183
  30.0 31.0 %all-to-all-done = bf16[128,2,8,128]{3,2,1,0:T(8,128)(2,1)S(1)} async-done(((bf16[128,2,8,128]{3,2,1,0:T(8,128)(2,1)}), bf16[128,2,8,128]{3,2,1,0:T(8,128)(2,1)S(1)}, u32[]{:S(2)}, u32[]{:S(2)}) %all-to-all-start) | async-done | bytes 524320 | tf_op jit(solution)/shard_map/all_to_all | solution.py:164
  61.0 0.0 copy-start
  61.0 0.0 copy-start.4
  61.0 0.0 copy-done.7
  61.0 0.4 convolution_bitcast_fusion.1
  61.5 0.4 copy-done
  61.9 0.0 copy-done.4
  61.9 0.3 subtract_convert_fusion.2
  62.2 0.1 maximum_bitcast_fusion
  62.3 0.5 copy-done.1
  62.8 0.3 fusion.1
  63.1 0.0 copy-start.9
  63.1 0.3 copy.86
  63.5 0.2 copy.53
  63.7 3.3 %collective-permute-start = (bf16[2,1024,31]{1,2,0:T(8,128)(2,1)S(1)}, bf16[2,1024,31]{1,2,0:T(8,128)(2,1)S(1)}, u32[]{:S(2)}, u32[]{:S(2)}) collective-permute-start(bf16[2,1024,31]{1,2,0:T(8,128)(2,1)S(1)} %slice.162), channel_id=1, source_target_pairs={{4,0},{8,4},{12,8},{16,12},{20,16},{24,20},{28,24},{32,28},{36,32}... | collective-permute-start | bytes 380936 | tf_op jit(solution)/shard_map/ppermute | solution.py:21
  67.0 0.0 copy-done.9
  67.0 0.3 rev.7
  67.4 0.3 rev.8
  67.7 0.1 convert_reduce_fusion
  67.8 3.3 %collective-permute-done = bf16[2,1024,31]{1,2,0:T(8,128)(2,1)S(1)} collective-permute-done((bf16[2,1024,31]{1,2,0:T(8,128)(2,1)S(1)}, bf16[2,1024,31]{1,2,0:T(8,128)(2,1)S(1)}, u32[]{:S(2)}, u32[]{:S(2)}) %collective-permute-start) | collective-permute-done | bytes 127008 | tf_op jit(solution)/shard_map/ppermute | solution.py:21
  71.1 0.5 fusion.29
  71.6 0.5 fusion.32
  72.1 0.5 fusion.35
  72.6 0.5 fusion.38
  73.1 0.5 fusion.41
  73.6 0.5 fusion.44
  74.1 0.5 fusion.47
  74.6 0.5 fusion.50
  75.1 2.5 %subtract_convert_fusion.1 = (bf16[1,1024,128]{2,1,0:T(8,128)(2,1)S(1)}, f32[1,1024,128]{2,1,0:T(8,128)S(1)}, f32[1,1024,128]{2,1,0:T(8,128)S(1)}) fusion(f32[1,511,128]{2,1,0:T(8,128)S(1)} %bitcast.112, f32[1,513,128]{2,1,0:T(8,128)S(1)} %get-tuple-element.23, f32[1,511,128]{2,1,0:T(8,128)S(1)} %bitcast.110, f32[1,513,128]{2,1,0:T(8,128)S(1)} %get-tuple-element.22, ...), kind=kLoop, calls=%fused_computation.57 | loop fusion | flops 4718592 | bytes 10780672 | tf_op jit(solution)/shard_map/convert_element_type | solution.py:187
  77.6 0.1 add_convert_fusion.1
  77.7 0.0 copy-start.6
  77.7 0.2 copy.55
  77.9 0.0 copy-start.3
  77.9 0.2 copy.54
  78.1 0.3 copy-done.6
  78.4 0.3 convolution_bitcast_fusion
  78.8 0.0 copy-done.3
  78.8 0.0 copy-start.2
  78.8 0.3 subtract_convert_fusion
  79.2 0.1 pad_maximum_fusion.3
  79.2 0.5 copy-done.2
  79.7 0.3 convolution_bitcast_fusion.2
  80.0 0.1 fusion.3
  80.1 0.2 copy.57
  80.3 0.1 convert_element_type.59
  80.4 0.2 fusion.25
  80.5 0.7 copy.59
  81.2 4.0 %all-to-all-start.1 = ((f32[4,64,128]{2,1,0:T(8,128)}), f32[4,64,128]{2,1,0:T(8,128)S(1)}, u32[]{:S(2)}, u32[]{:S(2)}) async-start(f32[4,64,128]{2,1,0:T(8,128)} %copy.59), calls=%async_computation.1 | async-start | bytes 262144 | tf_op jit(solution)/shard_map/all_to_all | solution.py:205
  85.2 0.6 fusion.72
  86.5 3.5 %all-to-all-done.1 = f32[4,64,128]{2,1,0:T(8,128)S(1)} async-done(((f32[4,64,128]{2,1,0:T(8,128)}), f32[4,64,128]{2,1,0:T(8,128)S(1)}, u32[]{:S(2)}, u32[]{:S(2)}) %all-to-all-start.1) | async-done | bytes 131104 | tf_op jit(solution)/shard_map/all_to_all | solution.py:205
  90.1 0.6 divide_bitcast_fusion
  (9 shorter events, 0.1 us)
Async XLA Ops:
  7.0 20.7 %copy-start.10 = (s32[128]{0:T(128)S(1)}, s32[128]{0:T(128)}, u32[]{:S(2)}) copy-start(s32[128]{0:T(128)} %param.23) | copy-start | bytes 1540
  7.0 20.8 %copy-start.5 = (f32[8,1024]{1,0:T(8,128)S(1)}, f32[8,1024]{1,0:T(8,128)}, u32[]{:S(2)}) copy-start(f32[8,1024]{1,0:T(8,128)} %param.22) | copy-start | bytes 98308
  7.0 20.8 %copy-start.8 = (f32[128]{0:T(128)S(1)}, f32[128]{0:T(128)}, u32[]{:S(2)}) copy-start(f32[128]{0:T(128)} %param.24) | copy-start | bytes 1540
  7.0 53.9 %all-to-all-start = ((bf16[128,2,8,128]{3,2,1,0:T(8,128)(2,1)}), bf16[128,2,8,128]{3,2,1,0:T(8,128)(2,1)S(1)}, u32[]{:S(2)}, u32[]{:S(2)}) async-start(bf16[128,2,8,128]{3,2,1,0:T(8,128)(2,1)} %bitcast.118), calls=%async_computation | async-start | bytes 1048576 | tf_op jit(solution)/shard_map/all_to_all | solution.py:164
  29.0 32.0 %copy-start.7 = (bf16[2,8,2,8,1]{3,1,2,4,0:T(8,128)(2,1)S(1)}, bf16[2,8,2,8,1]{3,1,2,4,0:T(8,128)(2,1)}, u32[]{:S(2)}) copy-start(bf16[2,8,2,8,1]{3,1,2,4,0:T(8,128)(2,1)} %constant.86) | copy-start | bytes 1540
  61.0 0.8 copy-start
  61.0 0.9 copy-start.4
  61.9 0.9 copy-start.1
  63.1 3.9 %copy-start.9 = (s32[4,16]{1,0:T(4,128)S(1)}, s32[4,16]{1,0:T(4,128)}, u32[]{:S(2)}) copy-start(s32[4,16]{1,0:T(4,128)} %param.25) | copy-start | bytes 772
  63.7 7.4 %collective-permute-start = (bf16[2,1024,31]{1,2,0:T(8,128)(2,1)S(1)}, bf16[2,1024,31]{1,2,0:T(8,128)(2,1)S(1)}, u32[]{:S(2)}, u32[]{:S(2)}) collective-permute-start(bf16[2,1024,31]{1,2,0:T(8,128)(2,1)S(1)} %slice.162), channel_id=1, source_target_pairs={{4,0},{8,4},{12,8},{16,12},{20,16},{24,20},{28,24},{32,28},{36,32}... | collective-permute-start | bytes 380936 | tf_op jit(solution)/shard_map/ppermute | solution.py:21
  77.7 0.7 copy-start.6
  77.9 0.9 copy-start.3
  78.8 0.9 %copy-start.2 = (bf16[2,128,2,128,1]{3,1,2,4,0:T(8,128)(2,1)S(1)}, bf16[2,128,2,128,1]{3,1,2,4,0:T(8,128)(2,1)}, u32[]{:S(2)}) copy-start(bf16[2,128,2,128,1]{3,1,2,4,0:T(8,128)(2,1)} %constant.84) | copy-start | bytes 393220
  81.2 8.8 %all-to-all-start.1 = ((f32[4,64,128]{2,1,0:T(8,128)}), f32[4,64,128]{2,1,0:T(8,128)S(1)}, u32[]{:S(2)}, u32[]{:S(2)}) async-start(f32[4,64,128]{2,1,0:T(8,128)} %copy.59), calls=%async_computation.1 | async-start | bytes 262144 | tf_op jit(solution)/shard_map/all_to_all | solution.py:205

commit v5 on v4

--- a/solution.py
+++ b/solution.py
@@ -154,6 +154,60 @@
     return out.reshape(2, length, width)
 
 
+def migrate_kernel(dop_ref, rim_ref, offset_ref, weight_ref, cos_ref, sin_ref, out_ref):
+    rows_total, width = dop_ref.shape[1], dop_ref.shape[2]
+    taps = weight_ref.shape[1]
+    span = 2 * width
+    column = lax.broadcasted_iota(jnp.int32, (span, width), 0)
+    first = lax.broadcasted_iota(jnp.int32, (span, width), 1) + offset_ref[...]
+    block = 256
+    for start in range(0, rows_total, block):
+        rows = pl.ds(start, block)
+        ext = jnp.concatenate(
+            [
+                jnp.concatenate([dop_ref[0, rows, :], rim_ref[0, rows, :]], axis=1),
+                jnp.concatenate([dop_ref[1, rows, :], rim_ref[1, rows, :]], axis=1),
+            ],
+            axis=0,
+        )
+        weights = weight_ref[rows, :]
+        moved = jnp.zeros((2 * block, width), jnp.float32)
+        for tap in range(taps):
+            select = (column == first + tap).astype(jnp.bfloat16)
+            picked = jnp.dot(ext, select, preferred_element_type=jnp.float32)
+            weight = weights[:, tap : tap + 1]
+            moved = moved + jnp.concatenate([weight, weight], axis=0) * picked
+        moved_real, moved_imag = moved[:block], moved[block:]
+        phase_cos, phase_sin = cos_ref[rows, :], sin_ref[rows, :]
+        out_ref[0, rows, :] = (moved_real * phase_cos - moved_imag * phase_sin).astype(jnp.bfloat16)
+        out_ref[1, rows, :] = (moved_real * phase_sin + moved_imag * phase_cos).astype(jnp.bfloat16)
+
+
+def migrate_and_focus(doppler, rim, band_offset, interp_weight, phase_cos, phase_sin):
+    _, rows, width = doppler.shape
+    taps = interp_weight.shape[0]
+    rim = jnp.pad(rim, ((0, 0), (0, 0), (0, width - rim.shape[2])))
+    whole = pl.BlockSpec(memory_space=pltpu.VMEM)
+    return pl.pallas_call(
+        migrate_kernel,
+        in_specs=[whole] * 6,
+        out_specs=whole,
+        out_shape=jax.ShapeDtypeStruct((2, rows, width), jnp.bfloat16),
+        cost_estimate=pl.CostEstimate(
+            flops=taps * 2 * (2 * rows) * (2 * width) * width,
+            bytes_accessed=2 * rows * width * (2 + 2 + 2 + 8),
+            transcendentals=0,
+        ),
+    )(
+        doppler,
+        rim,
+        band_offset.reshape(1, width),
+        interp_weight.T,
+        phase_cos,
+        phase_sin,
+    )
+
+
 def per_device(raw_echo, range_replica, interp_weight, band_offset, azimuth_rate, tile_owner):
     echo = raw_echo[:, 0]
     length = echo.shape[2]
@@ -164,18 +218,7 @@
     turned = lax.all_to_all(compressed, "wide", split_axis=0, concat_axis=2, tiled=True)[0]
     doppler = pulse_transform(turned, PUL_DEV, -1).astype(jnp.bfloat16)
     rim = passed_along(doppler[:, :, :HALO], "wide", -1)
-    extended = jnp.concatenate([doppler, rim], axis=2)
-    pulses = extended.shape[1]
-    columns = jnp.arange(width + HALO, dtype=jnp.int32)
-    bins = jnp.arange(width, dtype=jnp.int32) + band_offset
-    moved_real = jnp.zeros((pulses, width), jnp.float32)
-    moved_imag = jnp.zeros((pulses, width), jnp.float32)
-    for tap_index in range(interp_weight.shape[0]):
-        select = (columns[:, None] == (bins + tap_index)[None, :]).astype(jnp.bfloat16)
-        picked = jnp.einsum("xpc,cr->xpr", extended, select, preferred_element_type=jnp.float32)
-        weight = interp_weight[tap_index][:, None]
-        moved_real = moved_real + weight * picked[0]
-        moved_imag = moved_imag + weight * picked[1]
+    pulses = doppler.shape[1]
     half = pulses // 2
     freq = jnp.arange(half + 1, dtype=jnp.int32)
     shifted = ((freq + half) % pulses - half).astype(jnp.float32) / pulses
@@ -184,9 +227,8 @@
     half_sin = jnp.sin(phase)
     phase_cos = jnp.concatenate([half_cos, jnp.flip(half_cos[1:half], 0)], axis=0)
     phase_sin = jnp.concatenate([half_sin, jnp.flip(half_sin[1:half], 0)], axis=0)
-    focus_real = (moved_real * phase_cos - moved_imag * phase_sin).astype(jnp.bfloat16)
-    focus_imag = (moved_real * phase_sin + moved_imag * phase_cos).astype(jnp.bfloat16)
-    image = pulse_transform(jnp.stack([focus_real, focus_imag]), PUL_DEV, 1)
+    focused = migrate_and_focus(doppler, rim, band_offset, interp_weight, phase_cos, phase_sin)
+    image = pulse_transform(focused, PUL_DEV, 1)
     intensity = (image[0] * image[0] + image[1] * image[1]).astype(jnp.bfloat16)
     block_count = tile_owner.shape[1]
     block_rows = pulses // block_count

time: 91.2 us -> 95.5 us (1.047)
  Pallas kernels: 5.6 us -> 10.5 us
  matrix products: 5.4 us -> 2.68 us
  local copies, waits for them, and re-layouts: 6.8 us -> 9.24 us
  waiting for transfers between devices: 37.8 us -> 39.6 us
  other arithmetic: 6.04 us -> 4.31 us
    pallas_call x0 -> x1, Pallas kernels: none -> 4.9 us  [migrate_and_focus(): pl.pallas_call(migrate_kernel, in_specs=[whole] * 6, out_specs=whole, out...]
    ppermute x1, waiting for transfers between devices: 3.3 us -> 7.49 us  [passed_along(): return lax.ppermute(shard, axis, pairs)]
    dot_general x8 -> x0, matrix products: 3.87 us -> none  [per_device(): jnp.einsum('xpc,cr->xpr', extended, select, preferred_element_type=jnp.fl...]
    unnamed x22 -> x23, local copies, waits for them, and re-layouts: 1.75 us -> 4.85 us
    convert_element_type x2 -> x0, other arithmetic: 2.64 us -> none  [the longest x1 2.49 us: per_device(): (moved_real * phase_cos - moved_imag * phase_sin).astype(jnp.bfloat16)]
    all_to_all x1, waiting for transfers between devices: 31 us -> 28.6 us  [per_device(): lax.all_to_all(compressed, 'wide', split_axis=0, concat_axis=2, tiled=True)]
    dot_general x2, matrix products: 0.77 us -> 1.92 us  [pulse_transform(): jnp.einsum('okrn,rnmc->okmc', head, split, preferred_element_type=jnp.flo...]
    concatenate x0 -> x1, other arithmetic: none -> 1.05 us  [per_device(): jnp.concatenate([half_cos, jnp.flip(half_cos[1:half], 0)], axis=0)]
  transfers between devices with their start and end apart: 3 -> 3, of which waited for: 3 -> 3; matrix products, arithmetic and copies ran while one was open for 4% -> 5% of each run, Pallas kernels for 0% -> 0%
where the time goes in v5:
time: 95.5 us; the launch traced here: 94.9 us
  waiting for transfers between devices  39.6 us (41%)
  starting transfers between devices  27.7 us (29%)
  Pallas kernels  10.5 us (11%)
  local copies, waits for them, and re-layouts  9.24 us (10%)
  other arithmetic  4.31 us (5%)
  matrix products  2.68 us (3%)
    all_to_all x1, waiting for transfers between devices, per_device(): lax.all_to_all(compressed, 'wide', split_axis=0, concat_axis=2, tiled=True)  28.6 us
    all_to_all x1, starting transfers between devices, per_device(): lax.all_to_all(compressed, 'wide', split_axis=0, concat_axis=2, tiled=True)  20.6 us
    ppermute x1, waiting for transfers between devices, passed_along(): return lax.ppermute(shard, axis, pairs)  7.49 us
    pallas_call x1, Pallas kernels, range_compress(): pl.pallas_call(range_kernel, in_specs=[whole] * 8, out_specs=whole, out_s...  5.59 us
    pallas_call x1, Pallas kernels, migrate_and_focus(): pl.pallas_call(migrate_kernel, in_specs=[whole] * 6, out_specs=whole, out...  4.9 us
    unnamed x23, local copies, waits for them, and re-layouts  4.85 us
    all_to_all x1, starting transfers between devices, per_device(): lax.all_to_all(partial, 'narrow', split_axis=0, concat_axis=0, tiled=True)  4 us
    all_to_all x1, waiting for transfers between devices, per_device(): lax.all_to_all(partial, 'narrow', split_axis=0, concat_axis=0, tiled=True)  3.54 us
  transfers between devices with their start and end apart: 3, of which 3 were waited for; matrix products, arithmetic and copies ran while one was open for 5% of the time, Pallas kernels for 0%

profile of v5, /device:TPU:1, one launch (start us, length us, event | category | flops | bytes accessed | tf_op | source)
XLA Modules:
  0.0 94.9 jit_solution(7943907006369517846)
XLA Ops:
  0.0 0.8 pad.8
  0.8 0.7 reshape.70.replica_ref
  1.4 5.6 %shard_map.190 = bf16[2048,128]{1,0:T(8,128)(2,1)} custom-call(bf16[2,1024,128]{2,1,0:T(8,128)(2,1)} %bitcast.84, bf16[256,128]{1,0:T(8,128)(2,1)} %reshape.70.replica_ref, bf16[256,256]{1,0:T(8,128)(2,1)} %constant.57.clone.fwd_ref.inv_t_ref, bf16[256,256]{1,0:T(8,128)(2,1)} %constant.58.clone.fwd_t_ref.inv_ref, ...), custom_call_target="tpu_custom_call" | custom-call | flops 603979776 | bytes 1048576 | tf_op jit(solution)/shard_map/pallas_call | solution.py:107
  7.0 20.6 %all-to-all-start = ((bf16[128,2,8,128]{3,2,1,0:T(8,128)(2,1)}), bf16[128,2,8,128]{3,2,1,0:T(8,128)(2,1)S(1)}, u32[]{:S(2)}, u32[]{:S(2)}) async-start(bf16[128,2,8,128]{3,2,1,0:T(8,128)(2,1)} %bitcast.81), calls=%async_computation | async-start | bytes 1048576 | tf_op jit(solution)/shard_map/all_to_all | solution.py:218
  27.6 0.0 copy-start.10
  27.6 0.6 copy-done.10
  28.3 1.0 %divide_sine_fusion = (f32[513,128]{1,0:T(8,128)S(1)}, f32[513,128]{1,0:T(8,128)S(1)}) fusion(f32[128]{0:T(128)S(1)} %copy-done.10, f32[513]{0:T(1024)S(1)} %fusion.19), kind=kLoop, calls=%fused_computation.29 | loop fusion | flops 65664 | bytes 527876 | tf_op jit(solution)/shard_map/sin | solution.py:227
  29.3 0.3 rev.7
  29.7 0.0 copy-start.6
  29.7 0.3 rev.8
  30.0 0.4 copy-done.6
  30.4 1.0 %copy.49 = f32[8,1024]{0,1:T(8,128)} copy(f32[8,1024]{1,0:T(8,128)S(1)} %copy-done.6) | data formatting | bytes 65536 | tf_op args[2]
  31.4 0.0 copy-start.9
  31.4 0.7 copy-done.9
  32.1 0.1 convert_reduce_fusion
  32.2 0.0 copy-start.8
  32.2 28.6 %all-to-all-done = bf16[128,2,8,128]{3,2,1,0:T(8,128)(2,1)S(1)} async-done(((bf16[128,2,8,128]{3,2,1,0:T(8,128)(2,1)}), bf16[128,2,8,128]{3,2,1,0:T(8,128)(2,1)S(1)}, u32[]{:S(2)}, u32[]{:S(2)}) %all-to-all-start) | async-done | bytes 524320 | tf_op jit(solution)/shard_map/all_to_all | solution.py:218
  60.8 0.0 copy-done.8
  60.9 0.0 copy-start.1
  60.9 0.0 copy-start.5
  60.9 0.4 convolution_bitcast_fusion.1
  61.3 0.4 copy-done.1
  61.7 0.0 copy-done.5
  61.7 0.3 subtract_convert_fusion.1
  62.1 0.0 copy-start.2
  62.1 0.1 maximum_bitcast_fusion
  62.2 0.8 copy-done.2
  63.0 0.3 fusion.1
  63.3 0.3 copy.85
  63.7 0.0 copy-start
  63.7 3.1 %collective-permute-start = (bf16[2,1024,31]{2,1,0:T(8,128)(2,1)S(1)}, bf16[2,1024,31]{2,1,0:T(8,128)(2,1)S(1)}, u32[]{:S(2)}, u32[]{:S(2)}) collective-permute-start(bf16[2,1024,31]{2,1,0:T(8,128)(2,1)S(1)} %bitcast.82), channel_id=1, source_target_pairs={{4,0},{8,4},{12,8},{16,12},{20,16},{24,20},{28,24},{32,28},{36,32}... | collective-permute-start | bytes 380936 | tf_op jit(solution)/shard_map/ppermute | solution.py:21
  66.8 1.0 %pad_maximum_fusion = (f32[1024,128]{1,0:T(8,128)}, f32[1024,128]{1,0:T(8,128)}) fusion(f32[511,128]{1,0:T(8,128)S(1)} %rev.7, f32[513,128]{1,0:T(8,128)S(1)} %get-tuple-element.10, f32[511,128]{1,0:T(8,128)S(1)} %rev.8, f32[513,128]{1,0:T(8,128)S(1)} %get-tuple-element.9), kind=kLoop, calls=%fused_computation.11 | loop fusion | flops 262144 | bytes 2097152 | tf_op jit(solution)/shard_map/concatenate | solution.py:228
  67.8 0.0 copy-done
  67.8 7.5 %collective-permute-done = bf16[2,1024,31]{2,1,0:T(8,128)(2,1)S(1)} collective-permute-done((bf16[2,1024,31]{2,1,0:T(8,128)(2,1)S(1)}, bf16[2,1024,31]{2,1,0:T(8,128)(2,1)S(1)}, u32[]{:S(2)}, u32[]{:S(2)}) %collective-permute-start) | collective-permute-done | bytes 127008 | tf_op jit(solution)/shard_map/ppermute | solution.py:21
  75.3 0.9 pad.9.rim_ref
  76.2 0.0 copy-start.7
  76.2 4.9 %shard_map.191 = bf16[2,1024,128]{2,1,0:T(8,128)(2,1)} custom-call(bf16[2,1024,128]{2,1,0:T(8,128)(2,1)} %bitcast.83, bf16[2,1024,128]{2,1,0:T(8,128)(2,1)} %pad.9.rim_ref, s32[1,128]{1,0:T(1,128)} %bitcast.85, f32[1024,8]{1,0:T(8,128)} %bitcast.80, f32[1024,128]{1,0:T(8,128)} %get-tuple-element.11.cos_ref, f32[1024,128]{1,0:T(8,128)} %get-tuple-element.12.sin_ref), custom_call_target="tpu_custom_call" | custom-call | flops 1073741824 | bytes 3670016 | tf_op jit(solution)/shard_map/pallas_call | solution.py:191
  81.1 0.0 copy-done.7
  81.1 0.0 copy-start.4
  81.1 1.5 %convolution_bitcast_fusion = f32[2,8,128,128]{3,1,2,0:T(8,128)S(1)} fusion(bf16[2,8,2,8,1]{3,1,2,4,0:T(8,128)(2,1)S(1)} %copy-done.7, bf16[2,8,128,128]{3,2,1,0:T(8,128)(2,1)} %bitcast.79), kind=kOutput, calls=%fused_computation | convolution fusion | flops 8388608 | bytes 1573376 | tf_op jit(solution)/shard_map/okrn,rnmc->okmc/dot_general | solution.py:148
  82.6 0.0 copy-done.4
  82.7 0.3 subtract_convert_fusion
  83.0 0.0 copy-start.3
  83.0 0.1 pad_maximum_fusion.2
  83.1 0.8 copy-done.3
  83.9 0.3 convolution_bitcast_fusion.2
  84.2 0.1 fusion.3
  84.3 0.2 copy.52
  84.5 0.1 convert_element_type.39
  84.6 0.2 fusion.11
  84.8 0.6 copy.54
  85.4 4.0 %all-to-all-start.1 = ((f32[4,64,128]{2,1,0:T(8,128)}), f32[4,64,128]{2,1,0:T(8,128)S(1)}, u32[]{:S(2)}, u32[]{:S(2)}) async-start(f32[4,64,128]{2,1,0:T(8,128)} %copy.54), calls=%async_computation.1 | async-start | bytes 262144 | tf_op jit(solution)/shard_map/all_to_all | solution.py:247
  89.4 0.6 fusion.26
  90.7 3.5 %all-to-all-done.1 = f32[4,64,128]{2,1,0:T(8,128)S(1)} async-done(((f32[4,64,128]{2,1,0:T(8,128)}), f32[4,64,128]{2,1,0:T(8,128)S(1)}, u32[]{:S(2)}, u32[]{:S(2)}) %all-to-all-start.1) | async-done | bytes 131104 | tf_op jit(solution)/shard_map/all_to_all | solution.py:247
  94.3 0.6 divide_bitcast_fusion
  (6 shorter events, 0.1 us)
Async XLA Ops:
  7.0 53.8 %all-to-all-start = ((bf16[128,2,8,128]{3,2,1,0:T(8,128)(2,1)}), bf16[128,2,8,128]{3,2,1,0:T(8,128)(2,1)S(1)}, u32[]{:S(2)}, u32[]{:S(2)}) async-start(bf16[128,2,8,128]{3,2,1,0:T(8,128)(2,1)} %bitcast.81), calls=%async_computation | async-start | bytes 1048576 | tf_op jit(solution)/shard_map/all_to_all | solution.py:218
  27.6 0.7 copy-start.10
  29.7 0.8 copy-start.6
  31.4 0.7 copy-start.9
  32.2 28.6 %copy-start.8 = (bf16[2,8,2,8,1]{3,1,2,4,0:T(8,128)(2,1)S(1)}, bf16[2,8,2,8,1]{3,1,2,4,0:T(8,128)(2,1)}, u32[]{:S(2)}) copy-start(bf16[2,8,2,8,1]{3,1,2,4,0:T(8,128)(2,1)} %constant.75) | copy-start | bytes 1540
  60.9 0.8 copy-start.1
  60.9 0.9 copy-start.5
  62.1 0.9 copy-start.2
  63.7 4.2 %copy-start = (bf16[2,128,8,128]{3,2,1,0:T(8,128)(2,1)}, bf16[2,128,8,128]{3,2,1,0:T(8,128)(2,1)S(1)}, u32[]{:S(2)}) copy-start(bf16[2,128,8,128]{3,2,1,0:T(8,128)(2,1)S(1)} %copy.85) | copy-start | bytes 1572868
  63.7 11.7 %collective-permute-start = (bf16[2,1024,31]{2,1,0:T(8,128)(2,1)S(1)}, bf16[2,1024,31]{2,1,0:T(8,128)(2,1)S(1)}, u32[]{:S(2)}, u32[]{:S(2)}) collective-permute-start(bf16[2,1024,31]{2,1,0:T(8,128)(2,1)S(1)} %bitcast.82), channel_id=1, source_target_pairs={{4,0},{8,4},{12,8},{16,12},{20,16},{24,20},{28,24},{32,28},{36,32}... | collective-permute-start | bytes 380936 | tf_op jit(solution)/shard_map/ppermute | solution.py:21
  76.2 4.9 %copy-start.7 = (bf16[2,8,2,8,1]{3,1,2,4,0:T(8,128)(2,1)S(1)}, bf16[2,8,2,8,1]{3,1,2,4,0:T(8,128)(2,1)}, u32[]{:S(2)}) copy-start(bf16[2,8,2,8,1]{3,1,2,4,0:T(8,128)(2,1)} %constant.74) | copy-start | bytes 1540
  81.1 1.5 %copy-start.4 = (f32[8,128]{0,1:T(8,128)S(1)}, f32[8,128]{0,1:T(8,128)}, u32[]{:S(2)}) copy-start(f32[8,128]{0,1:T(8,128)} %constant.67.clone) | copy-start | bytes 12292
  83.0 0.9 copy-start.3
  85.4 8.8 %all-to-all-start.1 = ((f32[4,64,128]{2,1,0:T(8,128)}), f32[4,64,128]{2,1,0:T(8,128)S(1)}, u32[]{:S(2)}, u32[]{:S(2)}) async-start(f32[4,64,128]{2,1,0:T(8,128)} %copy.54), calls=%async_computation.1 | async-start | bytes 262144 | tf_op jit(solution)/shard_map/all_to_all | solution.py:247

commit v6 on v4

--- a/solution.py
+++ b/solution.py
@@ -77,7 +77,15 @@
     fwd, fwd_t = fwd_ref[...], fwd_t_ref[...]
     inv, inv_t = inv_ref[...], inv_t_ref[...]
     fwd_tw, inv_tw = fwd_tw_ref[...], inv_tw_ref[...]
-    rep_real, rep_imag = forward_transposed(replica_ref[...], fwd, fwd_t, fwd_tw)
+    taps = replica_ref[...].astype(jnp.float32)
+    filled = taps.shape[1] // side
+    blank = jnp.zeros((side - filled, side), jnp.float32)
+    pieces = []
+    for part in range(2):
+        pieces += [taps[part : part + 1, n * side : (n + 1) * side] for n in range(filled)]
+        pieces.append(blank)
+    replica = jnp.concatenate(pieces, axis=0).astype(jnp.bfloat16)
+    rep_real, rep_imag = forward_transposed(replica, fwd, fwd_t, fwd_tw)
     rep_real = rep_real * 128.0
     rep_imag = rep_imag * 128.0
     for pulse in range(pulses):
@@ -96,8 +104,7 @@
     pulses, length = echo.shape[1], echo.shape[2]
     side = RSPLIT
     assert length == side * side
-    padded = jnp.pad(range_replica, ((0, 0), (0, length - range_replica.shape[1])))
-    replica = padded.reshape(2 * side, side)
+    assert range_replica.shape[1] % side == 0 and range_replica.shape[1] <= length
     rows = echo.reshape(2, pulses, side, side).transpose(0, 2, 1, 3).reshape(2, side * pulses, side)
     fwd, fwd_t = host_tables(side, -1)
     inv, inv_t = host_tables(side, 1)
@@ -117,7 +124,7 @@
         ),
     )(
         rows,
-        replica,
+        range_replica,
         jnp.asarray(fwd),
         jnp.asarray(fwd_t),
         jnp.asarray(inv),

time: 91.2 us -> 89.8 us (0.985)
  local copies, waits for them, and re-layouts: 6.8 us -> 5.37 us
where the time goes in v6:
time: 89.8 us; the launch traced here: 89.2 us
  waiting for transfers between devices  37.8 us (42%)
  starting transfers between devices  28 us (31%)
  other arithmetic  6.04 us (7%)
  Pallas kernels  5.59 us (6%)
  matrix products  5.4 us (6%)
  local copies, waits for them, and re-layouts  5.37 us (6%)
  between operations  1.03 us (1%)
    all_to_all x1, waiting for transfers between devices, per_device(): lax.all_to_all(compressed, 'wide', split_axis=0, concat_axis=2, tiled=True)  31 us
    all_to_all x1, starting transfers between devices, per_device(): lax.all_to_all(compressed, 'wide', split_axis=0, concat_axis=2, tiled=True)  20.7 us
    pallas_call x1, Pallas kernels, range_compress(): pl.pallas_call(range_kernel, in_specs=[whole] * 8, out_specs=whole, out_s...  5.59 us
    all_to_all x1, starting transfers between devices, per_device(): lax.all_to_all(partial, 'narrow', split_axis=0, concat_axis=0, tiled=True)  4.02 us
    dot_general x8, matrix products, per_device(): jnp.einsum('xpc,cr->xpr', extended, select, preferred_element_type=jnp.fl...  3.87 us
    all_to_all x1, waiting for transfers between devices, per_device(): lax.all_to_all(partial, 'narrow', split_axis=0, concat_axis=0, tiled=True)  3.54 us
    ppermute x1, waiting for transfers between devices, passed_along(): return lax.ppermute(shard, axis, pairs)  3.3 us
    ppermute x1, starting transfers between devices, passed_along(): return lax.ppermute(shard, axis, pairs)  3.29 us
  transfers between devices with their start and end apart: 3, of which 3 were waited for; matrix products, arithmetic and copies ran while one was open for 4% of the time, Pallas kernels for 0%

profile of v6, /device:TPU:1, one launch (start us, length us, event | category | flops | bytes accessed | tf_op | source)
XLA Modules:
  0.0 89.2 jit_solution(7239832178621496091)
XLA Ops:
  0.0 5.6 %shard_map.190 = bf16[2048,128]{1,0:T(8,128)(2,1)} custom-call(bf16[2,1024,128]{2,1,0:T(8,128)(2,1)} %bitcast.127, bf16[2,4096]{1,0:T(2,128)(2,1)} %replica_ref.1, bf16[256,256]{1,0:T(8,128)(2,1)} %constant.68.clone.fwd_ref.inv_t_ref, bf16[256,256]{1,0:T(8,128)(2,1)} %constant.69.clone.fwd_t_ref.inv_ref, bf16[256,256]{1,0:T(8,128)(2,1)} %constant.69.clone.fwd_t_ref.inv_ref, ...), custom_call_target="tpu_custom_call" | custom-call | flops 603979776 | bytes 1048576 | tf_op jit(solution)/shard_map/pallas_call | solution.py:114
  5.6 0.0 copy-start.10
  5.6 0.0 copy-start.5
  5.6 0.0 copy-start.8
  5.6 20.7 %all-to-all-start = ((bf16[128,2,8,128]{3,2,1,0:T(8,128)(2,1)}), bf16[128,2,8,128]{3,2,1,0:T(8,128)(2,1)S(1)}, u32[]{:S(2)}, u32[]{:S(2)}) async-start(bf16[128,2,8,128]{3,2,1,0:T(8,128)(2,1)} %bitcast.118), calls=%async_computation | async-start | bytes 1048576 | tf_op jit(solution)/shard_map/all_to_all | solution.py:171
  26.3 0.0 copy-done.10
  26.4 0.0 copy-done.5
  26.4 0.0 copy-done.8
  26.4 0.1 broadcast_divide_fusion
  26.5 1.0 %divide_cosine_fusion = (f32[1,513,128]{2,1,0:T(8,128)S(1)}, f32[1,513,128]{2,1,0:T(8,128)S(1)}) fusion(f32[128]{0:T(128)S(1)} %copy-done.8, f32[513]{0:T(1024)S(1)} %fusion.65), kind=kLoop, calls=%fused_computation.66 | loop fusion | flops 65664 | bytes 527876 | tf_op jit(solution)/shard_map/cos | solution.py:190
  27.6 0.0 copy-start.7
  27.6 1.0 %slice_cosine_fusion = (f32[511,128]{1,0:T(8,128)S(1)}, f32[511,128]{1,0:T(8,128)S(1)}) fusion(f32[513,128]{1,0:T(8,128)S(1)} %broadcast_divide_fusion), kind=kLoop, calls=%fused_computation.64 | loop fusion | bytes 784896 | tf_op jit(solution)/shard_map/cos | solution.py:190
  28.6 31.0 %all-to-all-done = bf16[128,2,8,128]{3,2,1,0:T(8,128)(2,1)S(1)} async-done(((bf16[128,2,8,128]{3,2,1,0:T(8,128)(2,1)}), bf16[128,2,8,128]{3,2,1,0:T(8,128)(2,1)S(1)}, u32[]{:S(2)}, u32[]{:S(2)}) %all-to-all-start) | async-done | bytes 524320 | tf_op jit(solution)/shard_map/all_to_all | solution.py:171
  59.6 0.0 copy-start
  59.6 0.0 copy-start.4
  59.6 0.0 copy-done.7
  59.6 0.4 convolution_bitcast_fusion.1
  60.0 0.4 copy-done
  60.4 0.0 copy-done.4
  60.4 0.0 copy-start.1
  60.4 0.3 subtract_convert_fusion.2
  60.8 0.1 maximum_bitcast_fusion
  60.9 0.5 copy-done.1
  61.3 0.3 fusion.1
  61.7 0.0 copy-start.9
  61.7 0.3 copy.86
  62.0 0.2 copy.53
  62.3 3.3 %collective-permute-start = (bf16[2,1024,31]{1,2,0:T(8,128)(2,1)S(1)}, bf16[2,1024,31]{1,2,0:T(8,128)(2,1)S(1)}, u32[]{:S(2)}, u32[]{:S(2)}) collective-permute-start(bf16[2,1024,31]{1,2,0:T(8,128)(2,1)S(1)} %slice.162), channel_id=1, source_target_pairs={{4,0},{8,4},{12,8},{16,12},{20,16},{24,20},{28,24},{32,28},{36,32}... | collective-permute-start | bytes 380936 | tf_op jit(solution)/shard_map/ppermute | solution.py:21
  65.6 0.0 copy-done.9
  65.6 0.3 rev.7
  65.9 0.3 rev.8
  66.3 0.1 convert_reduce_fusion
  66.4 3.3 %collective-permute-done = bf16[2,1024,31]{1,2,0:T(8,128)(2,1)S(1)} collective-permute-done((bf16[2,1024,31]{1,2,0:T(8,128)(2,1)S(1)}, bf16[2,1024,31]{1,2,0:T(8,128)(2,1)S(1)}, u32[]{:S(2)}, u32[]{:S(2)}) %collective-permute-start) | collective-permute-done | bytes 127008 | tf_op jit(solution)/shard_map/ppermute | solution.py:21
  69.7 0.5 fusion.29
  70.2 0.5 fusion.32
  70.7 0.5 fusion.35
  71.2 0.5 fusion.38
  71.7 0.5 fusion.41
  72.2 0.5 fusion.44
  72.7 0.5 fusion.47
  73.1 0.5 fusion.50
  73.6 2.5 %subtract_convert_fusion.1 = (bf16[1,1024,128]{2,1,0:T(8,128)(2,1)S(1)}, f32[1,1024,128]{2,1,0:T(8,128)S(1)}, f32[1,1024,128]{2,1,0:T(8,128)S(1)}) fusion(f32[1,511,128]{2,1,0:T(8,128)S(1)} %bitcast.112, f32[1,513,128]{2,1,0:T(8,128)S(1)} %get-tuple-element.23, f32[1,511,128]{2,1,0:T(8,128)S(1)} %bitcast.110, f32[1,513,128]{2,1,0:T(8,128)S(1)} %get-tuple-element.22, ...), kind=kLoop, calls=%fused_computation.57 | loop fusion | flops 4718592 | bytes 10780672 | tf_op jit(solution)/shard_map/convert_element_type | solution.py:194
  76.1 0.1 add_convert_fusion.1
  76.3 0.0 copy-start.6
  76.3 0.2 copy.55
  76.5 0.0 copy-start.3
  76.5 0.2 copy.54
  76.7 0.3 copy-done.6
  77.0 0.3 convolution_bitcast_fusion
  77.3 0.0 copy-done.3
  77.3 0.0 copy-start.2
  77.4 0.3 subtract_convert_fusion
  77.7 0.1 pad_maximum_fusion.3
  77.8 0.5 copy-done.2
  78.2 0.3 convolution_bitcast_fusion.2
  78.5 0.1 fusion.3
  78.6 0.2 copy.57
  78.8 0.1 convert_element_type.57
  78.9 0.2 fusion.25
  79.1 0.7 copy.59
  79.8 4.0 %all-to-all-start.1 = ((f32[4,64,128]{2,1,0:T(8,128)}), f32[4,64,128]{2,1,0:T(8,128)S(1)}, u32[]{:S(2)}, u32[]{:S(2)}) async-start(f32[4,64,128]{2,1,0:T(8,128)} %copy.59), calls=%async_computation.1 | async-start | bytes 262144 | tf_op jit(solution)/shard_map/all_to_all | solution.py:212
  83.8 0.6 fusion.72
  85.1 3.5 %all-to-all-done.1 = f32[4,64,128]{2,1,0:T(8,128)S(1)} async-done(((f32[4,64,128]{2,1,0:T(8,128)}), f32[4,64,128]{2,1,0:T(8,128)S(1)}, u32[]{:S(2)}, u32[]{:S(2)}) %all-to-all-start.1) | async-done | bytes 131104 | tf_op jit(solution)/shard_map/all_to_all | solution.py:212
  88.6 0.6 divide_bitcast_fusion
  (7 shorter events, 0.1 us)
Async XLA Ops:
  5.6 20.7 %copy-start.10 = (s32[128]{0:T(128)S(1)}, s32[128]{0:T(128)}, u32[]{:S(2)}) copy-start(s32[128]{0:T(128)} %param.23) | copy-start | bytes 1540
  5.6 20.8 %copy-start.5 = (f32[8,1024]{1,0:T(8,128)S(1)}, f32[8,1024]{1,0:T(8,128)}, u32[]{:S(2)}) copy-start(f32[8,1024]{1,0:T(8,128)} %param.22) | copy-start | bytes 98308
  5.6 20.8 %copy-start.8 = (f32[128]{0:T(128)S(1)}, f32[128]{0:T(128)}, u32[]{:S(2)}) copy-start(f32[128]{0:T(128)} %param.24) | copy-start | bytes 1540
  5.6 53.9 %all-to-all-start = ((bf16[128,2,8,128]{3,2,1,0:T(8,128)(2,1)}), bf16[128,2,8,128]{3,2,1,0:T(8,128)(2,1)S(1)}, u32[]{:S(2)}, u32[]{:S(2)}) async-start(bf16[128,2,8,128]{3,2,1,0:T(8,128)(2,1)} %bitcast.118), calls=%async_computation | async-start | bytes 1048576 | tf_op jit(solution)/shard_map/all_to_all | solution.py:171
  27.6 32.0 %copy-start.7 = (bf16[2,8,2,8,1]{3,1,2,4,0:T(8,128)(2,1)S(1)}, bf16[2,8,2,8,1]{3,1,2,4,0:T(8,128)(2,1)}, u32[]{:S(2)}) copy-start(bf16[2,8,2,8,1]{3,1,2,4,0:T(8,128)(2,1)} %constant.82) | copy-start | bytes 1540
  59.6 0.8 copy-start
  59.6 0.9 copy-start.4
  60.4 0.9 %copy-start.1 = (bf16[2,128,2,128,1]{3,1,2,0,4:T(8,128)(2,1)S(1)}, bf16[2,128,2,128,1]{3,1,2,0,4:T(8,128)(2,1)}, u32[]{:S(2)}) copy-start(bf16[2,128,2,128,1]{3,1,2,0,4:T(8,128)(2,1)} %constant.83) | copy-start | bytes 393220
  61.7 3.9 %copy-start.9 = (s32[4,16]{1,0:T(4,128)S(1)}, s32[4,16]{1,0:T(4,128)}, u32[]{:S(2)}) copy-start(s32[4,16]{1,0:T(4,128)} %param.25) | copy-start | bytes 772
  62.3 7.4 %collective-permute-start = (bf16[2,1024,31]{1,2,0:T(8,128)(2,1)S(1)}, bf16[2,1024,31]{1,2,0:T(8,128)(2,1)S(1)}, u32[]{:S(2)}, u32[]{:S(2)}) collective-permute-start(bf16[2,1024,31]{1,2,0:T(8,128)(2,1)S(1)} %slice.162), channel_id=1, source_target_pairs={{4,0},{8,4},{12,8},{16,12},{20,16},{24,20},{28,24},{32,28},{36,32}... | collective-permute-start | bytes 380936 | tf_op jit(solution)/shard_map/ppermute | solution.py:21
  76.3 0.7 copy-start.6
  76.5 0.9 copy-start.3
  77.3 0.9 %copy-start.2 = (bf16[2,128,2,128,1]{3,1,2,4,0:T(8,128)(2,1)S(1)}, bf16[2,128,2,128,1]{3,1,2,4,0:T(8,128)(2,1)}, u32[]{:S(2)}) copy-start(bf16[2,128,2,128,1]{3,1,2,4,0:T(8,128)(2,1)} %constant.80) | copy-start | bytes 393220
  79.8 8.8 %all-to-all-start.1 = ((f32[4,64,128]{2,1,0:T(8,128)}), f32[4,64,128]{2,1,0:T(8,128)S(1)}, u32[]{:S(2)}, u32[]{:S(2)}) async-start(f32[4,64,128]{2,1,0:T(8,128)} %copy.59), calls=%async_computation.1 | async-start | bytes 262144 | tf_op jit(solution)/shard_map/all_to_all | solution.py:212

commit v7 on v6

--- a/solution.py
+++ b/solution.py
@@ -88,15 +88,43 @@
     rep_real, rep_imag = forward_transposed(replica, fwd, fwd_t, fwd_tw)
     rep_real = rep_real * 128.0
     rep_imag = rep_imag * 128.0
+    blocks = []
     for pulse in range(pulses):
         rows = pl.ds(pulse, side, stride=pulses)
-        stacked = jnp.concatenate([echo_ref[0, rows, :], echo_ref[1, rows, :]], axis=0)
-        spec_real, spec_imag = forward_transposed(stacked, fwd, fwd_t, fwd_tw)
-        match_real = (spec_real * rep_real + spec_imag * rep_imag).astype(jnp.bfloat16)
-        match_imag = (spec_imag * rep_real - spec_real * rep_imag).astype(jnp.bfloat16)
-        comp_real, comp_imag = inverse_from_transposed(match_real, match_imag, inv, inv_t, inv_tw)
-        wide_ref[pl.ds(pulse, side, stride=2 * pulses), :] = comp_real
-        wide_ref[pl.ds(pulses + pulse, side, stride=2 * pulses), :] = comp_imag
+        blocks.append(jnp.concatenate([echo_ref[0, rows, :], echo_ref[1, rows, :]], axis=0))
+    mid = jnp.dot(fwd, jnp.concatenate(blocks, axis=1), preferred_element_type=jnp.float32)
+    along = lambda x: jnp.concatenate([x] * pulses, axis=1)
+    down = lambda x: jnp.concatenate([x] * pulses, axis=0)
+    turn_real, turn_imag = twist(mid[:side], mid[side:], (along(fwd_tw[0]), along(fwd_tw[1])))
+    by_pulse = lambda x, p: x[:, p * side : (p + 1) * side]
+    stacked = jnp.concatenate(
+        [
+            jnp.concatenate([by_pulse(turn_real, p), by_pulse(turn_imag, p)], axis=1)
+            for p in range(pulses)
+        ],
+        axis=0,
+    )
+    spec = jnp.dot(stacked, fwd_t, preferred_element_type=jnp.float32)
+    spec_real, spec_imag = spec[:, :side], spec[:, side:]
+    rep_real, rep_imag = down(rep_real), down(rep_imag)
+    match_real = (spec_real * rep_real + spec_imag * rep_imag).astype(jnp.bfloat16)
+    match_imag = (spec_imag * rep_real - spec_real * rep_imag).astype(jnp.bfloat16)
+    mid = jnp.dot(
+        jnp.concatenate([match_real, match_imag], axis=1), inv_t, preferred_element_type=jnp.float32
+    )
+    turn_real, turn_imag = twist(mid[:, :side], mid[:, side:], (down(inv_tw[0]), down(inv_tw[1])))
+    rows_of = lambda x, p: x[p * side : (p + 1) * side]
+    stacked = jnp.concatenate(
+        [
+            jnp.concatenate([rows_of(turn_real, p), rows_of(turn_imag, p)], axis=0)
+            for p in range(pulses)
+        ],
+        axis=1,
+    )
+    comp = jnp.dot(inv, stacked, preferred_element_type=jnp.float32)
+    for pulse in range(pulses):
+        wide_ref[pl.ds(pulse, side, stride=2 * pulses), :] = by_pulse(comp[:side], pulse)
+        wide_ref[pl.ds(pulses + pulse, side, stride=2 * pulses), :] = by_pulse(comp[side:], pulse)
     out_ref[...] = wide_ref[...].astype(jnp.bfloat16)
 
 

time: 89.8 us -> 87.6 us (0.976)
  Pallas kernels: 5.59 us -> 3.41 us
    pallas_call x1, Pallas kernels: 5.59 us -> 3.41 us  [range_compress(): pl.pallas_call(range_kernel, in_specs=[whole] * 8, out_specs=whole, out_s...]
where the time goes in v7:
time: 87.6 us; the launch traced here: 87.1 us
  waiting for transfers between devices  37.8 us (43%)
  starting transfers between devices  28 us (32%)
  other arithmetic  6.04 us (7%)
  matrix products  5.41 us (6%)
  local copies, waits for them, and re-layouts  5.37 us (6%)
  Pallas kernels  3.41 us (4%)
  between operations  1.03 us (1%)
    all_to_all x1, waiting for transfers between devices, per_device(): lax.all_to_all(compressed, 'wide', split_axis=0, concat_axis=2, tiled=True)  31 us
    all_to_all x1, starting transfers between devices, per_device(): lax.all_to_all(compressed, 'wide', split_axis=0, concat_axis=2, tiled=True)  20.7 us
    all_to_all x1, starting transfers between devices, per_device(): lax.all_to_all(partial, 'narrow', split_axis=0, concat_axis=0, tiled=True)  3.99 us
    dot_general x8, matrix products, per_device(): jnp.einsum('xpc,cr->xpr', extended, select, preferred_element_type=jnp.fl...  3.88 us
    all_to_all x1, waiting for transfers between devices, per_device(): lax.all_to_all(partial, 'narrow', split_axis=0, concat_axis=0, tiled=True)  3.54 us
    pallas_call x1, Pallas kernels, range_compress(): pl.pallas_call(range_kernel, in_specs=[whole] * 8, out_specs=whole, out_s...  3.41 us
    ppermute x1, waiting for transfers between devices, passed_along(): return lax.ppermute(shard, axis, pairs)  3.3 us
    ppermute x1, starting transfers between devices, passed_along(): return lax.ppermute(shard, axis, pairs)  3.29 us
  transfers between devices with their start and end apart: 3, of which 3 were waited for; matrix products, arithmetic and copies ran while one was open for 4% of the time, Pallas kernels for 0%

profile of v7, /device:TPU:1, one launch (start us, length us, event | category | flops | bytes accessed | tf_op | source)
XLA Modules:
  0.0 87.1 jit_solution(5746665807170064519)
XLA Ops:
  0.0 3.4 %shard_map.190 = bf16[2048,128]{1,0:T(8,128)(2,1)} custom-call(bf16[2,1024,128]{2,1,0:T(8,128)(2,1)} %bitcast.127, bf16[2,4096]{1,0:T(2,128)(2,1)} %replica_ref.1, bf16[256,256]{1,0:T(8,128)(2,1)} %constant.68.clone.fwd_ref.inv_t_ref, bf16[256,256]{1,0:T(8,128)(2,1)} %constant.69.clone.fwd_t_ref.inv_ref, bf16[256,256]{1,0:T(8,128)(2,1)} %constant.69.clone.fwd_t_ref.inv_ref, ...), custom_call_target="tpu_custom_call" | custom-call | flops 603979776 | bytes 1048576 | tf_op jit(solution)/shard_map/pallas_call | solution.py:142
  3.4 0.0 copy-start.10
  3.4 0.0 copy-start.5
  3.4 0.0 copy-start.8
  3.4 20.7 %all-to-all-start = ((bf16[128,2,8,128]{3,2,1,0:T(8,128)(2,1)}), bf16[128,2,8,128]{3,2,1,0:T(8,128)(2,1)S(1)}, u32[]{:S(2)}, u32[]{:S(2)}) async-start(bf16[128,2,8,128]{3,2,1,0:T(8,128)(2,1)} %bitcast.118), calls=%async_computation | async-start | bytes 1048576 | tf_op jit(solution)/shard_map/all_to_all | solution.py:199
  24.2 0.0 copy-done.10
  24.2 0.0 copy-done.5
  24.2 0.0 copy-done.8
  24.2 0.1 broadcast_divide_fusion
  24.4 1.0 %divide_cosine_fusion = (f32[1,513,128]{2,1,0:T(8,128)S(1)}, f32[1,513,128]{2,1,0:T(8,128)S(1)}) fusion(f32[128]{0:T(128)S(1)} %copy-done.8, f32[513]{0:T(1024)S(1)} %fusion.65), kind=kLoop, calls=%fused_computation.66 | loop fusion | flops 65664 | bytes 527876 | tf_op jit(solution)/shard_map/cos | solution.py:218
  25.4 0.0 copy-start.7
  25.4 1.0 %slice_cosine_fusion = (f32[511,128]{1,0:T(8,128)S(1)}, f32[511,128]{1,0:T(8,128)S(1)}) fusion(f32[513,128]{1,0:T(8,128)S(1)} %broadcast_divide_fusion), kind=kLoop, calls=%fused_computation.64 | loop fusion | bytes 784896 | tf_op jit(solution)/shard_map/cos | solution.py:218
  26.4 31.0 %all-to-all-done = bf16[128,2,8,128]{3,2,1,0:T(8,128)(2,1)S(1)} async-done(((bf16[128,2,8,128]{3,2,1,0:T(8,128)(2,1)}), bf16[128,2,8,128]{3,2,1,0:T(8,128)(2,1)S(1)}, u32[]{:S(2)}, u32[]{:S(2)}) %all-to-all-start) | async-done | bytes 524320 | tf_op jit(solution)/shard_map/all_to_all | solution.py:199
  57.4 0.0 copy-start
  57.4 0.0 copy-start.4
  57.4 0.0 copy-done.7
  57.4 0.4 convolution_bitcast_fusion.1
  57.8 0.4 copy-done
  58.2 0.0 copy-done.4
  58.3 0.0 copy-start.1
  58.3 0.3 subtract_convert_fusion.2
  58.6 0.1 maximum_bitcast_fusion
  58.7 0.5 copy-done.1
  59.2 0.3 fusion.1
  59.5 0.0 copy-start.9
  59.5 0.3 copy.86
  59.8 0.2 copy.53
  60.1 3.3 %collective-permute-start = (bf16[2,1024,31]{1,2,0:T(8,128)(2,1)S(1)}, bf16[2,1024,31]{1,2,0:T(8,128)(2,1)S(1)}, u32[]{:S(2)}, u32[]{:S(2)}) collective-permute-start(bf16[2,1024,31]{1,2,0:T(8,128)(2,1)S(1)} %slice.162), channel_id=1, source_target_pairs={{4,0},{8,4},{12,8},{16,12},{20,16},{24,20},{28,24},{32,28},{36,32}... | collective-permute-start | bytes 380936 | tf_op jit(solution)/shard_map/ppermute | solution.py:21
  63.4 0.0 copy-done.9
  63.4 0.3 rev.7
  63.8 0.3 rev.8
  64.1 0.1 convert_reduce_fusion
  64.2 3.3 %collective-permute-done = bf16[2,1024,31]{1,2,0:T(8,128)(2,1)S(1)} collective-permute-done((bf16[2,1024,31]{1,2,0:T(8,128)(2,1)S(1)}, bf16[2,1024,31]{1,2,0:T(8,128)(2,1)S(1)}, u32[]{:S(2)}, u32[]{:S(2)}) %collective-permute-start) | collective-permute-done | bytes 127008 | tf_op jit(solution)/shard_map/ppermute | solution.py:21
  67.5 0.5 fusion.29
  68.0 0.5 fusion.32
  68.5 0.5 fusion.35
  69.0 0.5 fusion.38
  69.5 0.5 fusion.41
  70.0 0.5 fusion.44
  70.5 0.5 fusion.47
  71.0 0.5 fusion.50
  71.5 2.5 %subtract_convert_fusion.1 = (bf16[1,1024,128]{2,1,0:T(8,128)(2,1)S(1)}, f32[1,1024,128]{2,1,0:T(8,128)S(1)}, f32[1,1024,128]{2,1,0:T(8,128)S(1)}) fusion(f32[1,511,128]{2,1,0:T(8,128)S(1)} %bitcast.112, f32[1,513,128]{2,1,0:T(8,128)S(1)} %get-tuple-element.23, f32[1,511,128]{2,1,0:T(8,128)S(1)} %bitcast.110, f32[1,513,128]{2,1,0:T(8,128)S(1)} %get-tuple-element.22, ...), kind=kLoop, calls=%fused_computation.57 | loop fusion | flops 4718592 | bytes 10780672 | tf_op jit(solution)/shard_map/convert_element_type | solution.py:222
  74.0 0.1 add_convert_fusion.1
  74.1 0.0 copy-start.6
  74.1 0.2 copy.55
  74.3 0.0 copy-start.3
  74.3 0.2 copy.54
  74.5 0.3 copy-done.6
  74.8 0.3 convolution_bitcast_fusion
  75.2 0.0 copy-done.3
  75.2 0.0 copy-start.2
  75.2 0.3 subtract_convert_fusion
  75.5 0.1 pad_maximum_fusion.3
  75.6 0.5 copy-done.2
  76.1 0.3 convolution_bitcast_fusion.2
  76.4 0.1 fusion.3
  76.5 0.2 copy.57
  76.6 0.1 convert_element_type.57
  76.8 0.2 fusion.25
  76.9 0.7 copy.59
  77.6 4.0 %all-to-all-start.1 = ((f32[4,64,128]{2,1,0:T(8,128)}), f32[4,64,128]{2,1,0:T(8,128)S(1)}, u32[]{:S(2)}, u32[]{:S(2)}) async-start(f32[4,64,128]{2,1,0:T(8,128)} %copy.59), calls=%async_computation.1 | async-start | bytes 262144 | tf_op jit(solution)/shard_map/all_to_all | solution.py:240
  81.6 0.6 fusion.72
  82.9 3.5 %all-to-all-done.1 = f32[4,64,128]{2,1,0:T(8,128)S(1)} async-done(((f32[4,64,128]{2,1,0:T(8,128)}), f32[4,64,128]{2,1,0:T(8,128)S(1)}, u32[]{:S(2)}, u32[]{:S(2)}) %all-to-all-start.1) | async-done | bytes 131104 | tf_op jit(solution)/shard_map/all_to_all | solution.py:240
  86.4 0.6 divide_bitcast_fusion
  (7 shorter events, 0.1 us)
Async XLA Ops:
  3.4 20.7 %copy-start.10 = (s32[128]{0:T(128)S(1)}, s32[128]{0:T(128)}, u32[]{:S(2)}) copy-start(s32[128]{0:T(128)} %param.23) | copy-start | bytes 1540
  3.4 20.8 %copy-start.5 = (f32[8,1024]{1,0:T(8,128)S(1)}, f32[8,1024]{1,0:T(8,128)}, u32[]{:S(2)}) copy-start(f32[8,1024]{1,0:T(8,128)} %param.22) | copy-start | bytes 98308
  3.4 20.8 %copy-start.8 = (f32[128]{0:T(128)S(1)}, f32[128]{0:T(128)}, u32[]{:S(2)}) copy-start(f32[128]{0:T(128)} %param.24) | copy-start | bytes 1540
  3.4 53.9 %all-to-all-start = ((bf16[128,2,8,128]{3,2,1,0:T(8,128)(2,1)}), bf16[128,2,8,128]{3,2,1,0:T(8,128)(2,1)S(1)}, u32[]{:S(2)}, u32[]{:S(2)}) async-start(bf16[128,2,8,128]{3,2,1,0:T(8,128)(2,1)} %bitcast.118), calls=%async_computation | async-start | bytes 1048576 | tf_op jit(solution)/shard_map/all_to_all | solution.py:199
  25.4 32.0 %copy-start.7 = (bf16[2,8,2,8,1]{3,1,2,4,0:T(8,128)(2,1)S(1)}, bf16[2,8,2,8,1]{3,1,2,4,0:T(8,128)(2,1)}, u32[]{:S(2)}) copy-start(bf16[2,8,2,8,1]{3,1,2,4,0:T(8,128)(2,1)} %constant.82) | copy-start | bytes 1540
  57.4 0.8 copy-start
  57.4 0.9 copy-start.4
  58.3 0.9 %copy-start.1 = (bf16[2,128,2,128,1]{3,1,2,0,4:T(8,128)(2,1)S(1)}, bf16[2,128,2,128,1]{3,1,2,0,4:T(8,128)(2,1)}, u32[]{:S(2)}) copy-start(bf16[2,128,2,128,1]{3,1,2,0,4:T(8,128)(2,1)} %constant.83) | copy-start | bytes 393220
  59.5 3.9 %copy-start.9 = (s32[4,16]{1,0:T(4,128)S(1)}, s32[4,16]{1,0:T(4,128)}, u32[]{:S(2)}) copy-start(s32[4,16]{1,0:T(4,128)} %param.25) | copy-start | bytes 772
  60.1 7.4 %collective-permute-start = (bf16[2,1024,31]{1,2,0:T(8,128)(2,1)S(1)}, bf16[2,1024,31]{1,2,0:T(8,128)(2,1)S(1)}, u32[]{:S(2)}, u32[]{:S(2)}) collective-permute-start(bf16[2,1024,31]{1,2,0:T(8,128)(2,1)S(1)} %slice.162), channel_id=1, source_target_pairs={{4,0},{8,4},{12,8},{16,12},{20,16},{24,20},{28,24},{32,28},{36,32}... | collective-permute-start | bytes 380936 | tf_op jit(solution)/shard_map/ppermute | solution.py:21
  74.1 0.7 copy-start.6
  74.3 0.9 copy-start.3
  75.2 0.9 %copy-start.2 = (bf16[2,128,2,128,1]{3,1,2,4,0:T(8,128)(2,1)S(1)}, bf16[2,128,2,128,1]{3,1,2,4,0:T(8,128)(2,1)}, u32[]{:S(2)}) copy-start(bf16[2,128,2,128,1]{3,1,2,4,0:T(8,128)(2,1)} %constant.80) | copy-start | bytes 393220
  77.6 8.8 %all-to-all-start.1 = ((f32[4,64,128]{2,1,0:T(8,128)}), f32[4,64,128]{2,1,0:T(8,128)S(1)}, u32[]{:S(2)}, u32[]{:S(2)}) async-start(f32[4,64,128]{2,1,0:T(8,128)} %copy.59), calls=%async_computation.1 | async-start | bytes 262144 | tf_op jit(solution)/shard_map/all_to_all | solution.py:240

commit v8 on v7

--- a/solution.py
+++ b/solution.py
@@ -207,10 +207,10 @@
     moved_imag = jnp.zeros((pulses, width), jnp.float32)
     for tap_index in range(interp_weight.shape[0]):
         select = (columns[:, None] == (bins + tap_index)[None, :]).astype(jnp.bfloat16)
-        picked = jnp.einsum("xpc,cr->xpr", extended, select, preferred_element_type=jnp.float32)
+        picked = jnp.einsum("xpc,cr->xpr", extended, select, preferred_element_type=jnp.bfloat16)
         weight = interp_weight[tap_index][:, None]
-        moved_real = moved_real + weight * picked[0]
-        moved_imag = moved_imag + weight * picked[1]
+        moved_real = moved_real + weight * picked[0].astype(jnp.float32)
+        moved_imag = moved_imag + weight * picked[1].astype(jnp.float32)
     half = pulses // 2
     freq = jnp.arange(half + 1, dtype=jnp.int32)
     shifted = ((freq + half) % pulses - half).astype(jnp.float32) / pulses

time: 87.6 us -> 87.3 us (level)
  no operation moved by 1% of the time
where the time goes in v8:
time: 87.3 us; the launch traced here: 86.8 us
  waiting for transfers between devices  37.8 us (43%)
  starting transfers between devices  28 us (32%)
  other arithmetic  5.7 us (7%)
  matrix products  5.47 us (6%)
  local copies, waits for them, and re-layouts  5.37 us (6%)
  Pallas kernels  3.41 us (4%)
  between operations  1 us (1%)
    all_to_all x1, waiting for transfers between devices, per_device(): lax.all_to_all(compressed, 'wide', split_axis=0, concat_axis=2, tiled=True)  31 us
    all_to_all x1, starting transfers between devices, per_device(): lax.all_to_all(compressed, 'wide', split_axis=0, concat_axis=2, tiled=True)  20.7 us
    all_to_all x1, starting transfers between devices, per_device(): lax.all_to_all(partial, 'narrow', split_axis=0, concat_axis=0, tiled=True)  4.01 us
    dot_general x8, matrix products, per_device(): jnp.einsum('xpc,cr->xpr', extended, select, preferred_element_type=jnp.bf...  3.94 us
    all_to_all x1, waiting for transfers between devices, per_device(): lax.all_to_all(partial, 'narrow', split_axis=0, concat_axis=0, tiled=True)  3.54 us
    pallas_call x1, Pallas kernels, range_compress(): pl.pallas_call(range_kernel, in_specs=[whole] * 8, out_specs=whole, out_s...  3.41 us
    ppermute x1, waiting for transfers between devices, passed_along(): return lax.ppermute(shard, axis, pairs)  3.3 us
    ppermute x1, starting transfers between devices, passed_along(): return lax.ppermute(shard, axis, pairs)  3.29 us
  transfers between devices with their start and end apart: 3, of which 3 were waited for; matrix products, arithmetic and copies ran while one was open for 4% of the time, Pallas kernels for 0%

profile of v8, /device:TPU:1, one launch (start us, length us, event | category | flops | bytes accessed | tf_op | source)
XLA Modules:
  0.0 86.8 jit_solution(4495221501326608164)
XLA Ops:
  0.0 3.4 %shard_map.190 = bf16[2048,128]{1,0:T(8,128)(2,1)} custom-call(bf16[2,1024,128]{2,1,0:T(8,128)(2,1)} %bitcast.127, bf16[2,4096]{1,0:T(2,128)(2,1)} %replica_ref.1, bf16[256,256]{1,0:T(8,128)(2,1)} %constant.68.clone.fwd_ref.inv_t_ref, bf16[256,256]{1,0:T(8,128)(2,1)} %constant.69.clone.fwd_t_ref.inv_ref, bf16[256,256]{1,0:T(8,128)(2,1)} %constant.69.clone.fwd_t_ref.inv_ref, ...), custom_call_target="tpu_custom_call" | custom-call | flops 603979776 | bytes 1048576 | tf_op jit(solution)/shard_map/pallas_call | solution.py:142
  3.4 0.0 copy-start.10
  3.4 0.0 copy-start.5
  3.4 0.0 copy-start.8
  3.4 20.7 %all-to-all-start = ((bf16[128,2,8,128]{3,2,1,0:T(8,128)(2,1)}), bf16[128,2,8,128]{3,2,1,0:T(8,128)(2,1)S(1)}, u32[]{:S(2)}, u32[]{:S(2)}) async-start(bf16[128,2,8,128]{3,2,1,0:T(8,128)(2,1)} %bitcast.118), calls=%async_computation | async-start | bytes 1048576 | tf_op jit(solution)/shard_map/all_to_all | solution.py:199
  24.2 0.0 copy-done.10
  24.2 0.0 copy-done.5
  24.2 0.0 copy-done.8
  24.2 0.1 broadcast_divide_fusion
  24.4 1.0 %divide_cosine_fusion = (f32[1,513,128]{2,1,0:T(8,128)S(1)}, f32[1,513,128]{2,1,0:T(8,128)S(1)}) fusion(f32[128]{0:T(128)S(1)} %copy-done.8, f32[513]{0:T(1024)S(1)} %fusion.51), kind=kLoop, calls=%fused_computation.38 | loop fusion | flops 65664 | bytes 527876 | tf_op jit(solution)/shard_map/cos | solution.py:218
  25.4 0.0 copy-start.7
  25.4 1.0 %slice_cosine_fusion = (f32[511,128]{1,0:T(8,128)S(1)}, f32[511,128]{1,0:T(8,128)S(1)}) fusion(f32[513,128]{1,0:T(8,128)S(1)} %broadcast_divide_fusion), kind=kLoop, calls=%fused_computation.36 | loop fusion | bytes 784896 | tf_op jit(solution)/shard_map/cos | solution.py:218
  26.4 31.0 %all-to-all-done = bf16[128,2,8,128]{3,2,1,0:T(8,128)(2,1)S(1)} async-done(((bf16[128,2,8,128]{3,2,1,0:T(8,128)(2,1)}), bf16[128,2,8,128]{3,2,1,0:T(8,128)(2,1)S(1)}, u32[]{:S(2)}, u32[]{:S(2)}) %all-to-all-start) | async-done | bytes 524320 | tf_op jit(solution)/shard_map/all_to_all | solution.py:199
  57.4 0.0 copy-start
  57.4 0.0 copy-start.4
  57.4 0.0 copy-done.7
  57.4 0.4 convolution_bitcast_fusion.1
  57.8 0.4 copy-done
  58.2 0.0 copy-done.4
  58.3 0.0 copy-start.1
  58.3 0.3 subtract_convert_fusion.2
  58.6 0.1 maximum_bitcast_fusion
  58.7 0.5 copy-done.1
  59.2 0.3 fusion.1
  59.5 0.0 copy-start.9
  59.5 0.3 copy.86
  59.8 0.2 copy.53
  60.1 3.3 %collective-permute-start = (bf16[2,1024,31]{1,2,0:T(8,128)(2,1)S(1)}, bf16[2,1024,31]{1,2,0:T(8,128)(2,1)S(1)}, u32[]{:S(2)}, u32[]{:S(2)}) collective-permute-start(bf16[2,1024,31]{1,2,0:T(8,128)(2,1)S(1)} %slice.162), channel_id=1, source_target_pairs={{4,0},{8,4},{12,8},{16,12},{20,16},{24,20},{28,24},{32,28},{36,32}... | collective-permute-start | bytes 380936 | tf_op jit(solution)/shard_map/ppermute | solution.py:21
  63.4 0.0 copy-done.9
  63.4 0.3 rev.7
  63.8 0.3 rev.8
  64.1 0.1 convert_reduce_fusion
  64.2 3.3 %collective-permute-done = bf16[2,1024,31]{1,2,0:T(8,128)(2,1)S(1)} collective-permute-done((bf16[2,1024,31]{1,2,0:T(8,128)(2,1)S(1)}, bf16[2,1024,31]{1,2,0:T(8,128)(2,1)S(1)}, u32[]{:S(2)}, u32[]{:S(2)}) %collective-permute-start) | collective-permute-done | bytes 127008 | tf_op jit(solution)/shard_map/ppermute | solution.py:21
  67.5 0.5 fusion.15
  68.0 0.5 fusion.18
  68.5 0.5 fusion.21
  69.0 0.5 fusion.24
  69.5 0.5 fusion.27
  70.0 0.5 fusion.30
  70.5 0.5 fusion.33
  71.0 0.5 fusion.36
  71.5 2.1 %subtract_convert_fusion.1 = (bf16[1,1024,128]{2,1,0:T(8,128)(2,1)S(1)}, f32[1,1024,128]{2,1,0:T(8,128)S(1)}, f32[1,1024,128]{2,1,0:T(8,128)S(1)}) fusion(f32[1,511,128]{2,1,0:T(8,128)S(1)} %bitcast.112, f32[1,513,128]{2,1,0:T(8,128)S(1)} %get-tuple-element.23, f32[1,511,128]{2,1,0:T(8,128)S(1)} %bitcast.110, f32[1,513,128]{2,1,0:T(8,128)S(1)} %get-tuple-element.22, ...), kind=kLoop, calls=%fused_computation.27 | loop fusion | flops 6815744 | bytes 6586368 | tf_op jit(solution)/shard_map/convert_element_type | solution.py:222
  73.6 0.2 add_convert_fusion.1
  73.8 0.0 copy-start.6
  73.8 0.2 copy.55
  74.0 0.0 copy-start.3
  74.0 0.2 copy.54
  74.2 0.3 copy-done.6
  74.5 0.3 convolution_bitcast_fusion
  74.8 0.0 copy-done.3
  74.9 0.0 copy-start.2
  74.9 0.3 subtract_convert_fusion
  75.2 0.1 pad_maximum_fusion.3
  75.3 0.5 copy-done.2
  75.8 0.3 convolution_bitcast_fusion.2
  76.1 0.1 fusion.3
  76.1 0.2 copy.57
  76.3 0.1 convert_element_type.153
  76.5 0.2 fusion.11
  76.6 0.7 copy.59
  77.3 4.0 %all-to-all-start.1 = ((f32[4,64,128]{2,1,0:T(8,128)}), f32[4,64,128]{2,1,0:T(8,128)S(1)}, u32[]{:S(2)}, u32[]{:S(2)}) async-start(f32[4,64,128]{2,1,0:T(8,128)} %copy.59), calls=%async_computation.1 | async-start | bytes 262144 | tf_op jit(solution)/shard_map/all_to_all | solution.py:240
  81.3 0.6 fusion.58
  82.6 3.5 %all-to-all-done.1 = f32[4,64,128]{2,1,0:T(8,128)S(1)} async-done(((f32[4,64,128]{2,1,0:T(8,128)}), f32[4,64,128]{2,1,0:T(8,128)S(1)}, u32[]{:S(2)}, u32[]{:S(2)}) %all-to-all-start.1) | async-done | bytes 131104 | tf_op jit(solution)/shard_map/all_to_all | solution.py:240
  86.1 0.6 divide_bitcast_fusion
  (7 shorter events, 0.1 us)
Async XLA Ops:
  3.4 20.7 %copy-start.10 = (s32[128]{0:T(128)S(1)}, s32[128]{0:T(128)}, u32[]{:S(2)}) copy-start(s32[128]{0:T(128)} %param.23) | copy-start | bytes 1540
  3.4 20.8 %copy-start.5 = (f32[8,1024]{1,0:T(8,128)S(1)}, f32[8,1024]{1,0:T(8,128)}, u32[]{:S(2)}) copy-start(f32[8,1024]{1,0:T(8,128)} %param.22) | copy-start | bytes 98308
  3.4 20.8 %copy-start.8 = (f32[128]{0:T(128)S(1)}, f32[128]{0:T(128)}, u32[]{:S(2)}) copy-start(f32[128]{0:T(128)} %param.24) | copy-start | bytes 1540
  3.4 53.9 %all-to-all-start = ((bf16[128,2,8,128]{3,2,1,0:T(8,128)(2,1)}), bf16[128,2,8,128]{3,2,1,0:T(8,128)(2,1)S(1)}, u32[]{:S(2)}, u32[]{:S(2)}) async-start(bf16[128,2,8,128]{3,2,1,0:T(8,128)(2,1)} %bitcast.118), calls=%async_computation | async-start | bytes 1048576 | tf_op jit(solution)/shard_map/all_to_all | solution.py:199
  25.4 32.0 %copy-start.7 = (bf16[2,8,2,8,1]{3,1,2,4,0:T(8,128)(2,1)S(1)}, bf16[2,8,2,8,1]{3,1,2,4,0:T(8,128)(2,1)}, u32[]{:S(2)}) copy-start(bf16[2,8,2,8,1]{3,1,2,4,0:T(8,128)(2,1)} %constant.82) | copy-start | bytes 1540
  57.4 0.8 copy-start
  57.4 0.9 copy-start.4
  58.3 0.9 %copy-start.1 = (bf16[2,128,2,128,1]{3,1,2,0,4:T(8,128)(2,1)S(1)}, bf16[2,128,2,128,1]{3,1,2,0,4:T(8,128)(2,1)}, u32[]{:S(2)}) copy-start(bf16[2,128,2,128,1]{3,1,2,0,4:T(8,128)(2,1)} %constant.83) | copy-start | bytes 393220
  59.5 3.9 %copy-start.9 = (s32[4,16]{1,0:T(4,128)S(1)}, s32[4,16]{1,0:T(4,128)}, u32[]{:S(2)}) copy-start(s32[4,16]{1,0:T(4,128)} %param.25) | copy-start | bytes 772
  60.1 7.4 %collective-permute-start = (bf16[2,1024,31]{1,2,0:T(8,128)(2,1)S(1)}, bf16[2,1024,31]{1,2,0:T(8,128)(2,1)S(1)}, u32[]{:S(2)}, u32[]{:S(2)}) collective-permute-start(bf16[2,1024,31]{1,2,0:T(8,128)(2,1)S(1)} %slice.162), channel_id=1, source_target_pairs={{4,0},{8,4},{12,8},{16,12},{20,16},{24,20},{28,24},{32,28},{36,32}... | collective-permute-start | bytes 380936 | tf_op jit(solution)/shard_map/ppermute | solution.py:21
  73.8 0.7 copy-start.6
  74.0 0.9 copy-start.3
  74.9 0.9 %copy-start.2 = (bf16[2,128,2,128,1]{3,1,2,4,0:T(8,128)(2,1)S(1)}, bf16[2,128,2,128,1]{3,1,2,4,0:T(8,128)(2,1)}, u32[]{:S(2)}) copy-start(bf16[2,128,2,128,1]{3,1,2,4,0:T(8,128)(2,1)} %constant.80) | copy-start | bytes 393220
  77.3 8.8 %all-to-all-start.1 = ((f32[4,64,128]{2,1,0:T(8,128)}), f32[4,64,128]{2,1,0:T(8,128)S(1)}, u32[]{:S(2)}, u32[]{:S(2)}) async-start(f32[4,64,128]{2,1,0:T(8,128)} %copy.59), calls=%async_computation.1 | async-start | bytes 262144 | tf_op jit(solution)/shard_map/all_to_all | solution.py:240

commit v9 on v8

--- a/solution.py
+++ b/solution.py
@@ -205,12 +205,15 @@
     bins = jnp.arange(width, dtype=jnp.int32) + band_offset
     moved_real = jnp.zeros((pulses, width), jnp.float32)
     moved_imag = jnp.zeros((pulses, width), jnp.float32)
-    for tap_index in range(interp_weight.shape[0]):
-        select = (columns[:, None] == (bins + tap_index)[None, :]).astype(jnp.bfloat16)
-        picked = jnp.einsum("xpc,cr->xpr", extended, select, preferred_element_type=jnp.bfloat16)
+    taps = interp_weight.shape[0]
+    targets = (bins[None, :] + jnp.arange(taps, dtype=jnp.int32)[:, None]).reshape(taps * width)
+    select = (columns[:, None] == targets[None, :]).astype(jnp.bfloat16)
+    picked = jnp.einsum("xpc,cn->xpn", extended, select, preferred_element_type=jnp.bfloat16)
+    for tap_index in range(taps):
         weight = interp_weight[tap_index][:, None]
-        moved_real = moved_real + weight * picked[0].astype(jnp.float32)
-        moved_imag = moved_imag + weight * picked[1].astype(jnp.float32)
+        tap_values = picked[:, :, tap_index * width : (tap_index + 1) * width].astype(jnp.float32)
+        moved_real = moved_real + weight * tap_values[0]
+        moved_imag = moved_imag + weight * tap_values[1]
     half = pulses // 2
     freq = jnp.arange(half + 1, dtype=jnp.int32)
     shifted = ((freq + half) % pulses - half).astype(jnp.float32) / pulses

time: 87.3 us -> 84.1 us (0.963)
  other arithmetic: 5.7 us -> 8.84 us
  waiting for transfers between devices: 37.8 us -> 34.8 us
  matrix products: 5.47 us -> 2.84 us
    all_to_all x1, waiting for transfers between devices: 31 us -> 27.8 us  [per_device(): lax.all_to_all(compressed, 'wide', split_axis=0, concat_axis=2, tiled=True)]
    dot_general x8 -> x1, matrix products: 3.94 us -> 1.3 us  [per_device(): jnp.einsum('xpc,cn->xpn', extended, select, preferred_element_type=jnp.bf...]
    unnamed x22 -> x16, local copies, waits for them, and re-layouts: 1.75 us -> 0.04 us
    slice x1, local copies, waits for them, and re-layouts: 0.03 us -> 1.25 us  [per_device(): weight = interp_weight[tap_index][:, None]]
  transfers between devices with their start and end apart: 3 -> 3, of which waited for: 3 -> 3; matrix products, arithmetic and copies ran while one was open for 4% -> 8% of each run, Pallas kernels for 0% -> 0%
where the time goes in v9:
time: 84.1 us; the launch traced here: 83.6 us
  waiting for transfers between devices  34.8 us (41%)
  starting transfers between devices  27.8 us (33%)
  other arithmetic  8.84 us (11%)
  local copies, waits for them, and re-layouts  4.87 us (6%)
  Pallas kernels  3.45 us (4%)
  matrix products  2.84 us (3%)
  between operations  0.96 us (1%)
    all_to_all x1, waiting for transfers between devices, per_device(): lax.all_to_all(compressed, 'wide', split_axis=0, concat_axis=2, tiled=True)  27.8 us
    all_to_all x1, starting transfers between devices, per_device(): lax.all_to_all(compressed, 'wide', split_axis=0, concat_axis=2, tiled=True)  20.7 us
    all_to_all x1, starting transfers between devices, per_device(): lax.all_to_all(partial, 'narrow', split_axis=0, concat_axis=0, tiled=True)  4.02 us
    all_to_all x1, waiting for transfers between devices, per_device(): lax.all_to_all(partial, 'narrow', split_axis=0, concat_axis=0, tiled=True)  3.54 us
    ppermute x1, waiting for transfers between devices, passed_along(): return lax.ppermute(shard, axis, pairs)  3.48 us
    pallas_call x1, Pallas kernels, range_compress(): pl.pallas_call(range_kernel, in_specs=[whole] * 8, out_specs=whole, out_s...  3.45 us
    ppermute x1, starting transfers between devices, passed_along(): return lax.ppermute(shard, axis, pairs)  3.11 us
    convert_element_type x1, other arithmetic, per_device(): (moved_real * phase_cos - moved_imag * phase_sin).astype(jnp.bfloat16)  2.49 us
  transfers between devices with their start and end apart: 3, of which 3 were waited for; matrix products, arithmetic and copies ran while one was open for 8% of the time, Pallas kernels for 0%

profile of v9, /device:TPU:1, one launch (start us, length us, event | category | flops | bytes accessed | tf_op | source)
XLA Modules:
  0.0 83.6 jit_solution(13431292565797822430)
XLA Ops:
  0.0 0.0 copy-start.6
  0.0 0.0 copy-start
  0.0 0.0 copy-start.4
  0.0 3.4 %shard_map.190 = bf16[2048,128]{1,0:T(8,128)(2,1)} custom-call(bf16[2,1024,128]{2,1,0:T(8,128)(2,1)} %bitcast.108, bf16[2,4096]{1,0:T(2,128)(2,1)} %replica_ref.1, bf16[256,256]{1,0:T(8,128)(2,1)} %constant.55.clone.fwd_ref.inv_t_ref, bf16[256,256]{1,0:T(8,128)(2,1)} %constant.56.clone.fwd_t_ref.inv_ref, bf16[256,256]{1,0:T(8,128)(2,1)} %constant.56.clone.fwd_t_ref.inv_ref, ...), custom_call_target="tpu_custom_call" | custom-call | flops 603979776 | bytes 1048576 | tf_op jit(solution)/shard_map/pallas_call | solution.py:142
  3.5 0.0 copy-start.1
  3.5 20.7 %all-to-all-start = ((bf16[128,2,8,128]{3,2,1,0:T(8,128)(2,1)}), bf16[128,2,8,128]{3,2,1,0:T(8,128)(2,1)S(1)}, u32[]{:S(2)}, u32[]{:S(2)}) async-start(bf16[128,2,8,128]{3,2,1,0:T(8,128)(2,1)} %bitcast.99), calls=%async_computation | async-start | bytes 1048576 | tf_op jit(solution)/shard_map/all_to_all | solution.py:199
  24.2 0.7 iota_add_fusion
  24.9 1.2 %fusion.52 = (f32[1,1024]{1,0:T(1,128)S(1)}, f32[1,1024]{1,0:T(1,128)S(1)}, f32[1,1024]{1,0:T(1,128)S(1)}, f32[1,1024]{1,0:T(1,128)S(1)}, f32[1,1024]{1,0:T(1,12...) fusion(f32[8,1024]{1,0:T(8,128)} %param.22), kind=kLoop, calls=%fused_computation.107 | loop fusion | bytes 65536 | tf_op jit(solution)/shard_map/slice | solution.py:213
  26.1 0.8 broadcast_divide_fusion
  26.9 1.7 %divide_cosine_fusion = (f32[1,513,128]{2,1,0:T(8,128)S(1)}, f32[1,513,128]{2,1,0:T(8,128)S(1)}) fusion(f32[128]{0:T(128)} %param.24, f32[513]{0:T(1024)S(1)} %fusion.40), kind=kLoop, calls=%fused_computation.80 | loop fusion | flops 65664 | bytes 527876 | tf_op jit(solution)/shard_map/cos | solution.py:221
  28.6 1.0 %slice_cosine_fusion = (f32[511,128]{1,0:T(8,128)S(1)}, f32[511,128]{1,0:T(8,128)S(1)}) fusion(f32[513,128]{1,0:T(8,128)S(1)} %broadcast_divide_fusion), kind=kLoop, calls=%fused_computation.78 | loop fusion | bytes 784896 | tf_op jit(solution)/shard_map/cos | solution.py:221
  29.6 27.8 %all-to-all-done = bf16[128,2,8,128]{3,2,1,0:T(8,128)(2,1)S(1)} async-done(((bf16[128,2,8,128]{3,2,1,0:T(8,128)(2,1)}), bf16[128,2,8,128]{3,2,1,0:T(8,128)(2,1)S(1)}, u32[]{:S(2)}, u32[]{:S(2)}) %all-to-all-start) | async-done | bytes 524320 | tf_op jit(solution)/shard_map/all_to_all | solution.py:199
  57.4 0.0 copy-start.7
  57.4 0.0 copy-done.6
  57.4 0.4 convolution_bitcast_fusion.1
  57.9 0.0 copy-done
  57.9 0.0 copy-done.4
  57.9 0.4 subtract_convert_fusion.2
  58.2 0.1 maximum_bitcast_fusion
  58.3 0.0 copy-done.1
  58.3 0.3 fusion.1
  58.6 0.3 copy.86
  59.0 0.2 copy.53
  59.2 3.1 %collective-permute-start = (bf16[2,1024,31]{1,2,0:T(8,128)(2,1)S(1)}, bf16[2,1024,31]{1,2,0:T(8,128)(2,1)S(1)}, u32[]{:S(2)}, u32[]{:S(2)}) collective-permute-start(bf16[2,1024,31]{1,2,0:T(8,128)(2,1)S(1)} %slice.194), channel_id=1, source_target_pairs={{4,0},{8,4},{12,8},{16,12},{20,16},{24,20},{28,24},{32,28},{36,32}... | collective-permute-start | bytes 380936 | tf_op jit(solution)/shard_map/ppermute | solution.py:21
  62.3 0.0 copy-done.7
  62.4 0.3 rev.7
  62.7 0.3 rev.8
  63.1 0.1 convert_reduce_fusion
  63.2 3.5 %collective-permute-done = bf16[2,1024,31]{1,2,0:T(8,128)(2,1)S(1)} collective-permute-done((bf16[2,1024,31]{1,2,0:T(8,128)(2,1)S(1)}, bf16[2,1024,31]{1,2,0:T(8,128)(2,1)S(1)}, u32[]{:S(2)}, u32[]{:S(2)}) %collective-permute-start) | collective-permute-done | bytes 127008 | tf_op jit(solution)/shard_map/ppermute | solution.py:21
  66.7 1.3 %fusion.2 = bf16[2,1024,1024]{2,1,0:T(8,128)(2,1)S(1)} fusion(bf16[2,1024,31]{1,2,0:T(8,128)(2,1)S(1)} %collective-permute-done, bf16[2,1024,128]{1,2,0:T(8,128)(2,1)S(1)} %copy.53, s32[1024]{0:T(1024)S(1)} %add_bitcast_fusion), kind=kOutput, calls=%fused_computation.6 | convolution fusion | flops 668359680 | bytes 4849664 | tf_op jit(solution)/shard_map/xpc,cn->xpn/dot_general | solution.py:211
  68.0 0.8 slice_convert_fusion.7
  68.8 0.0 copy-start.5
  68.8 2.5 %subtract_convert_fusion.1 = (bf16[1,1024,128]{2,1,0:T(8,128)(2,1)S(1)}, f32[1,1024,128]{2,1,0:T(8,128)S(1)}, f32[1,1024,128]{2,1,0:T(8,128)S(1)}) fusion(f32[1,511,128]{2,1,0:T(8,128)S(1)} %bitcast.93, f32[1,513,128]{2,1,0:T(8,128)S(1)} %get-tuple-element.31, f32[1,511,128]{2,1,0:T(8,128)S(1)} %bitcast.91, f32[1,513,128]{2,1,0:T(8,128)S(1)} %get-tuple-element.30, ...), kind=kLoop, calls=%fused_computation.70 | loop fusion | flops 4718592 | bytes 10780672 | tf_op jit(solution)/shard_map/convert_element_type | solution.py:225
  71.3 0.0 copy-start.3
  71.3 0.0 copy-start.2
  71.3 0.1 add_convert_fusion.1
  71.5 0.2 copy.55
  71.7 0.2 copy.54
  71.8 0.0 copy-done.5
  71.8 0.3 convolution_bitcast_fusion
  72.2 0.0 copy-done.3
  72.2 0.4 subtract_convert_fusion
  72.6 0.1 pad_maximum_fusion.2
  72.6 0.0 copy-done.2
  72.6 0.3 convolution_bitcast_fusion.2
  72.9 0.1 fusion.9
  73.0 0.2 copy.57
  73.2 0.1 convert_element_type.82
  73.3 0.2 fusion.32
  73.5 0.6 copy.59
  74.1 4.0 %all-to-all-start.1 = ((f32[4,64,128]{2,1,0:T(8,128)}), f32[4,64,128]{2,1,0:T(8,128)S(1)}, u32[]{:S(2)}, u32[]{:S(2)}) async-start(f32[4,64,128]{2,1,0:T(8,128)} %copy.59), calls=%async_computation.1 | async-start | bytes 262144 | tf_op jit(solution)/shard_map/all_to_all | solution.py:243
  78.1 0.6 fusion.47
  79.4 3.5 %all-to-all-done.1 = f32[4,64,128]{2,1,0:T(8,128)S(1)} async-done(((f32[4,64,128]{2,1,0:T(8,128)}), f32[4,64,128]{2,1,0:T(8,128)S(1)}, u32[]{:S(2)}, u32[]{:S(2)}) %all-to-all-start.1) | async-done | bytes 131104 | tf_op jit(solution)/shard_map/all_to_all | solution.py:243
  83.0 0.6 divide_bitcast_fusion
  (6 shorter events, 0.1 us)
Async XLA Ops:
  0.0 57.4 %copy-start.6 = (bf16[2,8,2,8,1]{3,1,2,4,0:T(8,128)(2,1)S(1)}, bf16[2,8,2,8,1]{3,1,2,4,0:T(8,128)(2,1)}, u32[]{:S(2)}) copy-start(bf16[2,8,2,8,1]{3,1,2,4,0:T(8,128)(2,1)} %constant.69) | copy-start | bytes 1540
  0.0 57.9 %copy-start = (f32[8,128]{0,1:T(8,128)S(1)}, f32[8,128]{0,1:T(8,128)}, u32[]{:S(2)}) copy-start(f32[8,128]{0,1:T(8,128)} %constant.61.clone) | copy-start | bytes 12292
  0.0 57.9 %copy-start.4 = (f32[8,128]{0,1:T(8,128)S(1)}, f32[8,128]{0,1:T(8,128)}, u32[]{:S(2)}) copy-start(f32[8,128]{0,1:T(8,128)} %constant.62.clone) | copy-start | bytes 12292
  3.5 54.8 %copy-start.1 = (bf16[2,128,2,128,1]{3,1,2,0,4:T(8,128)(2,1)S(1)}, bf16[2,128,2,128,1]{3,1,2,0,4:T(8,128)(2,1)}, u32[]{:S(2)}) copy-start(bf16[2,128,2,128,1]{3,1,2,0,4:T(8,128)(2,1)} %constant.70) | copy-start | bytes 393220
  3.5 53.9 %all-to-all-start = ((bf16[128,2,8,128]{3,2,1,0:T(8,128)(2,1)}), bf16[128,2,8,128]{3,2,1,0:T(8,128)(2,1)S(1)}, u32[]{:S(2)}, u32[]{:S(2)}) async-start(bf16[128,2,8,128]{3,2,1,0:T(8,128)(2,1)} %bitcast.99), calls=%async_computation | async-start | bytes 1048576 | tf_op jit(solution)/shard_map/all_to_all | solution.py:199
  57.4 4.9 %copy-start.7 = (s32[4,16]{1,0:T(4,128)S(1)}, s32[4,16]{1,0:T(4,128)}, u32[]{:S(2)}) copy-start(s32[4,16]{1,0:T(4,128)} %param.25) | copy-start | bytes 772
  59.2 7.4 %collective-permute-start = (bf16[2,1024,31]{1,2,0:T(8,128)(2,1)S(1)}, bf16[2,1024,31]{1,2,0:T(8,128)(2,1)S(1)}, u32[]{:S(2)}, u32[]{:S(2)}) collective-permute-start(bf16[2,1024,31]{1,2,0:T(8,128)(2,1)S(1)} %slice.194), channel_id=1, source_target_pairs={{4,0},{8,4},{12,8},{16,12},{20,16},{24,20},{28,24},{32,28},{36,32}... | collective-permute-start | bytes 380936 | tf_op jit(solution)/shard_map/ppermute | solution.py:21
  68.8 3.0 %copy-start.5 = (bf16[2,8,2,8,1]{3,1,2,4,0:T(8,128)(2,1)S(1)}, bf16[2,8,2,8,1]{3,1,2,4,0:T(8,128)(2,1)}, u32[]{:S(2)}) copy-start(bf16[2,8,2,8,1]{3,1,2,4,0:T(8,128)(2,1)} %constant.68) | copy-start | bytes 1540
  71.3 0.9 %copy-start.3 = (f32[8,128]{0,1:T(8,128)S(1)}, f32[8,128]{0,1:T(8,128)}, u32[]{:S(2)}) copy-start(f32[8,128]{0,1:T(8,128)} %constant.65.clone) | copy-start | bytes 12292
  71.3 1.3 %copy-start.2 = (bf16[2,128,2,128,1]{3,1,2,4,0:T(8,128)(2,1)S(1)}, bf16[2,128,2,128,1]{3,1,2,4,0:T(8,128)(2,1)}, u32[]{:S(2)}) copy-start(bf16[2,128,2,128,1]{3,1,2,4,0:T(8,128)(2,1)} %constant.67) | copy-start | bytes 393220
  74.1 8.8 %all-to-all-start.1 = ((f32[4,64,128]{2,1,0:T(8,128)}), f32[4,64,128]{2,1,0:T(8,128)S(1)}, u32[]{:S(2)}, u32[]{:S(2)}) async-start(f32[4,64,128]{2,1,0:T(8,128)} %copy.59), calls=%async_computation.1 | async-start | bytes 262144 | tf_op jit(solution)/shard_map/all_to_all | solution.py:243

commit v10 on v9

--- a/solution.py
+++ b/solution.py
@@ -228,7 +228,10 @@
     intensity = (image[0] * image[0] + image[1] * image[1]).astype(jnp.bfloat16)
     block_count = tile_owner.shape[1]
     block_rows = pulses // block_count
-    blocks = intensity.reshape(block_count, block_rows * width)
+    second = pulses // PUL_DEV
+    per_block = block_rows // PUL_DEV
+    blocks = intensity.reshape(second, PUL_DEV, width).transpose(1, 0, 2)
+    blocks = blocks.reshape(PUL_DEV, block_count, per_block, width)
     tiles = lax.axis_size("narrow")
     group = lax.axis_index("narrow")
     tile_ids = jnp.arange(tiles, dtype=jnp.int32)
@@ -238,10 +241,9 @@
         (tile_owner[:, :, None] == tile_ids[None, None, :]).astype(jnp.int32), axis=(0, 1)
     )
     own_count = jnp.sum(jnp.where(tile_ids == group, counts, 0)).astype(jnp.float32)
-    partial = jnp.dot(member, blocks, preferred_element_type=jnp.float32)
-    partial = partial.reshape(tiles, block_rows, width)
+    partial = jnp.einsum("tb,kbjc->tkjc", member, blocks, preferred_element_type=jnp.float32)
     incoming = lax.all_to_all(partial, "narrow", split_axis=0, concat_axis=0, tiled=True)
-    summed = jnp.sum(incoming, axis=0)[None]
+    summed = jnp.sum(incoming, axis=0).transpose(1, 0, 2).reshape(1, block_rows, width)
     return summed / own_count
 
 

time: 84.1 us -> 83.8 us (level)
  no operation moved by 1% of the time
where the time goes in v10:
time: 83.8 us; the launch traced here: 83.3 us
  waiting for transfers between devices  34.8 us (42%)
  starting transfers between devices  27.8 us (33%)
  other arithmetic  8.22 us (10%)
  local copies, waits for them, and re-layouts  5.2 us (6%)
  Pallas kernels  3.45 us (4%)
  matrix products  2.84 us (3%)
  between operations  0.96 us (1%)
    all_to_all x1, waiting for transfers between devices, per_device(): lax.all_to_all(compressed, 'wide', split_axis=0, concat_axis=2, tiled=True)  27.8 us
    all_to_all x1, starting transfers between devices, per_device(): lax.all_to_all(compressed, 'wide', split_axis=0, concat_axis=2, tiled=True)  20.7 us
    all_to_all x1, starting transfers between devices, per_device(): lax.all_to_all(partial, 'narrow', split_axis=0, concat_axis=0, tiled=True)  4.02 us
    all_to_all x1, waiting for transfers between devices, per_device(): lax.all_to_all(partial, 'narrow', split_axis=0, concat_axis=0, tiled=True)  3.54 us
    ppermute x1, waiting for transfers between devices, passed_along(): return lax.ppermute(shard, axis, pairs)  3.48 us
    pallas_call x1, Pallas kernels, range_compress(): pl.pallas_call(range_kernel, in_specs=[whole] * 8, out_specs=whole, out_s...  3.45 us
    ppermute x1, starting transfers between devices, passed_along(): return lax.ppermute(shard, axis, pairs)  3.11 us
    convert_element_type x1, other arithmetic, per_device(): (moved_real * phase_cos - moved_imag * phase_sin).astype(jnp.bfloat16)  2.49 us
  transfers between devices with their start and end apart: 3, of which 3 were waited for; matrix products, arithmetic and copies ran while one was open for 8% of the time, Pallas kernels for 0%

profile of v10, /device:TPU:1, one launch (start us, length us, event | category | flops | bytes accessed | tf_op | source)
XLA Modules:
  0.0 83.3 jit_solution(14772016622420970659)
XLA Ops:
  0.0 0.0 copy-start.6
  0.0 0.0 copy-start
  0.0 0.0 copy-start.4
  0.0 3.4 %shard_map.190 = bf16[2048,128]{1,0:T(8,128)(2,1)} custom-call(bf16[2,1024,128]{2,1,0:T(8,128)(2,1)} %bitcast.109, bf16[2,4096]{1,0:T(2,128)(2,1)} %replica_ref.1, bf16[256,256]{1,0:T(8,128)(2,1)} %constant.55.clone.fwd_ref.inv_t_ref, bf16[256,256]{1,0:T(8,128)(2,1)} %constant.56.clone.fwd_t_ref.inv_ref, bf16[256,256]{1,0:T(8,128)(2,1)} %constant.56.clone.fwd_t_ref.inv_ref, ...), custom_call_target="tpu_custom_call" | custom-call | flops 603979776 | bytes 1048576 | tf_op jit(solution)/shard_map/pallas_call | solution.py:142
  3.5 0.0 copy-start.1
  3.5 20.7 %all-to-all-start = ((bf16[128,2,8,128]{3,2,1,0:T(8,128)(2,1)}), bf16[128,2,8,128]{3,2,1,0:T(8,128)(2,1)S(1)}, u32[]{:S(2)}, u32[]{:S(2)}) async-start(bf16[128,2,8,128]{3,2,1,0:T(8,128)(2,1)} %bitcast.100), calls=%async_computation | async-start | bytes 1048576 | tf_op jit(solution)/shard_map/all_to_all | solution.py:199
  24.2 0.7 iota_add_fusion
  24.9 1.2 %fusion.52 = (f32[1,1024]{1,0:T(1,128)S(1)}, f32[1,1024]{1,0:T(1,128)S(1)}, f32[1,1024]{1,0:T(1,128)S(1)}, f32[1,1024]{1,0:T(1,128)S(1)}, f32[1,1024]{1,0:T(1,12...) fusion(f32[8,1024]{1,0:T(8,128)} %param.22), kind=kLoop, calls=%fused_computation.108 | loop fusion | bytes 65536 | tf_op jit(solution)/shard_map/slice | solution.py:213
  26.1 0.8 broadcast_divide_fusion
  26.9 1.7 %divide_cosine_fusion = (f32[1,513,128]{2,1,0:T(8,128)S(1)}, f32[1,513,128]{2,1,0:T(8,128)S(1)}) fusion(f32[128]{0:T(128)} %param.24, f32[513]{0:T(1024)S(1)} %fusion.40), kind=kLoop, calls=%fused_computation.80 | loop fusion | flops 65664 | bytes 527876 | tf_op jit(solution)/shard_map/cos | solution.py:221
  28.6 1.0 %slice_cosine_fusion = (f32[511,128]{1,0:T(8,128)S(1)}, f32[511,128]{1,0:T(8,128)S(1)}) fusion(f32[513,128]{1,0:T(8,128)S(1)} %broadcast_divide_fusion), kind=kLoop, calls=%fused_computation.78 | loop fusion | bytes 784896 | tf_op jit(solution)/shard_map/cos | solution.py:221
  29.6 27.8 %all-to-all-done = bf16[128,2,8,128]{3,2,1,0:T(8,128)(2,1)S(1)} async-done(((bf16[128,2,8,128]{3,2,1,0:T(8,128)(2,1)}), bf16[128,2,8,128]{3,2,1,0:T(8,128)(2,1)S(1)}, u32[]{:S(2)}, u32[]{:S(2)}) %all-to-all-start) | async-done | bytes 524320 | tf_op jit(solution)/shard_map/all_to_all | solution.py:199
  57.4 0.0 copy-start.7
  57.4 0.0 copy-done.6
  57.4 0.4 convolution_bitcast_fusion.1
  57.9 0.0 copy-done
  57.9 0.0 copy-done.4
  57.9 0.4 subtract_convert_fusion.2
  58.2 0.1 maximum_bitcast_fusion
  58.3 0.0 copy-done.1
  58.3 0.3 fusion.1
  58.6 0.3 copy.100
  59.0 0.2 copy.66
  59.2 3.1 %collective-permute-start = (bf16[2,1024,31]{1,2,0:T(8,128)(2,1)S(1)}, bf16[2,1024,31]{1,2,0:T(8,128)(2,1)S(1)}, u32[]{:S(2)}, u32[]{:S(2)}) collective-permute-start(bf16[2,1024,31]{1,2,0:T(8,128)(2,1)S(1)} %slice.194), channel_id=1, source_target_pairs={{4,0},{8,4},{12,8},{16,12},{20,16},{24,20},{28,24},{32,28},{36,32}... | collective-permute-start | bytes 380936 | tf_op jit(solution)/shard_map/ppermute | solution.py:21
  62.3 0.0 copy-done.7
  62.4 0.3 rev.7
  62.7 0.3 rev.8
  63.1 0.1 convert_reduce_fusion
  63.2 3.5 %collective-permute-done = bf16[2,1024,31]{1,2,0:T(8,128)(2,1)S(1)} collective-permute-done((bf16[2,1024,31]{1,2,0:T(8,128)(2,1)S(1)}, bf16[2,1024,31]{1,2,0:T(8,128)(2,1)S(1)}, u32[]{:S(2)}, u32[]{:S(2)}) %collective-permute-start) | collective-permute-done | bytes 127008 | tf_op jit(solution)/shard_map/ppermute | solution.py:21
  66.7 1.3 %fusion.2 = bf16[2,1024,1024]{2,1,0:T(8,128)(2,1)S(1)} fusion(bf16[2,1024,31]{1,2,0:T(8,128)(2,1)S(1)} %collective-permute-done, bf16[2,1024,128]{1,2,0:T(8,128)(2,1)S(1)} %copy.66, s32[1024]{0:T(1024)S(1)} %add_bitcast_fusion), kind=kOutput, calls=%fused_computation.6 | convolution fusion | flops 668359680 | bytes 4849664 | tf_op jit(solution)/shard_map/xpc,cn->xpn/dot_general | solution.py:211
  68.0 0.8 slice_convert_fusion.7
  68.8 0.0 copy-start.5
  68.8 2.5 %subtract_convert_fusion.1 = (bf16[1,1024,128]{2,1,0:T(8,128)(2,1)S(1)}, f32[1,1024,128]{2,1,0:T(8,128)S(1)}, f32[1,1024,128]{2,1,0:T(8,128)S(1)}) fusion(f32[1,511,128]{2,1,0:T(8,128)S(1)} %bitcast.94, f32[1,513,128]{2,1,0:T(8,128)S(1)} %get-tuple-element.31, f32[1,511,128]{2,1,0:T(8,128)S(1)} %bitcast.92, f32[1,513,128]{2,1,0:T(8,128)S(1)} %get-tuple-element.30, ...), kind=kLoop, calls=%fused_computation.70 | loop fusion | flops 4718592 | bytes 10780672 | tf_op jit(solution)/shard_map/convert_element_type | solution.py:225
  71.3 0.0 copy-start.3
  71.3 0.0 copy-start.2
  71.3 0.1 add_convert_fusion.1
  71.5 0.2 copy.68
  71.7 0.2 copy.67
  71.8 0.0 copy-done.5
  71.8 0.3 convolution_bitcast_fusion
  72.2 0.0 copy-done.3
  72.2 0.4 subtract_convert_fusion
  72.6 0.1 pad_maximum_fusion.2
  72.6 0.0 copy-done.2
  72.6 0.3 convolution_bitcast_fusion.2
  72.9 0.1 fusion.32
  73.0 0.2 fusion.33
  73.2 0.6 copy.71
  73.8 4.0 %all-to-all-start.1 = ((f32[4,8,8,128]{3,2,1,0:T(8,128)}), f32[4,8,8,128]{3,2,1,0:T(8,128)S(1)}, u32[]{:S(2)}, u32[]{:S(2)}) async-start(f32[4,8,8,128]{3,2,1,0:T(8,128)} %copy.71), calls=%async_computation.1 | async-start | bytes 262144 | tf_op jit(solution)/shard_map/all_to_all | solution.py:245
  77.8 0.6 fusion.47
  79.1 3.5 %all-to-all-done.1 = f32[4,8,8,128]{3,2,1,0:T(8,128)S(1)} async-done(((f32[4,8,8,128]{3,2,1,0:T(8,128)}), f32[4,8,8,128]{3,2,1,0:T(8,128)S(1)}, u32[]{:S(2)}, u32[]{:S(2)}) %all-to-all-start.1) | async-done | bytes 131104 | tf_op jit(solution)/shard_map/all_to_all | solution.py:245
  82.7 0.6 copy.101
  (7 shorter events, 0.1 us)
Async XLA Ops:
  0.0 57.4 %copy-start.6 = (bf16[2,8,2,8,1]{3,1,2,4,0:T(8,128)(2,1)S(1)}, bf16[2,8,2,8,1]{3,1,2,4,0:T(8,128)(2,1)}, u32[]{:S(2)}) copy-start(bf16[2,8,2,8,1]{3,1,2,4,0:T(8,128)(2,1)} %constant.69) | copy-start | bytes 1540
  0.0 57.9 %copy-start = (f32[8,128]{0,1:T(8,128)S(1)}, f32[8,128]{0,1:T(8,128)}, u32[]{:S(2)}) copy-start(f32[8,128]{0,1:T(8,128)} %constant.61.clone) | copy-start | bytes 12292
  0.0 57.9 %copy-start.4 = (f32[8,128]{0,1:T(8,128)S(1)}, f32[8,128]{0,1:T(8,128)}, u32[]{:S(2)}) copy-start(f32[8,128]{0,1:T(8,128)} %constant.62.clone) | copy-start | bytes 12292
  3.5 54.8 %copy-start.1 = (bf16[2,128,2,128,1]{3,1,2,0,4:T(8,128)(2,1)S(1)}, bf16[2,128,2,128,1]{3,1,2,0,4:T(8,128)(2,1)}, u32[]{:S(2)}) copy-start(bf16[2,128,2,128,1]{3,1,2,0,4:T(8,128)(2,1)} %constant.70) | copy-start | bytes 393220
  3.5 53.9 %all-to-all-start = ((bf16[128,2,8,128]{3,2,1,0:T(8,128)(2,1)}), bf16[128,2,8,128]{3,2,1,0:T(8,128)(2,1)S(1)}, u32[]{:S(2)}, u32[]{:S(2)}) async-start(bf16[128,2,8,128]{3,2,1,0:T(8,128)(2,1)} %bitcast.100), calls=%async_computation | async-start | bytes 1048576 | tf_op jit(solution)/shard_map/all_to_all | solution.py:199
  57.4 4.9 %copy-start.7 = (s32[4,16]{1,0:T(4,128)S(1)}, s32[4,16]{1,0:T(4,128)}, u32[]{:S(2)}) copy-start(s32[4,16]{1,0:T(4,128)} %param.25) | copy-start | bytes 772
  59.2 7.4 %collective-permute-start = (bf16[2,1024,31]{1,2,0:T(8,128)(2,1)S(1)}, bf16[2,1024,31]{1,2,0:T(8,128)(2,1)S(1)}, u32[]{:S(2)}, u32[]{:S(2)}) collective-permute-start(bf16[2,1024,31]{1,2,0:T(8,128)(2,1)S(1)} %slice.194), channel_id=1, source_target_pairs={{4,0},{8,4},{12,8},{16,12},{20,16},{24,20},{28,24},{32,28},{36,32}... | collective-permute-start | bytes 380936 | tf_op jit(solution)/shard_map/ppermute | solution.py:21
  68.8 3.0 %copy-start.5 = (bf16[2,8,2,8,1]{3,1,2,4,0:T(8,128)(2,1)S(1)}, bf16[2,8,2,8,1]{3,1,2,4,0:T(8,128)(2,1)}, u32[]{:S(2)}) copy-start(bf16[2,8,2,8,1]{3,1,2,4,0:T(8,128)(2,1)} %constant.68) | copy-start | bytes 1540
  71.3 0.9 %copy-start.3 = (f32[8,128]{0,1:T(8,128)S(1)}, f32[8,128]{0,1:T(8,128)}, u32[]{:S(2)}) copy-start(f32[8,128]{0,1:T(8,128)} %constant.65.clone) | copy-start | bytes 12292
  71.3 1.3 %copy-start.2 = (bf16[2,128,2,128,1]{3,1,2,4,0:T(8,128)(2,1)S(1)}, bf16[2,128,2,128,1]{3,1,2,4,0:T(8,128)(2,1)}, u32[]{:S(2)}) copy-start(bf16[2,128,2,128,1]{3,1,2,4,0:T(8,128)(2,1)} %constant.67) | copy-start | bytes 393220
  73.8 8.8 %all-to-all-start.1 = ((f32[4,8,8,128]{3,2,1,0:T(8,128)}), f32[4,8,8,128]{3,2,1,0:T(8,128)S(1)}, u32[]{:S(2)}, u32[]{:S(2)}) async-start(f32[4,8,8,128]{3,2,1,0:T(8,128)} %copy.71), calls=%async_computation.1 | async-start | bytes 262144 | tf_op jit(solution)/shard_map/all_to_all | solution.py:245

commit v11 on v10

--- a/solution.py
+++ b/solution.py
@@ -199,8 +199,7 @@
     turned = lax.all_to_all(compressed, "wide", split_axis=0, concat_axis=2, tiled=True)[0]
     doppler = pulse_transform(turned, PUL_DEV, -1).astype(jnp.bfloat16)
     rim = passed_along(doppler[:, :, :HALO], "wide", -1)
-    extended = jnp.concatenate([doppler, rim], axis=2)
-    pulses = extended.shape[1]
+    pulses = doppler.shape[1]
     columns = jnp.arange(width + HALO, dtype=jnp.int32)
     bins = jnp.arange(width, dtype=jnp.int32) + band_offset
     moved_real = jnp.zeros((pulses, width), jnp.float32)
@@ -208,10 +207,18 @@
     taps = interp_weight.shape[0]
     targets = (bins[None, :] + jnp.arange(taps, dtype=jnp.int32)[:, None]).reshape(taps * width)
     select = (columns[:, None] == targets[None, :]).astype(jnp.bfloat16)
-    picked = jnp.einsum("xpc,cn->xpn", extended, select, preferred_element_type=jnp.bfloat16)
+    picked = jnp.einsum("xpc,cn->xpn", doppler, select[:width], preferred_element_type=jnp.bfloat16)
+    reach = 32
+    assert reach > HALO and reach <= width
+    rim_select = select[width:].reshape(HALO, taps, width)[:, :, width - reach :]
+    rim_picked = jnp.einsum(
+        "xpc,ckn->xpkn", rim, rim_select, preferred_element_type=jnp.bfloat16
+    )
     for tap_index in range(taps):
         weight = interp_weight[tap_index][:, None]
-        tap_values = picked[:, :, tap_index * width : (tap_index + 1) * width].astype(jnp.float32)
+        own = picked[:, :, tap_index * width : (tap_index + 1) * width]
+        beyond = jnp.pad(rim_picked[:, :, tap_index], ((0, 0), (0, 0), (width - reach, 0)))
+        tap_values = (own + beyond).astype(jnp.float32)
         moved_real = moved_real + weight * tap_values[0]
         moved_imag = moved_imag + weight * tap_values[1]
     half = pulses // 2

time: 83.8 us -> 84.6 us (level)
  matrix products: 2.84 us -> 4.1 us
    dot_general x1 -> x2, matrix products: 1.3 us -> 2.57 us  [the longest x1 1.31 us: per_device(): jnp.einsum('xpc,ckn->xpkn', rim, rim_select, preferred_element_type=jnp.b...]
    slice x1, local copies, waits for them, and re-layouts: 1.25 us -> 0.03 us  [per_device(): weight = interp_weight[tap_index][:, None]]
where the time goes in v11:
time: 84.6 us; the launch traced here: 84.3 us
  waiting for transfers between devices  34.9 us (41%)
  starting transfers between devices  27.9 us (33%)
  other arithmetic  8.39 us (10%)
  local copies, waits for them, and re-layouts  4.51 us (5%)
  matrix products  4.1 us (5%)
  Pallas kernels  3.48 us (4%)
  between operations  1.01 us (1%)
    all_to_all x1, waiting for transfers between devices, per_device(): lax.all_to_all(compressed, 'wide', split_axis=0, concat_axis=2, tiled=True)  28.5 us
    all_to_all x1, starting transfers between devices, per_device(): lax.all_to_all(compressed, 'wide', split_axis=0, concat_axis=2, tiled=True)  20.6 us
    all_to_all x1, starting transfers between devices, per_device(): lax.all_to_all(partial, 'narrow', split_axis=0, concat_axis=0, tiled=True)  4.01 us
    all_to_all x1, waiting for transfers between devices, per_device(): lax.all_to_all(partial, 'narrow', split_axis=0, concat_axis=0, tiled=True)  3.54 us
    pallas_call x1, Pallas kernels, range_compress(): pl.pallas_call(range_kernel, in_specs=[whole] * 8, out_specs=whole, out_s...  3.48 us
    ppermute x1, starting transfers between devices, passed_along(): return lax.ppermute(shard, axis, pairs)  3.29 us
    ppermute x1, waiting for transfers between devices, passed_along(): return lax.ppermute(shard, axis, pairs)  2.87 us
    convert_element_type x1, other arithmetic, per_device(): (moved_real * phase_cos - moved_imag * phase_sin).astype(jnp.bfloat16)  2.49 us
  transfers between devices with their start and end apart: 3, of which 3 were waited for; matrix products, arithmetic and copies ran while one was open for 8% of the time, Pallas kernels for 0%

profile of v11, /device:TPU:1, one launch (start us, length us, event | category | flops | bytes accessed | tf_op | source)
XLA Modules:
  0.0 84.3 jit_solution(13731915858666744398)
XLA Ops:
  0.0 0.0 copy-start.7
  0.0 0.0 copy-start.8
  0.0 0.0 copy-start.9
  0.0 0.0 copy-start.5
  0.0 0.0 copy-start
  0.0 0.0 copy-start.4
  0.0 3.5 %shard_map.190 = bf16[2048,128]{1,0:T(8,128)(2,1)} custom-call(bf16[2,1024,128]{2,1,0:T(8,128)(2,1)} %bitcast.137, bf16[2,4096]{1,0:T(2,128)(2,1)} %replica_ref.1, bf16[256,256]{1,0:T(8,128)(2,1)} %constant.57.clone.fwd_ref.inv_t_ref, bf16[256,256]{1,0:T(8,128)(2,1)} %constant.58.clone.fwd_t_ref.inv_ref, bf16[256,256]{1,0:T(8,128)(2,1)} %constant.58.clone.fwd_t_ref.inv_ref, ...), custom_call_target="tpu_custom_call" | custom-call | flops 603979776 | bytes 1048576 | tf_op jit(solution)/shard_map/pallas_call | solution.py:142
  3.5 20.6 %all-to-all-start = ((bf16[128,2,8,128]{3,2,1,0:T(8,128)(2,1)}), bf16[128,2,8,128]{3,2,1,0:T(8,128)(2,1)S(1)}, u32[]{:S(2)}, u32[]{:S(2)}) async-start(bf16[128,2,8,128]{3,2,1,0:T(8,128)(2,1)} %bitcast.127), calls=%async_computation | async-start | bytes 1048576 | tf_op jit(solution)/shard_map/all_to_all | solution.py:199
  24.1 0.7 iota_add_fusion
  24.8 0.1 iota_compare_fusion
  24.9 0.0 copy-start.1
  24.9 0.2 copy.129
  25.1 0.8 broadcast_divide_fusion
  25.9 1.0 %slice_cosine_fusion = (f32[511,128]{1,0:T(8,128)S(1)}, f32[511,128]{1,0:T(8,128)S(1)}) fusion(f32[513,128]{1,0:T(8,128)S(1)} %broadcast_divide_fusion), kind=kLoop, calls=%fused_computation.90 | loop fusion | bytes 784896 | tf_op jit(solution)/shard_map/cos | solution.py:228
  26.9 0.3 rev.7
  27.3 0.3 rev.8
  27.6 0.0 copy-done.9
  27.6 0.1 convert_reduce_fusion
  27.8 0.0 copy-done.5
  27.8 0.0 copy-done.8
  27.8 1.0 %divide_cosine_fusion = (f32[1,513,128]{2,1,0:T(8,128)S(1)}, f32[1,513,128]{2,1,0:T(8,128)S(1)}) fusion(f32[128]{0:T(128)S(1)} %copy-done.8, f32[513]{0:T(1024)S(1)} %fusion.44), kind=kLoop, calls=%fused_computation.92 | loop fusion | flops 65664 | bytes 527876 | tf_op jit(solution)/shard_map/cos | solution.py:228
  28.8 28.5 %all-to-all-done = bf16[128,2,8,128]{3,2,1,0:T(8,128)(2,1)S(1)} async-done(((bf16[128,2,8,128]{3,2,1,0:T(8,128)(2,1)}), bf16[128,2,8,128]{3,2,1,0:T(8,128)(2,1)S(1)}, u32[]{:S(2)}, u32[]{:S(2)}) %all-to-all-start) | async-done | bytes 524320 | tf_op jit(solution)/shard_map/all_to_all | solution.py:199
  57.4 0.0 copy-done.7
  57.4 0.4 convolution_bitcast_fusion.1
  57.8 0.0 copy-done
  57.8 0.0 copy-done.4
  57.8 0.4 subtract_convert_fusion.2
  58.2 0.1 maximum_bitcast_fusion
  58.2 0.0 copy-done.1
  58.2 0.3 fusion.1
  58.5 0.3 copy.147
  58.9 0.2 copy.131
  59.1 3.3 %collective-permute-start = (bf16[2,1024,31]{1,2,0:T(8,128)(2,1)S(1)}, bf16[2,1024,31]{1,2,0:T(8,128)(2,1)S(1)}, u32[]{:S(2)}, u32[]{:S(2)}) collective-permute-start(bf16[2,1024,31]{1,2,0:T(8,128)(2,1)S(1)} %copy.131), channel_id=1, source_target_pairs={{4,0},{8,4},{12,8},{16,12},{20,16},{24,20},{28,24},{32,28},{36,32}... | collective-permute-start | bytes 380936 | tf_op jit(solution)/shard_map/ppermute | solution.py:21
  62.4 1.3 %fusion.33 = bf16[2,1024,1024]{2,1,0:T(8,128)(2,1)S(1)} fusion(pred[159,1024]{1,0:T(8,128)(4,1)S(1)} %iota_compare_fusion, bf16[2,128,8,128]{3,1,0,2:T(8,128)(2,1)S(1)} %fusion.1), kind=kOutput, calls=%fused_computation.85 | convolution fusion | flops 536870912 | bytes 4849664 | tf_op jit(solution)/shard_map/xpc,cn->xpn/dot_general | solution.py:210
  63.7 2.9 %collective-permute-done = bf16[2,1024,31]{1,2,0:T(8,128)(2,1)S(1)} collective-permute-done((bf16[2,1024,31]{1,2,0:T(8,128)(2,1)S(1)}, bf16[2,1024,31]{1,2,0:T(8,128)(2,1)S(1)}, u32[]{:S(2)}, u32[]{:S(2)}) %collective-permute-start) | collective-permute-done | bytes 127008 | tf_op jit(solution)/shard_map/ppermute | solution.py:21
  66.6 1.3 %fusion.37 = bf16[2,1024,8,32]{3,1,0,2:T(8,128)(2,1)S(1)} fusion(bf16[2,1024,31]{1,2,0:T(8,128)(2,1)S(1)} %collective-permute-done, pred[31,8,128]{0,2,1:T(32,128)(4,1)S(1)} %bitcast.128), kind=kOutput, calls=%fused_computation.94 | convolution fusion | flops 32505856 | bytes 1212416 | tf_op jit(solution)/shard_map/xpc,ckn->xpkn/dot_general | solution.py:214
  67.9 0.3 slice_bitcast_fusion.7
  68.2 1.5 %fusion.25 = (f32[2,1024,128]{2,1,0:T(8,128)S(1)}, f32[2,1024,128]{2,1,0:T(8,128)S(1)}, f32[2,1024,128]{2,1,0:T(8,128)S(1)}, f32[2,1024,128]{2,1,0:T(8,128)S(1)}...) fusion(bf16[2,1024,1024]{2,1,0:T(8,128)(2,1)S(1)} %fusion.33, ...), kind=kLoop, calls=%fused_computation.64 | loop fusion | flops 8388608 | bytes 13631488 | tf_op jit(solution)/shard_map/convert_element_type | solution.py:221
  69.7 0.0 copy-start.6
  69.7 2.5 %subtract_convert_fusion.1 = (bf16[1,1024,128]{2,1,0:T(8,128)(2,1)S(1)}, f32[1,1024,128]{2,1,0:T(8,128)S(1)}, f32[1,1024,128]{2,1,0:T(8,128)S(1)}) fusion(f32[1,511,128]{2,1,0:T(8,128)S(1)} %bitcast.121, f32[1,513,128]{2,1,0:T(8,128)S(1)} %get-tuple-element.39, f32[1,511,128]{2,1,0:T(8,128)S(1)} %bitcast.119, f32[1,513,128]{2,1,0:T(8,128)S(1)} %get-tuple-element.38, ...), kind=kLoop, calls=%fused_computation.81 | loop fusion | flops 4718592 | bytes 10780672 | tf_op jit(solution)/shard_map/convert_element_type | solution.py:232
  72.2 0.0 copy-start.3
  72.2 0.0 copy-start.2
  72.3 0.2 add_convert_fusion.1
  72.4 0.2 copy.110
  72.6 0.2 copy.109
  72.8 0.0 copy-done.6
  72.8 0.3 convolution_bitcast_fusion
  73.1 0.0 copy-done.3
  73.2 0.4 subtract_convert_fusion
  73.5 0.1 pad_maximum_fusion.2
  73.6 0.0 copy-done.2
  73.6 0.3 convolution_bitcast_fusion.2
  73.9 0.1 fusion.34
  74.0 0.2 fusion.35
  74.1 0.7 copy.113
  74.8 4.0 %all-to-all-start.1 = ((f32[4,8,8,128]{3,2,1,0:T(8,128)}), f32[4,8,8,128]{3,2,1,0:T(8,128)S(1)}, u32[]{:S(2)}, u32[]{:S(2)}) async-start(f32[4,8,8,128]{3,2,1,0:T(8,128)} %copy.113), calls=%async_computation.1 | async-start | bytes 262144 | tf_op jit(solution)/shard_map/all_to_all | solution.py:252
  78.8 0.6 fusion.51
  80.1 3.5 %all-to-all-done.1 = f32[4,8,8,128]{3,2,1,0:T(8,128)S(1)} async-done(((f32[4,8,8,128]{3,2,1,0:T(8,128)}), f32[4,8,8,128]{3,2,1,0:T(8,128)S(1)}, u32[]{:S(2)}, u32[]{:S(2)}) %all-to-all-start.1) | async-done | bytes 131104 | tf_op jit(solution)/shard_map/all_to_all | solution.py:252
  83.7 0.6 copy.148
  (8 shorter events, 0.1 us)
Async XLA Ops:
  0.0 57.4 %copy-start.7 = (bf16[2,8,2,8,1]{3,1,2,4,0:T(8,128)(2,1)S(1)}, bf16[2,8,2,8,1]{3,1,2,4,0:T(8,128)(2,1)}, u32[]{:S(2)}) copy-start(bf16[2,8,2,8,1]{3,1,2,4,0:T(8,128)(2,1)} %constant.87) | copy-start | bytes 1540
  0.0 27.8 %copy-start.8 = (f32[128]{0:T(128)S(1)}, f32[128]{0:T(128)}, u32[]{:S(2)}) copy-start(f32[128]{0:T(128)} %param.24) | copy-start | bytes 1540
  0.0 27.6 %copy-start.9 = (s32[4,16]{1,0:T(4,128)S(1)}, s32[4,16]{1,0:T(4,128)}, u32[]{:S(2)}) copy-start(s32[4,16]{1,0:T(4,128)} %param.25) | copy-start | bytes 772
  0.0 27.8 %copy-start.5 = (f32[8,1024]{1,0:T(8,128)S(1)}, f32[8,1024]{1,0:T(8,128)}, u32[]{:S(2)}) copy-start(f32[8,1024]{1,0:T(8,128)} %param.22) | copy-start | bytes 98308
  0.0 57.8 %copy-start = (f32[8,128]{0,1:T(8,128)S(1)}, f32[8,128]{0,1:T(8,128)}, u32[]{:S(2)}) copy-start(f32[8,128]{0,1:T(8,128)} %constant.63.clone) | copy-start | bytes 12292
  0.0 57.8 %copy-start.4 = (f32[8,128]{0,1:T(8,128)S(1)}, f32[8,128]{0,1:T(8,128)}, u32[]{:S(2)}) copy-start(f32[8,128]{0,1:T(8,128)} %constant.64.clone) | copy-start | bytes 12292
  3.5 53.8 %all-to-all-start = ((bf16[128,2,8,128]{3,2,1,0:T(8,128)(2,1)}), bf16[128,2,8,128]{3,2,1,0:T(8,128)(2,1)S(1)}, u32[]{:S(2)}, u32[]{:S(2)}) async-start(bf16[128,2,8,128]{3,2,1,0:T(8,128)(2,1)} %bitcast.127), calls=%async_computation | async-start | bytes 1048576 | tf_op jit(solution)/shard_map/all_to_all | solution.py:199
  24.9 33.4 %copy-start.1 = (bf16[2,128,2,128,1]{3,1,2,0,4:T(8,128)(2,1)S(1)}, bf16[2,128,2,128,1]{3,1,2,0,4:T(8,128)(2,1)}, u32[]{:S(2)}) copy-start(bf16[2,128,2,128,1]{3,1,2,0,4:T(8,128)(2,1)} %constant.88) | copy-start | bytes 393220
  59.1 7.4 %collective-permute-start = (bf16[2,1024,31]{1,2,0:T(8,128)(2,1)S(1)}, bf16[2,1024,31]{1,2,0:T(8,128)(2,1)S(1)}, u32[]{:S(2)}, u32[]{:S(2)}) collective-permute-start(bf16[2,1024,31]{1,2,0:T(8,128)(2,1)S(1)} %copy.131), channel_id=1, source_target_pairs={{4,0},{8,4},{12,8},{16,12},{20,16},{24,20},{28,24},{32,28},{36,32}... | collective-permute-start | bytes 380936 | tf_op jit(solution)/shard_map/ppermute | solution.py:21
  69.7 3.1 %copy-start.6 = (bf16[2,8,2,8,1]{3,1,2,4,0:T(8,128)(2,1)S(1)}, bf16[2,8,2,8,1]{3,1,2,4,0:T(8,128)(2,1)}, u32[]{:S(2)}) copy-start(bf16[2,8,2,8,1]{3,1,2,4,0:T(8,128)(2,1)} %constant.86) | copy-start | bytes 1540
  72.2 0.9 %copy-start.3 = (f32[8,128]{0,1:T(8,128)S(1)}, f32[8,128]{0,1:T(8,128)}, u32[]{:S(2)}) copy-start(f32[8,128]{0,1:T(8,128)} %constant.67.clone) | copy-start | bytes 12292
  72.2 1.3 %copy-start.2 = (bf16[2,128,2,128,1]{3,1,2,4,0:T(8,128)(2,1)S(1)}, bf16[2,128,2,128,1]{3,1,2,4,0:T(8,128)(2,1)}, u32[]{:S(2)}) copy-start(bf16[2,128,2,128,1]{3,1,2,4,0:T(8,128)(2,1)} %constant.85) | copy-start | bytes 393220
  74.8 8.8 %all-to-all-start.1 = ((f32[4,8,8,128]{3,2,1,0:T(8,128)}), f32[4,8,8,128]{3,2,1,0:T(8,128)S(1)}, u32[]{:S(2)}, u32[]{:S(2)}) async-start(f32[4,8,8,128]{3,2,1,0:T(8,128)} %copy.113), calls=%async_computation.1 | async-start | bytes 262144 | tf_op jit(solution)/shard_map/all_to_all | solution.py:252

commit v12 on v10

--- a/solution.py
+++ b/solution.py
@@ -70,7 +70,7 @@
 
 
 def range_kernel(
-    echo_ref, replica_ref, fwd_ref, fwd_t_ref, inv_ref, inv_t_ref, fwd_tw_ref, inv_tw_ref, out_ref, wide_ref
+    echo_ref, replica_ref, fwd_ref, fwd_t_ref, inv_ref, inv_t_ref, fwd_tw_ref, inv_tw_ref, out_ref
 ):
     pulses = echo_ref.shape[1] // echo_ref.shape[2]
     side = echo_ref.shape[2]
@@ -122,10 +122,7 @@
         axis=1,
     )
     comp = jnp.dot(inv, stacked, preferred_element_type=jnp.float32)
-    for pulse in range(pulses):
-        wide_ref[pl.ds(pulse, side, stride=2 * pulses), :] = by_pulse(comp[:side], pulse)
-        wide_ref[pl.ds(pulses + pulse, side, stride=2 * pulses), :] = by_pulse(comp[side:], pulse)
-    out_ref[...] = wide_ref[...].astype(jnp.bfloat16)
+    out_ref[...] = pltpu.einshape("(rd)(pb)->(drp)b", comp, r=2, p=pulses).astype(jnp.bfloat16)
 
 
 def range_compress(echo, range_replica):
@@ -144,7 +141,6 @@
         in_specs=[whole] * 8,
         out_specs=whole,
         out_shape=jax.ShapeDtypeStruct((side * 2 * pulses, side), jnp.bfloat16),
-        scratch_shapes=[pltpu.VMEM((side * 2 * pulses, side), jnp.float32)],
         cost_estimate=pl.CostEstimate(
             flops=(pulses + 1) * 4 * 2 * (2 * side) ** 2 * side,
             bytes_accessed=pulses * 2 * 2 * length * 2,

time: 83.8 us -> 83.7 us (level)
  no operation moved by 1% of the time
where the time goes in v12:
time: 83.7 us; the launch traced here: 83.3 us
  waiting for transfers between devices  34.8 us (42%)
  starting transfers between devices  27.8 us (33%)
  other arithmetic  8.22 us (10%)
  local copies, waits for them, and re-layouts  5.2 us (6%)
  Pallas kernels  3.41 us (4%)
  matrix products  2.84 us (3%)
  between operations  0.96 us (1%)
    all_to_all x1, waiting for transfers between devices, per_device(): lax.all_to_all(compressed, 'wide', split_axis=0, concat_axis=2, tiled=True)  27.8 us
    all_to_all x1, starting transfers between devices, per_device(): lax.all_to_all(compressed, 'wide', split_axis=0, concat_axis=2, tiled=True)  20.7 us
    all_to_all x1, starting transfers between devices, per_device(): lax.all_to_all(partial, 'narrow', split_axis=0, concat_axis=0, tiled=True)  4.01 us
    all_to_all x1, waiting for transfers between devices, per_device(): lax.all_to_all(partial, 'narrow', split_axis=0, concat_axis=0, tiled=True)  3.54 us
    ppermute x1, waiting for transfers between devices, passed_along(): return lax.ppermute(shard, axis, pairs)  3.48 us
    pallas_call x1, Pallas kernels, range_compress(): pl.pallas_call(range_kernel, in_specs=[whole] * 8, out_specs=whole, out_s...  3.41 us
    ppermute x1, starting transfers between devices, passed_along(): return lax.ppermute(shard, axis, pairs)  3.11 us
    convert_element_type x1, other arithmetic, per_device(): (moved_real * phase_cos - moved_imag * phase_sin).astype(jnp.bfloat16)  2.49 us
  transfers between devices with their start and end apart: 3, of which 3 were waited for; matrix products, arithmetic and copies ran while one was open for 8% of the time, Pallas kernels for 0%

profile of v12, /device:TPU:1, one launch (start us, length us, event | category | flops | bytes accessed | tf_op | source)
XLA Modules:
  0.0 83.3 jit_solution(3706829233605981206)
XLA Ops:
  0.0 0.0 copy-start.6
  0.0 0.0 copy-start
  0.0 0.0 copy-start.4
  0.0 3.4 %shard_map.190 = bf16[2048,128]{1,0:T(8,128)(2,1)} custom-call(bf16[2,1024,128]{2,1,0:T(8,128)(2,1)} %bitcast.109, bf16[2,4096]{1,0:T(2,128)(2,1)} %replica_ref.1, bf16[256,256]{1,0:T(8,128)(2,1)} %constant.55.clone.fwd_ref.inv_t_ref, bf16[256,256]{1,0:T(8,128)(2,1)} %constant.56.clone.fwd_t_ref.inv_ref, bf16[256,256]{1,0:T(8,128)(2,1)} %constant.56.clone.fwd_t_ref.inv_ref, ...), custom_call_target="tpu_custom_call" | custom-call | flops 603979776 | bytes 1048576 | tf_op jit(solution)/shard_map/pallas_call | solution.py:139
  3.4 0.0 copy-start.1
  3.4 20.7 %all-to-all-start = ((bf16[128,2,8,128]{3,2,1,0:T(8,128)(2,1)}), bf16[128,2,8,128]{3,2,1,0:T(8,128)(2,1)S(1)}, u32[]{:S(2)}, u32[]{:S(2)}) async-start(bf16[128,2,8,128]{3,2,1,0:T(8,128)(2,1)} %bitcast.100), calls=%async_computation | async-start | bytes 1048576 | tf_op jit(solution)/shard_map/all_to_all | solution.py:195
  24.1 0.7 iota_add_fusion
  24.8 1.2 %fusion.52 = (f32[1,1024]{1,0:T(1,128)S(1)}, f32[1,1024]{1,0:T(1,128)S(1)}, f32[1,1024]{1,0:T(1,128)S(1)}, f32[1,1024]{1,0:T(1,128)S(1)}, f32[1,1024]{1,0:T(1,12...) fusion(f32[8,1024]{1,0:T(8,128)} %param.22), kind=kLoop, calls=%fused_computation.108 | loop fusion | bytes 65536 | tf_op jit(solution)/shard_map/slice | solution.py:209
  26.1 0.8 broadcast_divide_fusion
  26.9 1.7 %divide_cosine_fusion = (f32[1,513,128]{2,1,0:T(8,128)S(1)}, f32[1,513,128]{2,1,0:T(8,128)S(1)}) fusion(f32[128]{0:T(128)} %param.24, f32[513]{0:T(1024)S(1)} %fusion.40), kind=kLoop, calls=%fused_computation.80 | loop fusion | flops 65664 | bytes 527876 | tf_op jit(solution)/shard_map/cos | solution.py:217
  28.5 1.0 %slice_cosine_fusion = (f32[511,128]{1,0:T(8,128)S(1)}, f32[511,128]{1,0:T(8,128)S(1)}) fusion(f32[513,128]{1,0:T(8,128)S(1)} %broadcast_divide_fusion), kind=kLoop, calls=%fused_computation.78 | loop fusion | bytes 784896 | tf_op jit(solution)/shard_map/cos | solution.py:217
  29.5 27.8 %all-to-all-done = bf16[128,2,8,128]{3,2,1,0:T(8,128)(2,1)S(1)} async-done(((bf16[128,2,8,128]{3,2,1,0:T(8,128)(2,1)}), bf16[128,2,8,128]{3,2,1,0:T(8,128)(2,1)S(1)}, u32[]{:S(2)}, u32[]{:S(2)}) %all-to-all-start) | async-done | bytes 524320 | tf_op jit(solution)/shard_map/all_to_all | solution.py:195
  57.4 0.0 copy-start.7
  57.4 0.0 copy-done.6
  57.4 0.4 convolution_bitcast_fusion.1
  57.8 0.0 copy-done
  57.8 0.0 copy-done.4
  57.8 0.4 subtract_convert_fusion.2
  58.2 0.1 maximum_bitcast_fusion
  58.3 0.0 copy-done.1
  58.3 0.3 fusion.1
  58.6 0.3 copy.100
  58.9 0.2 copy.66
  59.2 3.1 %collective-permute-start = (bf16[2,1024,31]{1,2,0:T(8,128)(2,1)S(1)}, bf16[2,1024,31]{1,2,0:T(8,128)(2,1)S(1)}, u32[]{:S(2)}, u32[]{:S(2)}) collective-permute-start(bf16[2,1024,31]{1,2,0:T(8,128)(2,1)S(1)} %slice.194), channel_id=1, source_target_pairs={{4,0},{8,4},{12,8},{16,12},{20,16},{24,20},{28,24},{32,28},{36,32}... | collective-permute-start | bytes 380936 | tf_op jit(solution)/shard_map/ppermute | solution.py:21
  62.3 0.0 copy-done.7
  62.3 0.3 rev.7
  62.7 0.3 rev.8
  63.0 0.1 convert_reduce_fusion
  63.1 3.5 %collective-permute-done = bf16[2,1024,31]{1,2,0:T(8,128)(2,1)S(1)} collective-permute-done((bf16[2,1024,31]{1,2,0:T(8,128)(2,1)S(1)}, bf16[2,1024,31]{1,2,0:T(8,128)(2,1)S(1)}, u32[]{:S(2)}, u32[]{:S(2)}) %collective-permute-start) | collective-permute-done | bytes 127008 | tf_op jit(solution)/shard_map/ppermute | solution.py:21
  66.6 1.3 %fusion.2 = bf16[2,1024,1024]{2,1,0:T(8,128)(2,1)S(1)} fusion(bf16[2,1024,31]{1,2,0:T(8,128)(2,1)S(1)} %collective-permute-done, bf16[2,1024,128]{1,2,0:T(8,128)(2,1)S(1)} %copy.66, s32[1024]{0:T(1024)S(1)} %add_bitcast_fusion), kind=kOutput, calls=%fused_computation.6 | convolution fusion | flops 668359680 | bytes 4849664 | tf_op jit(solution)/shard_map/xpc,cn->xpn/dot_general | solution.py:207
  67.9 0.8 slice_convert_fusion.7
  68.8 0.0 copy-start.5
  68.8 2.5 %subtract_convert_fusion.1 = (bf16[1,1024,128]{2,1,0:T(8,128)(2,1)S(1)}, f32[1,1024,128]{2,1,0:T(8,128)S(1)}, f32[1,1024,128]{2,1,0:T(8,128)S(1)}) fusion(f32[1,511,128]{2,1,0:T(8,128)S(1)} %bitcast.94, f32[1,513,128]{2,1,0:T(8,128)S(1)} %get-tuple-element.31, f32[1,511,128]{2,1,0:T(8,128)S(1)} %bitcast.92, f32[1,513,128]{2,1,0:T(8,128)S(1)} %get-tuple-element.30, ...), kind=kLoop, calls=%fused_computation.70 | loop fusion | flops 4718592 | bytes 10780672 | tf_op jit(solution)/shard_map/convert_element_type | solution.py:221
  71.3 0.0 copy-start.3
  71.3 0.0 copy-start.2
  71.3 0.1 add_convert_fusion.1
  71.4 0.2 copy.68
  71.6 0.2 copy.67
  71.8 0.0 copy-done.5
  71.8 0.3 convolution_bitcast_fusion
  72.2 0.0 copy-done.3
  72.2 0.4 subtract_convert_fusion
  72.5 0.1 pad_maximum_fusion.2
  72.6 0.0 copy-done.2
  72.6 0.3 convolution_bitcast_fusion.2
  72.9 0.1 fusion.32
  73.0 0.2 fusion.33
  73.1 0.6 copy.71
  73.8 4.0 %all-to-all-start.1 = ((f32[4,8,8,128]{3,2,1,0:T(8,128)}), f32[4,8,8,128]{3,2,1,0:T(8,128)S(1)}, u32[]{:S(2)}, u32[]{:S(2)}) async-start(f32[4,8,8,128]{3,2,1,0:T(8,128)} %copy.71), calls=%async_computation.1 | async-start | bytes 262144 | tf_op jit(solution)/shard_map/all_to_all | solution.py:241
  77.8 0.6 fusion.47
  79.1 3.5 %all-to-all-done.1 = f32[4,8,8,128]{3,2,1,0:T(8,128)S(1)} async-done(((f32[4,8,8,128]{3,2,1,0:T(8,128)}), f32[4,8,8,128]{3,2,1,0:T(8,128)S(1)}, u32[]{:S(2)}, u32[]{:S(2)}) %all-to-all-start.1) | async-done | bytes 131104 | tf_op jit(solution)/shard_map/all_to_all | solution.py:241
  82.7 0.6 copy.101
  (7 shorter events, 0.1 us)
Async XLA Ops:
  0.0 57.4 %copy-start.6 = (bf16[2,8,2,8,1]{3,1,2,4,0:T(8,128)(2,1)S(1)}, bf16[2,8,2,8,1]{3,1,2,4,0:T(8,128)(2,1)}, u32[]{:S(2)}) copy-start(bf16[2,8,2,8,1]{3,1,2,4,0:T(8,128)(2,1)} %constant.69) | copy-start | bytes 1540
  0.0 57.8 %copy-start = (f32[8,128]{0,1:T(8,128)S(1)}, f32[8,128]{0,1:T(8,128)}, u32[]{:S(2)}) copy-start(f32[8,128]{0,1:T(8,128)} %constant.61.clone) | copy-start | bytes 12292
  0.0 57.8 %copy-start.4 = (f32[8,128]{0,1:T(8,128)S(1)}, f32[8,128]{0,1:T(8,128)}, u32[]{:S(2)}) copy-start(f32[8,128]{0,1:T(8,128)} %constant.62.clone) | copy-start | bytes 12292
  3.4 54.8 %copy-start.1 = (bf16[2,128,2,128,1]{3,1,2,0,4:T(8,128)(2,1)S(1)}, bf16[2,128,2,128,1]{3,1,2,0,4:T(8,128)(2,1)}, u32[]{:S(2)}) copy-start(bf16[2,128,2,128,1]{3,1,2,0,4:T(8,128)(2,1)} %constant.70) | copy-start | bytes 393220
  3.4 53.9 %all-to-all-start = ((bf16[128,2,8,128]{3,2,1,0:T(8,128)(2,1)}), bf16[128,2,8,128]{3,2,1,0:T(8,128)(2,1)S(1)}, u32[]{:S(2)}, u32[]{:S(2)}) async-start(bf16[128,2,8,128]{3,2,1,0:T(8,128)(2,1)} %bitcast.100), calls=%async_computation | async-start | bytes 1048576 | tf_op jit(solution)/shard_map/all_to_all | solution.py:195
  57.4 4.9 %copy-start.7 = (s32[4,16]{1,0:T(4,128)S(1)}, s32[4,16]{1,0:T(4,128)}, u32[]{:S(2)}) copy-start(s32[4,16]{1,0:T(4,128)} %param.25) | copy-start | bytes 772
  59.2 7.4 %collective-permute-start = (bf16[2,1024,31]{1,2,0:T(8,128)(2,1)S(1)}, bf16[2,1024,31]{1,2,0:T(8,128)(2,1)S(1)}, u32[]{:S(2)}, u32[]{:S(2)}) collective-permute-start(bf16[2,1024,31]{1,2,0:T(8,128)(2,1)S(1)} %slice.194), channel_id=1, source_target_pairs={{4,0},{8,4},{12,8},{16,12},{20,16},{24,20},{28,24},{32,28},{36,32}... | collective-permute-start | bytes 380936 | tf_op jit(solution)/shard_map/ppermute | solution.py:21
  68.8 3.0 %copy-start.5 = (bf16[2,8,2,8,1]{3,1,2,4,0:T(8,128)(2,1)S(1)}, bf16[2,8,2,8,1]{3,1,2,4,0:T(8,128)(2,1)}, u32[]{:S(2)}) copy-start(bf16[2,8,2,8,1]{3,1,2,4,0:T(8,128)(2,1)} %constant.68) | copy-start | bytes 1540
  71.3 0.9 %copy-start.3 = (f32[8,128]{0,1:T(8,128)S(1)}, f32[8,128]{0,1:T(8,128)}, u32[]{:S(2)}) copy-start(f32[8,128]{0,1:T(8,128)} %constant.65.clone) | copy-start | bytes 12292
  71.3 1.3 %copy-start.2 = (bf16[2,128,2,128,1]{3,1,2,4,0:T(8,128)(2,1)S(1)}, bf16[2,128,2,128,1]{3,1,2,4,0:T(8,128)(2,1)}, u32[]{:S(2)}) copy-start(bf16[2,128,2,128,1]{3,1,2,4,0:T(8,128)(2,1)} %constant.67) | copy-start | bytes 393220
  73.8 8.8 %all-to-all-start.1 = ((f32[4,8,8,128]{3,2,1,0:T(8,128)}), f32[4,8,8,128]{3,2,1,0:T(8,128)S(1)}, u32[]{:S(2)}, u32[]{:S(2)}) async-start(f32[4,8,8,128]{3,2,1,0:T(8,128)} %copy.71), calls=%async_computation.1 | async-start | bytes 262144 | tf_op jit(solution)/shard_map/all_to_all | solution.py:241

commit v13 on v12

--- a/solution.py
+++ b/solution.py
@@ -88,11 +88,12 @@
     rep_real, rep_imag = forward_transposed(replica, fwd, fwd_t, fwd_tw)
     rep_real = rep_real * 128.0
     rep_imag = rep_imag * 128.0
-    blocks = []
-    for pulse in range(pulses):
-        rows = pl.ds(pulse, side, stride=pulses)
-        blocks.append(jnp.concatenate([echo_ref[0, rows, :], echo_ref[1, rows, :]], axis=0))
-    mid = jnp.dot(fwd, jnp.concatenate(blocks, axis=1), preferred_element_type=jnp.float32)
+    split = [
+        pltpu.einshape("(np)b->n(pb)", echo_ref[part].astype(jnp.float32), p=pulses)
+        for part in range(2)
+    ]
+    stacked = jnp.concatenate(split, axis=0).astype(jnp.bfloat16)
+    mid = jnp.dot(fwd, stacked, preferred_element_type=jnp.float32)
     along = lambda x: jnp.concatenate([x] * pulses, axis=1)
     down = lambda x: jnp.concatenate([x] * pulses, axis=0)
     turn_real, turn_imag = twist(mid[:side], mid[side:], (along(fwd_tw[0]), along(fwd_tw[1])))

time: 83.7 us -> 83.8 us (level)
  no operation moved by 1% of the time
where the time goes in v13:
time: 83.8 us; the launch traced here: 83.4 us
  waiting for transfers between devices  34.8 us (42%)
  starting transfers between devices  27.8 us (33%)
  other arithmetic  8.22 us (10%)
  local copies, waits for them, and re-layouts  5.2 us (6%)
  Pallas kernels  3.49 us (4%)
  matrix products  2.84 us (3%)
  between operations  0.96 us (1%)
    all_to_all x1, waiting for transfers between devices, per_device(): lax.all_to_all(compressed, 'wide', split_axis=0, concat_axis=2, tiled=True)  27.8 us
    all_to_all x1, starting transfers between devices, per_device(): lax.all_to_all(compressed, 'wide', split_axis=0, concat_axis=2, tiled=True)  20.7 us
    all_to_all x1, starting transfers between devices, per_device(): lax.all_to_all(partial, 'narrow', split_axis=0, concat_axis=0, tiled=True)  4.01 us
    all_to_all x1, waiting for transfers between devices, per_device(): lax.all_to_all(partial, 'narrow', split_axis=0, concat_axis=0, tiled=True)  3.54 us
    pallas_call x1, Pallas kernels, range_compress(): pl.pallas_call(range_kernel, in_specs=[whole] * 8, out_specs=whole, out_s...  3.49 us
    ppermute x1, waiting for transfers between devices, passed_along(): return lax.ppermute(shard, axis, pairs)  3.48 us
    ppermute x1, starting transfers between devices, passed_along(): return lax.ppermute(shard, axis, pairs)  3.11 us
    convert_element_type x1, other arithmetic, per_device(): (moved_real * phase_cos - moved_imag * phase_sin).astype(jnp.bfloat16)  2.49 us
  transfers between devices with their start and end apart: 3, of which 3 were waited for; matrix products, arithmetic and copies ran while one was open for 8% of the time, Pallas kernels for 0%

profile of v13, /device:TPU:1, one launch (start us, length us, event | category | flops | bytes accessed | tf_op | source)
XLA Modules:
  0.0 83.4 jit_solution(16495804820234860986)
XLA Ops:
  0.0 0.0 copy-start.6
  0.0 0.0 copy-start
  0.0 0.0 copy-start.4
  0.0 3.5 %shard_map.190 = bf16[2048,128]{1,0:T(8,128)(2,1)} custom-call(bf16[2,1024,128]{2,1,0:T(8,128)(2,1)} %bitcast.109, bf16[2,4096]{1,0:T(2,128)(2,1)} %replica_ref.1, bf16[256,256]{1,0:T(8,128)(2,1)} %constant.55.clone.fwd_ref.inv_t_ref, bf16[256,256]{1,0:T(8,128)(2,1)} %constant.56.clone.fwd_t_ref.inv_ref, bf16[256,256]{1,0:T(8,128)(2,1)} %constant.56.clone.fwd_t_ref.inv_ref, ...), custom_call_target="tpu_custom_call" | custom-call | flops 603979776 | bytes 1048576 | tf_op jit(solution)/shard_map/pallas_call | solution.py:140
  3.5 0.0 copy-start.1
  3.5 20.7 %all-to-all-start = ((bf16[128,2,8,128]{3,2,1,0:T(8,128)(2,1)}), bf16[128,2,8,128]{3,2,1,0:T(8,128)(2,1)S(1)}, u32[]{:S(2)}, u32[]{:S(2)}) async-start(bf16[128,2,8,128]{3,2,1,0:T(8,128)(2,1)} %bitcast.100), calls=%async_computation | async-start | bytes 1048576 | tf_op jit(solution)/shard_map/all_to_all | solution.py:196
  24.2 0.7 iota_add_fusion
  24.9 1.2 %fusion.52 = (f32[1,1024]{1,0:T(1,128)S(1)}, f32[1,1024]{1,0:T(1,128)S(1)}, f32[1,1024]{1,0:T(1,128)S(1)}, f32[1,1024]{1,0:T(1,128)S(1)}, f32[1,1024]{1,0:T(1,12...) fusion(f32[8,1024]{1,0:T(8,128)} %param.22), kind=kLoop, calls=%fused_computation.108 | loop fusion | bytes 65536 | tf_op jit(solution)/shard_map/slice | solution.py:210
  26.1 0.8 broadcast_divide_fusion
  26.9 1.7 %divide_cosine_fusion = (f32[1,513,128]{2,1,0:T(8,128)S(1)}, f32[1,513,128]{2,1,0:T(8,128)S(1)}) fusion(f32[128]{0:T(128)} %param.24, f32[513]{0:T(1024)S(1)} %fusion.40), kind=kLoop, calls=%fused_computation.80 | loop fusion | flops 65664 | bytes 527876 | tf_op jit(solution)/shard_map/cos | solution.py:218
  28.6 1.0 %slice_cosine_fusion = (f32[511,128]{1,0:T(8,128)S(1)}, f32[511,128]{1,0:T(8,128)S(1)}) fusion(f32[513,128]{1,0:T(8,128)S(1)} %broadcast_divide_fusion), kind=kLoop, calls=%fused_computation.78 | loop fusion | bytes 784896 | tf_op jit(solution)/shard_map/cos | solution.py:218
  29.6 27.8 %all-to-all-done = bf16[128,2,8,128]{3,2,1,0:T(8,128)(2,1)S(1)} async-done(((bf16[128,2,8,128]{3,2,1,0:T(8,128)(2,1)}), bf16[128,2,8,128]{3,2,1,0:T(8,128)(2,1)S(1)}, u32[]{:S(2)}, u32[]{:S(2)}) %all-to-all-start) | async-done | bytes 524320 | tf_op jit(solution)/shard_map/all_to_all | solution.py:196
  57.5 0.0 copy-start.7
  57.5 0.0 copy-done.6
  57.5 0.4 convolution_bitcast_fusion.1
  57.9 0.0 copy-done
  57.9 0.0 copy-done.4
  57.9 0.4 subtract_convert_fusion.2
  58.3 0.1 maximum_bitcast_fusion
  58.3 0.0 copy-done.1
  58.4 0.3 fusion.1
  58.7 0.3 copy.100
  59.0 0.2 copy.66
  59.3 3.1 %collective-permute-start = (bf16[2,1024,31]{1,2,0:T(8,128)(2,1)S(1)}, bf16[2,1024,31]{1,2,0:T(8,128)(2,1)S(1)}, u32[]{:S(2)}, u32[]{:S(2)}) collective-permute-start(bf16[2,1024,31]{1,2,0:T(8,128)(2,1)S(1)} %slice.194), channel_id=1, source_target_pairs={{4,0},{8,4},{12,8},{16,12},{20,16},{24,20},{28,24},{32,28},{36,32}... | collective-permute-start | bytes 380936 | tf_op jit(solution)/shard_map/ppermute | solution.py:21
  62.4 0.0 copy-done.7
  62.4 0.3 rev.7
  62.7 0.3 rev.8
  63.1 0.1 convert_reduce_fusion
  63.2 3.5 %collective-permute-done = bf16[2,1024,31]{1,2,0:T(8,128)(2,1)S(1)} collective-permute-done((bf16[2,1024,31]{1,2,0:T(8,128)(2,1)S(1)}, bf16[2,1024,31]{1,2,0:T(8,128)(2,1)S(1)}, u32[]{:S(2)}, u32[]{:S(2)}) %collective-permute-start) | collective-permute-done | bytes 127008 | tf_op jit(solution)/shard_map/ppermute | solution.py:21
  66.7 1.3 %fusion.2 = bf16[2,1024,1024]{2,1,0:T(8,128)(2,1)S(1)} fusion(bf16[2,1024,31]{1,2,0:T(8,128)(2,1)S(1)} %collective-permute-done, bf16[2,1024,128]{1,2,0:T(8,128)(2,1)S(1)} %copy.66, s32[1024]{0:T(1024)S(1)} %add_bitcast_fusion), kind=kOutput, calls=%fused_computation.6 | convolution fusion | flops 668359680 | bytes 4849664 | tf_op jit(solution)/shard_map/xpc,cn->xpn/dot_general | solution.py:208
  68.0 0.8 slice_convert_fusion.7
  68.8 0.0 copy-start.5
  68.8 2.5 %subtract_convert_fusion.1 = (bf16[1,1024,128]{2,1,0:T(8,128)(2,1)S(1)}, f32[1,1024,128]{2,1,0:T(8,128)S(1)}, f32[1,1024,128]{2,1,0:T(8,128)S(1)}) fusion(f32[1,511,128]{2,1,0:T(8,128)S(1)} %bitcast.94, f32[1,513,128]{2,1,0:T(8,128)S(1)} %get-tuple-element.31, f32[1,511,128]{2,1,0:T(8,128)S(1)} %bitcast.92, f32[1,513,128]{2,1,0:T(8,128)S(1)} %get-tuple-element.30, ...), kind=kLoop, calls=%fused_computation.70 | loop fusion | flops 4718592 | bytes 10780672 | tf_op jit(solution)/shard_map/convert_element_type | solution.py:222
  71.3 0.0 copy-start.3
  71.4 0.0 copy-start.2
  71.4 0.1 add_convert_fusion.1
  71.5 0.2 copy.68
  71.7 0.2 copy.67
  71.9 0.0 copy-done.5
  71.9 0.3 convolution_bitcast_fusion
  72.2 0.0 copy-done.3
  72.2 0.4 subtract_convert_fusion
  72.6 0.1 pad_maximum_fusion.2
  72.7 0.0 copy-done.2
  72.7 0.3 convolution_bitcast_fusion.2
  73.0 0.1 fusion.32
  73.1 0.2 fusion.33
  73.2 0.6 copy.71
  73.9 4.0 %all-to-all-start.1 = ((f32[4,8,8,128]{3,2,1,0:T(8,128)}), f32[4,8,8,128]{3,2,1,0:T(8,128)S(1)}, u32[]{:S(2)}, u32[]{:S(2)}) async-start(f32[4,8,8,128]{3,2,1,0:T(8,128)} %copy.71), calls=%async_computation.1 | async-start | bytes 262144 | tf_op jit(solution)/shard_map/all_to_all | solution.py:242
  77.9 0.6 fusion.47
  79.2 3.5 %all-to-all-done.1 = f32[4,8,8,128]{3,2,1,0:T(8,128)S(1)} async-done(((f32[4,8,8,128]{3,2,1,0:T(8,128)}), f32[4,8,8,128]{3,2,1,0:T(8,128)S(1)}, u32[]{:S(2)}, u32[]{:S(2)}) %all-to-all-start.1) | async-done | bytes 131104 | tf_op jit(solution)/shard_map/all_to_all | solution.py:242
  82.7 0.6 copy.101
  (7 shorter events, 0.1 us)
Async XLA Ops:
  0.0 57.5 %copy-start.6 = (bf16[2,8,2,8,1]{3,1,2,4,0:T(8,128)(2,1)S(1)}, bf16[2,8,2,8,1]{3,1,2,4,0:T(8,128)(2,1)}, u32[]{:S(2)}) copy-start(bf16[2,8,2,8,1]{3,1,2,4,0:T(8,128)(2,1)} %constant.69) | copy-start | bytes 1540
  0.0 57.9 %copy-start = (f32[8,128]{0,1:T(8,128)S(1)}, f32[8,128]{0,1:T(8,128)}, u32[]{:S(2)}) copy-start(f32[8,128]{0,1:T(8,128)} %constant.61.clone) | copy-start | bytes 12292
  0.0 57.9 %copy-start.4 = (f32[8,128]{0,1:T(8,128)S(1)}, f32[8,128]{0,1:T(8,128)}, u32[]{:S(2)}) copy-start(f32[8,128]{0,1:T(8,128)} %constant.62.clone) | copy-start | bytes 12292
  3.5 54.8 %copy-start.1 = (bf16[2,128,2,128,1]{3,1,2,0,4:T(8,128)(2,1)S(1)}, bf16[2,128,2,128,1]{3,1,2,0,4:T(8,128)(2,1)}, u32[]{:S(2)}) copy-start(bf16[2,128,2,128,1]{3,1,2,0,4:T(8,128)(2,1)} %constant.70) | copy-start | bytes 393220
  3.5 53.9 %all-to-all-start = ((bf16[128,2,8,128]{3,2,1,0:T(8,128)(2,1)}), bf16[128,2,8,128]{3,2,1,0:T(8,128)(2,1)S(1)}, u32[]{:S(2)}, u32[]{:S(2)}) async-start(bf16[128,2,8,128]{3,2,1,0:T(8,128)(2,1)} %bitcast.100), calls=%async_computation | async-start | bytes 1048576 | tf_op jit(solution)/shard_map/all_to_all | solution.py:196
  57.5 4.9 %copy-start.7 = (s32[4,16]{1,0:T(4,128)S(1)}, s32[4,16]{1,0:T(4,128)}, u32[]{:S(2)}) copy-start(s32[4,16]{1,0:T(4,128)} %param.25) | copy-start | bytes 772
  59.3 7.4 %collective-permute-start = (bf16[2,1024,31]{1,2,0:T(8,128)(2,1)S(1)}, bf16[2,1024,31]{1,2,0:T(8,128)(2,1)S(1)}, u32[]{:S(2)}, u32[]{:S(2)}) collective-permute-start(bf16[2,1024,31]{1,2,0:T(8,128)(2,1)S(1)} %slice.194), channel_id=1, source_target_pairs={{4,0},{8,4},{12,8},{16,12},{20,16},{24,20},{28,24},{32,28},{36,32}... | collective-permute-start | bytes 380936 | tf_op jit(solution)/shard_map/ppermute | solution.py:21
  68.8 3.0 %copy-start.5 = (bf16[2,8,2,8,1]{3,1,2,4,0:T(8,128)(2,1)S(1)}, bf16[2,8,2,8,1]{3,1,2,4,0:T(8,128)(2,1)}, u32[]{:S(2)}) copy-start(bf16[2,8,2,8,1]{3,1,2,4,0:T(8,128)(2,1)} %constant.68) | copy-start | bytes 1540
  71.3 0.9 %copy-start.3 = (f32[8,128]{0,1:T(8,128)S(1)}, f32[8,128]{0,1:T(8,128)}, u32[]{:S(2)}) copy-start(f32[8,128]{0,1:T(8,128)} %constant.65.clone) | copy-start | bytes 12292
  71.4 1.3 %copy-start.2 = (bf16[2,128,2,128,1]{3,1,2,4,0:T(8,128)(2,1)S(1)}, bf16[2,128,2,128,1]{3,1,2,4,0:T(8,128)(2,1)}, u32[]{:S(2)}) copy-start(bf16[2,128,2,128,1]{3,1,2,4,0:T(8,128)(2,1)} %constant.67) | copy-start | bytes 393220
  73.9 8.8 %all-to-all-start.1 = ((f32[4,8,8,128]{3,2,1,0:T(8,128)}), f32[4,8,8,128]{3,2,1,0:T(8,128)S(1)}, u32[]{:S(2)}, u32[]{:S(2)}) async-start(f32[4,8,8,128]{3,2,1,0:T(8,128)} %copy.71), calls=%async_computation.1 | async-start | bytes 262144 | tf_op jit(solution)/shard_map/all_to_all | solution.py:242

commit v14 on v9

--- a/solution.py
+++ b/solution.py
@@ -70,7 +70,7 @@
 
 
 def range_kernel(
-    echo_ref, replica_ref, fwd_ref, fwd_t_ref, inv_ref, inv_t_ref, fwd_tw_ref, inv_tw_ref, out_ref, wide_ref
+    echo_ref, replica_ref, fwd_ref, fwd_t_ref, inv_ref, inv_t_ref, fwd_tw_ref, inv_tw_ref, out_ref
 ):
     pulses = echo_ref.shape[1] // echo_ref.shape[2]
     side = echo_ref.shape[2]
@@ -122,10 +122,7 @@
         axis=1,
     )
     comp = jnp.dot(inv, stacked, preferred_element_type=jnp.float32)
-    for pulse in range(pulses):
-        wide_ref[pl.ds(pulse, side, stride=2 * pulses), :] = by_pulse(comp[:side], pulse)
-        wide_ref[pl.ds(pulses + pulse, side, stride=2 * pulses), :] = by_pulse(comp[side:], pulse)
-    out_ref[...] = wide_ref[...].astype(jnp.bfloat16)
+    out_ref[...] = pltpu.einshape("(rd)(pb)->(drp)b", comp, r=2, p=pulses).astype(jnp.bfloat16)
 
 
 def range_compress(echo, range_replica):
@@ -144,7 +141,6 @@
         in_specs=[whole] * 8,
         out_specs=whole,
         out_shape=jax.ShapeDtypeStruct((side * 2 * pulses, side), jnp.bfloat16),
-        scratch_shapes=[pltpu.VMEM((side * 2 * pulses, side), jnp.float32)],
         cost_estimate=pl.CostEstimate(
             flops=(pulses + 1) * 4 * 2 * (2 * side) ** 2 * side,
             bytes_accessed=pulses * 2 * 2 * length * 2,

time: 84.1 us -> 84 us (level)
  no operation moved by 1% of the time
where the time goes in v14:
time: 84 us; the launch traced here: 83.6 us
  waiting for transfers between devices  34.8 us (41%)
  starting transfers between devices  27.8 us (33%)
  other arithmetic  8.84 us (11%)
  local copies, waits for them, and re-layouts  4.87 us (6%)
  Pallas kernels  3.41 us (4%)
  matrix products  2.84 us (3%)
  between operations  0.96 us (1%)
    all_to_all x1, waiting for transfers between devices, per_device(): lax.all_to_all(compressed, 'wide', split_axis=0, concat_axis=2, tiled=True)  27.8 us
    all_to_all x1, starting transfers between devices, per_device(): lax.all_to_all(compressed, 'wide', split_axis=0, concat_axis=2, tiled=True)  20.7 us
    all_to_all x1, starting transfers between devices, per_device(): lax.all_to_all(partial, 'narrow', split_axis=0, concat_axis=0, tiled=True)  4.01 us
    all_to_all x1, waiting for transfers between devices, per_device(): lax.all_to_all(partial, 'narrow', split_axis=0, concat_axis=0, tiled=True)  3.54 us
    ppermute x1, waiting for transfers between devices, passed_along(): return lax.ppermute(shard, axis, pairs)  3.48 us
    pallas_call x1, Pallas kernels, range_compress(): pl.pallas_call(range_kernel, in_specs=[whole] * 8, out_specs=whole, out_s...  3.41 us
    ppermute x1, starting transfers between devices, passed_along(): return lax.ppermute(shard, axis, pairs)  3.11 us
    convert_element_type x1, other arithmetic, per_device(): (moved_real * phase_cos - moved_imag * phase_sin).astype(jnp.bfloat16)  2.49 us
  transfers between devices with their start and end apart: 3, of which 3 were waited for; matrix products, arithmetic and copies ran while one was open for 8% of the time, Pallas kernels for 0%

profile of v14, /device:TPU:1, one launch (start us, length us, event | category | flops | bytes accessed | tf_op | source)
XLA Modules:
  0.0 83.6 jit_solution(14490736937389475713)
XLA Ops:
  0.0 0.0 copy-start.6
  0.0 0.0 copy-start
  0.0 0.0 copy-start.4
  0.0 3.4 %shard_map.190 = bf16[2048,128]{1,0:T(8,128)(2,1)} custom-call(bf16[2,1024,128]{2,1,0:T(8,128)(2,1)} %bitcast.108, bf16[2,4096]{1,0:T(2,128)(2,1)} %replica_ref.1, bf16[256,256]{1,0:T(8,128)(2,1)} %constant.55.clone.fwd_ref.inv_t_ref, bf16[256,256]{1,0:T(8,128)(2,1)} %constant.56.clone.fwd_t_ref.inv_ref, bf16[256,256]{1,0:T(8,128)(2,1)} %constant.56.clone.fwd_t_ref.inv_ref, ...), custom_call_target="tpu_custom_call" | custom-call | flops 603979776 | bytes 1048576 | tf_op jit(solution)/shard_map/pallas_call | solution.py:139
  3.4 0.0 copy-start.1
  3.4 20.7 %all-to-all-start = ((bf16[128,2,8,128]{3,2,1,0:T(8,128)(2,1)}), bf16[128,2,8,128]{3,2,1,0:T(8,128)(2,1)S(1)}, u32[]{:S(2)}, u32[]{:S(2)}) async-start(bf16[128,2,8,128]{3,2,1,0:T(8,128)(2,1)} %bitcast.99), calls=%async_computation | async-start | bytes 1048576 | tf_op jit(solution)/shard_map/all_to_all | solution.py:195
  24.1 0.7 iota_add_fusion
  24.8 1.2 %fusion.52 = (f32[1,1024]{1,0:T(1,128)S(1)}, f32[1,1024]{1,0:T(1,128)S(1)}, f32[1,1024]{1,0:T(1,128)S(1)}, f32[1,1024]{1,0:T(1,128)S(1)}, f32[1,1024]{1,0:T(1,12...) fusion(f32[8,1024]{1,0:T(8,128)} %param.22), kind=kLoop, calls=%fused_computation.107 | loop fusion | bytes 65536 | tf_op jit(solution)/shard_map/slice | solution.py:209
  26.1 0.8 broadcast_divide_fusion
  26.9 1.7 %divide_cosine_fusion = (f32[1,513,128]{2,1,0:T(8,128)S(1)}, f32[1,513,128]{2,1,0:T(8,128)S(1)}) fusion(f32[128]{0:T(128)} %param.24, f32[513]{0:T(1024)S(1)} %fusion.40), kind=kLoop, calls=%fused_computation.80 | loop fusion | flops 65664 | bytes 527876 | tf_op jit(solution)/shard_map/cos | solution.py:217
  28.5 1.0 %slice_cosine_fusion = (f32[511,128]{1,0:T(8,128)S(1)}, f32[511,128]{1,0:T(8,128)S(1)}) fusion(f32[513,128]{1,0:T(8,128)S(1)} %broadcast_divide_fusion), kind=kLoop, calls=%fused_computation.78 | loop fusion | bytes 784896 | tf_op jit(solution)/shard_map/cos | solution.py:217
  29.5 27.8 %all-to-all-done = bf16[128,2,8,128]{3,2,1,0:T(8,128)(2,1)S(1)} async-done(((bf16[128,2,8,128]{3,2,1,0:T(8,128)(2,1)}), bf16[128,2,8,128]{3,2,1,0:T(8,128)(2,1)S(1)}, u32[]{:S(2)}, u32[]{:S(2)}) %all-to-all-start) | async-done | bytes 524320 | tf_op jit(solution)/shard_map/all_to_all | solution.py:195
  57.4 0.0 copy-start.7
  57.4 0.0 copy-done.6
  57.4 0.4 convolution_bitcast_fusion.1
  57.8 0.0 copy-done
  57.8 0.0 copy-done.4
  57.8 0.4 subtract_convert_fusion.2
  58.2 0.1 maximum_bitcast_fusion
  58.3 0.0 copy-done.1
  58.3 0.3 fusion.1
  58.6 0.3 copy.86
  58.9 0.2 copy.53
  59.2 3.1 %collective-permute-start = (bf16[2,1024,31]{1,2,0:T(8,128)(2,1)S(1)}, bf16[2,1024,31]{1,2,0:T(8,128)(2,1)S(1)}, u32[]{:S(2)}, u32[]{:S(2)}) collective-permute-start(bf16[2,1024,31]{1,2,0:T(8,128)(2,1)S(1)} %slice.194), channel_id=1, source_target_pairs={{4,0},{8,4},{12,8},{16,12},{20,16},{24,20},{28,24},{32,28},{36,32}... | collective-permute-start | bytes 380936 | tf_op jit(solution)/shard_map/ppermute | solution.py:21
  62.3 0.0 copy-done.7
  62.3 0.3 rev.7
  62.7 0.3 rev.8
  63.0 0.1 convert_reduce_fusion
  63.1 3.5 %collective-permute-done = bf16[2,1024,31]{1,2,0:T(8,128)(2,1)S(1)} collective-permute-done((bf16[2,1024,31]{1,2,0:T(8,128)(2,1)S(1)}, bf16[2,1024,31]{1,2,0:T(8,128)(2,1)S(1)}, u32[]{:S(2)}, u32[]{:S(2)}) %collective-permute-start) | collective-permute-done | bytes 127008 | tf_op jit(solution)/shard_map/ppermute | solution.py:21
  66.6 1.3 %fusion.2 = bf16[2,1024,1024]{2,1,0:T(8,128)(2,1)S(1)} fusion(bf16[2,1024,31]{1,2,0:T(8,128)(2,1)S(1)} %collective-permute-done, bf16[2,1024,128]{1,2,0:T(8,128)(2,1)S(1)} %copy.53, s32[1024]{0:T(1024)S(1)} %add_bitcast_fusion), kind=kOutput, calls=%fused_computation.6 | convolution fusion | flops 668359680 | bytes 4849664 | tf_op jit(solution)/shard_map/xpc,cn->xpn/dot_general | solution.py:207
  67.9 0.8 slice_convert_fusion.7
  68.8 0.0 copy-start.5
  68.8 2.5 %subtract_convert_fusion.1 = (bf16[1,1024,128]{2,1,0:T(8,128)(2,1)S(1)}, f32[1,1024,128]{2,1,0:T(8,128)S(1)}, f32[1,1024,128]{2,1,0:T(8,128)S(1)}) fusion(f32[1,511,128]{2,1,0:T(8,128)S(1)} %bitcast.93, f32[1,513,128]{2,1,0:T(8,128)S(1)} %get-tuple-element.31, f32[1,511,128]{2,1,0:T(8,128)S(1)} %bitcast.91, f32[1,513,128]{2,1,0:T(8,128)S(1)} %get-tuple-element.30, ...), kind=kLoop, calls=%fused_computation.70 | loop fusion | flops 4718592 | bytes 10780672 | tf_op jit(solution)/shard_map/convert_element_type | solution.py:221
  71.3 0.0 copy-start.3
  71.3 0.0 copy-start.2
  71.3 0.1 add_convert_fusion.1
  71.4 0.2 copy.55
  71.6 0.2 copy.54
  71.8 0.0 copy-done.5
  71.8 0.3 convolution_bitcast_fusion
  72.2 0.0 copy-done.3
  72.2 0.4 subtract_convert_fusion
  72.5 0.1 pad_maximum_fusion.2
  72.6 0.0 copy-done.2
  72.6 0.3 convolution_bitcast_fusion.2
  72.9 0.1 fusion.9
  73.0 0.2 copy.57
  73.2 0.1 convert_element_type.82
  73.3 0.2 fusion.32
  73.4 0.6 copy.59
  74.1 4.0 %all-to-all-start.1 = ((f32[4,64,128]{2,1,0:T(8,128)}), f32[4,64,128]{2,1,0:T(8,128)S(1)}, u32[]{:S(2)}, u32[]{:S(2)}) async-start(f32[4,64,128]{2,1,0:T(8,128)} %copy.59), calls=%async_computation.1 | async-start | bytes 262144 | tf_op jit(solution)/shard_map/all_to_all | solution.py:239
  78.1 0.6 fusion.47
  79.4 3.5 %all-to-all-done.1 = f32[4,64,128]{2,1,0:T(8,128)S(1)} async-done(((f32[4,64,128]{2,1,0:T(8,128)}), f32[4,64,128]{2,1,0:T(8,128)S(1)}, u32[]{:S(2)}, u32[]{:S(2)}) %all-to-all-start.1) | async-done | bytes 131104 | tf_op jit(solution)/shard_map/all_to_all | solution.py:239
  82.9 0.6 divide_bitcast_fusion
  (6 shorter events, 0.1 us)
Async XLA Ops:
  0.0 57.4 %copy-start.6 = (bf16[2,8,2,8,1]{3,1,2,4,0:T(8,128)(2,1)S(1)}, bf16[2,8,2,8,1]{3,1,2,4,0:T(8,128)(2,1)}, u32[]{:S(2)}) copy-start(bf16[2,8,2,8,1]{3,1,2,4,0:T(8,128)(2,1)} %constant.69) | copy-start | bytes 1540
  0.0 57.8 %copy-start = (f32[8,128]{0,1:T(8,128)S(1)}, f32[8,128]{0,1:T(8,128)}, u32[]{:S(2)}) copy-start(f32[8,128]{0,1:T(8,128)} %constant.61.clone) | copy-start | bytes 12292
  0.0 57.8 %copy-start.4 = (f32[8,128]{0,1:T(8,128)S(1)}, f32[8,128]{0,1:T(8,128)}, u32[]{:S(2)}) copy-start(f32[8,128]{0,1:T(8,128)} %constant.62.clone) | copy-start | bytes 12292
  3.4 54.8 %copy-start.1 = (bf16[2,128,2,128,1]{3,1,2,0,4:T(8,128)(2,1)S(1)}, bf16[2,128,2,128,1]{3,1,2,0,4:T(8,128)(2,1)}, u32[]{:S(2)}) copy-start(bf16[2,128,2,128,1]{3,1,2,0,4:T(8,128)(2,1)} %constant.70) | copy-start | bytes 393220
  3.4 53.9 %all-to-all-start = ((bf16[128,2,8,128]{3,2,1,0:T(8,128)(2,1)}), bf16[128,2,8,128]{3,2,1,0:T(8,128)(2,1)S(1)}, u32[]{:S(2)}, u32[]{:S(2)}) async-start(bf16[128,2,8,128]{3,2,1,0:T(8,128)(2,1)} %bitcast.99), calls=%async_computation | async-start | bytes 1048576 | tf_op jit(solution)/shard_map/all_to_all | solution.py:195
  57.4 4.9 %copy-start.7 = (s32[4,16]{1,0:T(4,128)S(1)}, s32[4,16]{1,0:T(4,128)}, u32[]{:S(2)}) copy-start(s32[4,16]{1,0:T(4,128)} %param.25) | copy-start | bytes 772
  59.2 7.4 %collective-permute-start = (bf16[2,1024,31]{1,2,0:T(8,128)(2,1)S(1)}, bf16[2,1024,31]{1,2,0:T(8,128)(2,1)S(1)}, u32[]{:S(2)}, u32[]{:S(2)}) collective-permute-start(bf16[2,1024,31]{1,2,0:T(8,128)(2,1)S(1)} %slice.194), channel_id=1, source_target_pairs={{4,0},{8,4},{12,8},{16,12},{20,16},{24,20},{28,24},{32,28},{36,32}... | collective-permute-start | bytes 380936 | tf_op jit(solution)/shard_map/ppermute | solution.py:21
  68.8 3.0 %copy-start.5 = (bf16[2,8,2,8,1]{3,1,2,4,0:T(8,128)(2,1)S(1)}, bf16[2,8,2,8,1]{3,1,2,4,0:T(8,128)(2,1)}, u32[]{:S(2)}) copy-start(bf16[2,8,2,8,1]{3,1,2,4,0:T(8,128)(2,1)} %constant.68) | copy-start | bytes 1540
  71.3 0.9 %copy-start.3 = (f32[8,128]{0,1:T(8,128)S(1)}, f32[8,128]{0,1:T(8,128)}, u32[]{:S(2)}) copy-start(f32[8,128]{0,1:T(8,128)} %constant.65.clone) | copy-start | bytes 12292
  71.3 1.3 %copy-start.2 = (bf16[2,128,2,128,1]{3,1,2,4,0:T(8,128)(2,1)S(1)}, bf16[2,128,2,128,1]{3,1,2,4,0:T(8,128)(2,1)}, u32[]{:S(2)}) copy-start(bf16[2,128,2,128,1]{3,1,2,4,0:T(8,128)(2,1)} %constant.67) | copy-start | bytes 393220
  74.1 8.8 %all-to-all-start.1 = ((f32[4,64,128]{2,1,0:T(8,128)}), f32[4,64,128]{2,1,0:T(8,128)S(1)}, u32[]{:S(2)}, u32[]{:S(2)}) async-start(f32[4,64,128]{2,1,0:T(8,128)} %copy.59), calls=%async_computation.1 | async-start | bytes 262144 | tf_op jit(solution)/shard_map/all_to_all | solution.py:239

commit v15 on v12

--- a/solution.py
+++ b/solution.py
@@ -79,12 +79,10 @@
     fwd_tw, inv_tw = fwd_tw_ref[...], inv_tw_ref[...]
     taps = replica_ref[...].astype(jnp.float32)
     filled = taps.shape[1] // side
+    rows = pltpu.einshape("r(nb)->(rn)b", taps, b=side)
     blank = jnp.zeros((side - filled, side), jnp.float32)
-    pieces = []
-    for part in range(2):
-        pieces += [taps[part : part + 1, n * side : (n + 1) * side] for n in range(filled)]
-        pieces.append(blank)
-    replica = jnp.concatenate(pieces, axis=0).astype(jnp.bfloat16)
+    replica = jnp.concatenate([rows[:filled], blank, rows[filled:], blank], axis=0)
+    replica = replica.astype(jnp.bfloat16)
     rep_real, rep_imag = forward_transposed(replica, fwd, fwd_t, fwd_tw)
     rep_real = rep_real * 128.0
     rep_imag = rep_imag * 128.0

time: 83.7 us -> 83.7 us (level)
  no operation moved by 1% of the time
where the time goes in v15:
time: 83.7 us; the launch traced here: 83.3 us
  waiting for transfers between devices  34.8 us (42%)
  starting transfers between devices  27.8 us (33%)
  other arithmetic  8.22 us (10%)
  local copies, waits for them, and re-layouts  5.2 us (6%)
  Pallas kernels  3.4 us (4%)
  matrix products  2.84 us (3%)
  between operations  0.96 us (1%)
    all_to_all x1, waiting for transfers between devices, per_device(): lax.all_to_all(compressed, 'wide', split_axis=0, concat_axis=2, tiled=True)  27.8 us
    all_to_all x1, starting transfers between devices, per_device(): lax.all_to_all(compressed, 'wide', split_axis=0, concat_axis=2, tiled=True)  20.7 us
    all_to_all x1, starting transfers between devices, per_device(): lax.all_to_all(partial, 'narrow', split_axis=0, concat_axis=0, tiled=True)  4.01 us
    all_to_all x1, waiting for transfers between devices, per_device(): lax.all_to_all(partial, 'narrow', split_axis=0, concat_axis=0, tiled=True)  3.54 us
    ppermute x1, waiting for transfers between devices, passed_along(): return lax.ppermute(shard, axis, pairs)  3.48 us
    pallas_call x1, Pallas kernels, range_compress(): pl.pallas_call(range_kernel, in_specs=[whole] * 8, out_specs=whole, out_s...  3.4 us
    ppermute x1, starting transfers between devices, passed_along(): return lax.ppermute(shard, axis, pairs)  3.11 us
    convert_element_type x1, other arithmetic, per_device(): (moved_real * phase_cos - moved_imag * phase_sin).astype(jnp.bfloat16)  2.49 us
  transfers between devices with their start and end apart: 3, of which 3 were waited for; matrix products, arithmetic and copies ran while one was open for 8% of the time, Pallas kernels for 0%

profile of v15, /device:TPU:1, one launch (start us, length us, event | category | flops | bytes accessed | tf_op | source)
XLA Modules:
  0.0 83.3 jit_solution(3384730764755691634)
XLA Ops:
  0.0 0.0 copy-start.6
  0.0 0.0 copy-start
  0.0 0.0 copy-start.4
  0.0 3.4 %shard_map.190 = bf16[2048,128]{1,0:T(8,128)(2,1)} custom-call(bf16[2,1024,128]{2,1,0:T(8,128)(2,1)} %bitcast.109, bf16[2,4096]{1,0:T(2,128)(2,1)} %replica_ref.1, bf16[256,256]{1,0:T(8,128)(2,1)} %constant.55.clone.fwd_ref.inv_t_ref, bf16[256,256]{1,0:T(8,128)(2,1)} %constant.56.clone.fwd_t_ref.inv_ref, bf16[256,256]{1,0:T(8,128)(2,1)} %constant.56.clone.fwd_t_ref.inv_ref, ...), custom_call_target="tpu_custom_call" | custom-call | flops 603979776 | bytes 1048576 | tf_op jit(solution)/shard_map/pallas_call | solution.py:137
  3.4 0.0 copy-start.1
  3.4 20.7 %all-to-all-start = ((bf16[128,2,8,128]{3,2,1,0:T(8,128)(2,1)}), bf16[128,2,8,128]{3,2,1,0:T(8,128)(2,1)S(1)}, u32[]{:S(2)}, u32[]{:S(2)}) async-start(bf16[128,2,8,128]{3,2,1,0:T(8,128)(2,1)} %bitcast.100), calls=%async_computation | async-start | bytes 1048576 | tf_op jit(solution)/shard_map/all_to_all | solution.py:193
  24.1 0.7 iota_add_fusion
  24.8 1.2 %fusion.52 = (f32[1,1024]{1,0:T(1,128)S(1)}, f32[1,1024]{1,0:T(1,128)S(1)}, f32[1,1024]{1,0:T(1,128)S(1)}, f32[1,1024]{1,0:T(1,128)S(1)}, f32[1,1024]{1,0:T(1,12...) fusion(f32[8,1024]{1,0:T(8,128)} %param.22), kind=kLoop, calls=%fused_computation.108 | loop fusion | bytes 65536 | tf_op jit(solution)/shard_map/slice | solution.py:207
  26.1 0.8 broadcast_divide_fusion
  26.8 1.7 %divide_cosine_fusion = (f32[1,513,128]{2,1,0:T(8,128)S(1)}, f32[1,513,128]{2,1,0:T(8,128)S(1)}) fusion(f32[128]{0:T(128)} %param.24, f32[513]{0:T(1024)S(1)} %fusion.40), kind=kLoop, calls=%fused_computation.80 | loop fusion | flops 65664 | bytes 527876 | tf_op jit(solution)/shard_map/cos | solution.py:215
  28.5 1.0 %slice_cosine_fusion = (f32[511,128]{1,0:T(8,128)S(1)}, f32[511,128]{1,0:T(8,128)S(1)}) fusion(f32[513,128]{1,0:T(8,128)S(1)} %broadcast_divide_fusion), kind=kLoop, calls=%fused_computation.78 | loop fusion | bytes 784896 | tf_op jit(solution)/shard_map/cos | solution.py:215
  29.5 27.8 %all-to-all-done = bf16[128,2,8,128]{3,2,1,0:T(8,128)(2,1)S(1)} async-done(((bf16[128,2,8,128]{3,2,1,0:T(8,128)(2,1)}), bf16[128,2,8,128]{3,2,1,0:T(8,128)(2,1)S(1)}, u32[]{:S(2)}, u32[]{:S(2)}) %all-to-all-start) | async-done | bytes 524320 | tf_op jit(solution)/shard_map/all_to_all | solution.py:193
  57.4 0.0 copy-start.7
  57.4 0.0 copy-done.6
  57.4 0.4 convolution_bitcast_fusion.1
  57.8 0.0 copy-done
  57.8 0.0 copy-done.4
  57.8 0.4 subtract_convert_fusion.2
  58.2 0.1 maximum_bitcast_fusion
  58.3 0.0 copy-done.1
  58.3 0.3 fusion.1
  58.6 0.3 copy.100
  58.9 0.2 copy.66
  59.2 3.1 %collective-permute-start = (bf16[2,1024,31]{1,2,0:T(8,128)(2,1)S(1)}, bf16[2,1024,31]{1,2,0:T(8,128)(2,1)S(1)}, u32[]{:S(2)}, u32[]{:S(2)}) collective-permute-start(bf16[2,1024,31]{1,2,0:T(8,128)(2,1)S(1)} %slice.194), channel_id=1, source_target_pairs={{4,0},{8,4},{12,8},{16,12},{20,16},{24,20},{28,24},{32,28},{36,32}... | collective-permute-start | bytes 380936 | tf_op jit(solution)/shard_map/ppermute | solution.py:21
  62.3 0.0 copy-done.7
  62.3 0.3 rev.7
  62.7 0.3 rev.8
  63.0 0.1 convert_reduce_fusion
  63.1 3.5 %collective-permute-done = bf16[2,1024,31]{1,2,0:T(8,128)(2,1)S(1)} collective-permute-done((bf16[2,1024,31]{1,2,0:T(8,128)(2,1)S(1)}, bf16[2,1024,31]{1,2,0:T(8,128)(2,1)S(1)}, u32[]{:S(2)}, u32[]{:S(2)}) %collective-permute-start) | collective-permute-done | bytes 127008 | tf_op jit(solution)/shard_map/ppermute | solution.py:21
  66.6 1.3 %fusion.2 = bf16[2,1024,1024]{2,1,0:T(8,128)(2,1)S(1)} fusion(bf16[2,1024,31]{1,2,0:T(8,128)(2,1)S(1)} %collective-permute-done, bf16[2,1024,128]{1,2,0:T(8,128)(2,1)S(1)} %copy.66, s32[1024]{0:T(1024)S(1)} %add_bitcast_fusion), kind=kOutput, calls=%fused_computation.6 | convolution fusion | flops 668359680 | bytes 4849664 | tf_op jit(solution)/shard_map/xpc,cn->xpn/dot_general | solution.py:205
  67.9 0.8 slice_convert_fusion.7
  68.7 0.0 copy-start.5
  68.8 2.5 %subtract_convert_fusion.1 = (bf16[1,1024,128]{2,1,0:T(8,128)(2,1)S(1)}, f32[1,1024,128]{2,1,0:T(8,128)S(1)}, f32[1,1024,128]{2,1,0:T(8,128)S(1)}) fusion(f32[1,511,128]{2,1,0:T(8,128)S(1)} %bitcast.94, f32[1,513,128]{2,1,0:T(8,128)S(1)} %get-tuple-element.31, f32[1,511,128]{2,1,0:T(8,128)S(1)} %bitcast.92, f32[1,513,128]{2,1,0:T(8,128)S(1)} %get-tuple-element.30, ...), kind=kLoop, calls=%fused_computation.70 | loop fusion | flops 4718592 | bytes 10780672 | tf_op jit(solution)/shard_map/convert_element_type | solution.py:219
  71.3 0.0 copy-start.3
  71.3 0.0 copy-start.2
  71.3 0.1 add_convert_fusion.1
  71.4 0.2 copy.68
  71.6 0.2 copy.67
  71.8 0.0 copy-done.5
  71.8 0.3 convolution_bitcast_fusion
  72.2 0.0 copy-done.3
  72.2 0.4 subtract_convert_fusion
  72.5 0.1 pad_maximum_fusion.2
  72.6 0.0 copy-done.2
  72.6 0.3 convolution_bitcast_fusion.2
  72.9 0.1 fusion.32
  73.0 0.2 fusion.33
  73.1 0.6 copy.71
  73.8 4.0 %all-to-all-start.1 = ((f32[4,8,8,128]{3,2,1,0:T(8,128)}), f32[4,8,8,128]{3,2,1,0:T(8,128)S(1)}, u32[]{:S(2)}, u32[]{:S(2)}) async-start(f32[4,8,8,128]{3,2,1,0:T(8,128)} %copy.71), calls=%async_computation.1 | async-start | bytes 262144 | tf_op jit(solution)/shard_map/all_to_all | solution.py:239
  77.8 0.6 fusion.47
  79.1 3.5 %all-to-all-done.1 = f32[4,8,8,128]{3,2,1,0:T(8,128)S(1)} async-done(((f32[4,8,8,128]{3,2,1,0:T(8,128)}), f32[4,8,8,128]{3,2,1,0:T(8,128)S(1)}, u32[]{:S(2)}, u32[]{:S(2)}) %all-to-all-start.1) | async-done | bytes 131104 | tf_op jit(solution)/shard_map/all_to_all | solution.py:239
  82.7 0.6 copy.101
  (7 shorter events, 0.1 us)
Async XLA Ops:
  0.0 57.4 %copy-start.6 = (bf16[2,8,2,8,1]{3,1,2,4,0:T(8,128)(2,1)S(1)}, bf16[2,8,2,8,1]{3,1,2,4,0:T(8,128)(2,1)}, u32[]{:S(2)}) copy-start(bf16[2,8,2,8,1]{3,1,2,4,0:T(8,128)(2,1)} %constant.69) | copy-start | bytes 1540
  0.0 57.8 %copy-start = (f32[8,128]{0,1:T(8,128)S(1)}, f32[8,128]{0,1:T(8,128)}, u32[]{:S(2)}) copy-start(f32[8,128]{0,1:T(8,128)} %constant.61.clone) | copy-start | bytes 12292
  0.0 57.8 %copy-start.4 = (f32[8,128]{0,1:T(8,128)S(1)}, f32[8,128]{0,1:T(8,128)}, u32[]{:S(2)}) copy-start(f32[8,128]{0,1:T(8,128)} %constant.62.clone) | copy-start | bytes 12292
  3.4 54.8 %copy-start.1 = (bf16[2,128,2,128,1]{3,1,2,0,4:T(8,128)(2,1)S(1)}, bf16[2,128,2,128,1]{3,1,2,0,4:T(8,128)(2,1)}, u32[]{:S(2)}) copy-start(bf16[2,128,2,128,1]{3,1,2,0,4:T(8,128)(2,1)} %constant.70) | copy-start | bytes 393220
  3.4 53.9 %all-to-all-start = ((bf16[128,2,8,128]{3,2,1,0:T(8,128)(2,1)}), bf16[128,2,8,128]{3,2,1,0:T(8,128)(2,1)S(1)}, u32[]{:S(2)}, u32[]{:S(2)}) async-start(bf16[128,2,8,128]{3,2,1,0:T(8,128)(2,1)} %bitcast.100), calls=%async_computation | async-start | bytes 1048576 | tf_op jit(solution)/shard_map/all_to_all | solution.py:193
  57.4 4.9 %copy-start.7 = (s32[4,16]{1,0:T(4,128)S(1)}, s32[4,16]{1,0:T(4,128)}, u32[]{:S(2)}) copy-start(s32[4,16]{1,0:T(4,128)} %param.25) | copy-start | bytes 772
  59.2 7.4 %collective-permute-start = (bf16[2,1024,31]{1,2,0:T(8,128)(2,1)S(1)}, bf16[2,1024,31]{1,2,0:T(8,128)(2,1)S(1)}, u32[]{:S(2)}, u32[]{:S(2)}) collective-permute-start(bf16[2,1024,31]{1,2,0:T(8,128)(2,1)S(1)} %slice.194), channel_id=1, source_target_pairs={{4,0},{8,4},{12,8},{16,12},{20,16},{24,20},{28,24},{32,28},{36,32}... | collective-permute-start | bytes 380936 | tf_op jit(solution)/shard_map/ppermute | solution.py:21
  68.7 3.0 %copy-start.5 = (bf16[2,8,2,8,1]{3,1,2,4,0:T(8,128)(2,1)S(1)}, bf16[2,8,2,8,1]{3,1,2,4,0:T(8,128)(2,1)}, u32[]{:S(2)}) copy-start(bf16[2,8,2,8,1]{3,1,2,4,0:T(8,128)(2,1)} %constant.68) | copy-start | bytes 1540
  71.3 0.9 %copy-start.3 = (f32[8,128]{0,1:T(8,128)S(1)}, f32[8,128]{0,1:T(8,128)}, u32[]{:S(2)}) copy-start(f32[8,128]{0,1:T(8,128)} %constant.65.clone) | copy-start | bytes 12292
  71.3 1.3 %copy-start.2 = (bf16[2,128,2,128,1]{3,1,2,4,0:T(8,128)(2,1)S(1)}, bf16[2,128,2,128,1]{3,1,2,4,0:T(8,128)(2,1)}, u32[]{:S(2)}) copy-start(bf16[2,128,2,128,1]{3,1,2,4,0:T(8,128)(2,1)} %constant.67) | copy-start | bytes 393220
  73.8 8.8 %all-to-all-start.1 = ((f32[4,8,8,128]{3,2,1,0:T(8,128)}), f32[4,8,8,128]{3,2,1,0:T(8,128)S(1)}, u32[]{:S(2)}, u32[]{:S(2)}) async-start(f32[4,8,8,128]{3,2,1,0:T(8,128)} %copy.71), calls=%async_computation.1 | async-start | bytes 262144 | tf_op jit(solution)/shard_map/all_to_all | solution.py:239

commit v16 on v14

--- a/solution.py
+++ b/solution.py
@@ -234,10 +234,10 @@
         (tile_owner[:, :, None] == tile_ids[None, None, :]).astype(jnp.int32), axis=(0, 1)
     )
     own_count = jnp.sum(jnp.where(tile_ids == group, counts, 0)).astype(jnp.float32)
-    partial = jnp.dot(member, blocks, preferred_element_type=jnp.float32)
-    partial = partial.reshape(tiles, block_rows, width)
+    spaced = jnp.stack([member, jnp.zeros_like(member)], axis=1).reshape(2 * tiles, block_count)
+    partial = jnp.dot(spaced, blocks, preferred_element_type=jnp.float32)
     incoming = lax.all_to_all(partial, "narrow", split_axis=0, concat_axis=0, tiled=True)
-    summed = jnp.sum(incoming, axis=0)[None]
+    summed = jnp.sum(incoming, axis=0).reshape(1, block_rows, width)
     return summed / own_count
 
 

time: 84 us -> 84.8 us (level)
  waiting for transfers between devices: 34.8 us -> 38 us
  local copies, waits for them, and re-layouts: 4.87 us -> 3.02 us
  other arithmetic: 8.84 us -> 7.7 us
    all_to_all x1, waiting for transfers between devices: 27.8 us -> 29.5 us  [per_device(): lax.all_to_all(compressed, 'wide', split_axis=0, concat_axis=2, tiled=True)]
    slice x1, local copies, waits for them, and re-layouts: 1.25 us -> 0.03 us  [per_device(): weight = interp_weight[tap_index][:, None]]
  transfers between devices with their start and end apart: 3 -> 3, of which waited for: 3 -> 3; matrix products, arithmetic and copies ran while one was open for 8% -> 5% of each run, Pallas kernels for 0% -> 0%
where the time goes in v16:
time: 84.8 us; the launch traced here: 84.4 us
  waiting for transfers between devices  38 us (45%)
  starting transfers between devices  27.7 us (33%)
  other arithmetic  7.7 us (9%)
  matrix products  3.58 us (4%)
  Pallas kernels  3.45 us (4%)
  local copies, waits for them, and re-layouts  3.02 us (4%)
  between operations  1.04 us (1%)
    all_to_all x1, waiting for transfers between devices, per_device(): lax.all_to_all(compressed, 'wide', split_axis=0, concat_axis=2, tiled=True)  29.5 us
    all_to_all x1, starting transfers between devices, per_device(): lax.all_to_all(compressed, 'wide', split_axis=0, concat_axis=2, tiled=True)  20.6 us
    ppermute x1, waiting for transfers between devices, passed_along(): return lax.ppermute(shard, axis, pairs)  4.31 us
    all_to_all x1, waiting for transfers between devices, per_device(): lax.all_to_all(partial, 'narrow', split_axis=0, concat_axis=0, tiled=True)  4.12 us
    all_to_all x1, starting transfers between devices, per_device(): lax.all_to_all(partial, 'narrow', split_axis=0, concat_axis=0, tiled=True)  4.01 us
    pallas_call x1, Pallas kernels, range_compress(): pl.pallas_call(range_kernel, in_specs=[whole] * 8, out_specs=whole, out_s...  3.45 us
    ppermute x1, starting transfers between devices, passed_along(): return lax.ppermute(shard, axis, pairs)  3.11 us
    convert_element_type x1, other arithmetic, per_device(): (moved_real * phase_cos - moved_imag * phase_sin).astype(jnp.bfloat16)  2.49 us
  transfers between devices with their start and end apart: 3, of which 3 were waited for; matrix products, arithmetic and copies ran while one was open for 5% of the time, Pallas kernels for 0%

profile of v16, /device:TPU:1, one launch (start us, length us, event | category | flops | bytes accessed | tf_op | source)
XLA Modules:
  0.0 84.4 jit_solution(16702577671995084567)
XLA Ops:
  0.0 0.0 copy-start.7
  0.0 0.0 copy-start.8
  0.0 0.0 copy-start.9
  0.0 0.0 copy-start.10
  0.0 0.0 copy-start.5
  0.0 0.0 copy-start
  0.0 0.0 copy-start.4
  0.1 3.5 %shard_map.190 = bf16[2048,128]{1,0:T(8,128)(2,1)} custom-call(bf16[2,1024,128]{2,1,0:T(8,128)(2,1)} %bitcast.98, bf16[2,4096]{1,0:T(2,128)(2,1)} %replica_ref.1, bf16[256,256]{1,0:T(8,128)(2,1)} %constant.58.clone.fwd_ref.inv_t_ref, bf16[256,256]{1,0:T(8,128)(2,1)} %constant.59.clone.fwd_t_ref.inv_ref, bf16[256,256]{1,0:T(8,128)(2,1)} %constant.59.clone.fwd_t_ref.inv_ref, ...), custom_call_target="tpu_custom_call" | custom-call | flops 603979776 | bytes 1048576 | tf_op jit(solution)/shard_map/pallas_call | solution.py:139
  3.5 20.6 %all-to-all-start = ((bf16[128,2,8,128]{3,2,1,0:T(8,128)(2,1)}), bf16[128,2,8,128]{3,2,1,0:T(8,128)(2,1)S(1)}, u32[]{:S(2)}, u32[]{:S(2)}) async-start(bf16[128,2,8,128]{3,2,1,0:T(8,128)(2,1)} %bitcast.89), calls=%async_computation | async-start | bytes 1048576 | tf_op jit(solution)/shard_map/all_to_all | solution.py:195
  24.1 0.0 copy-start.1
  24.1 0.8 broadcast_divide_fusion
  24.9 1.0 %slice_cosine_fusion = (f32[511,128]{1,0:T(8,128)S(1)}, f32[511,128]{1,0:T(8,128)S(1)}) fusion(f32[513,128]{1,0:T(8,128)S(1)} %broadcast_divide_fusion), kind=kLoop, calls=%fused_computation.75 | loop fusion | bytes 784896 | tf_op jit(solution)/shard_map/cos | solution.py:217
  25.9 0.3 rev.7
  26.3 0.3 rev.8
  26.6 0.0 copy-done.9
  26.7 0.0 copy-done.10
  26.7 0.0 copy-done.5
  26.7 0.0 copy-done.8
  26.8 1.0 %divide_cosine_fusion = (f32[1,513,128]{2,1,0:T(8,128)S(1)}, f32[1,513,128]{2,1,0:T(8,128)S(1)}) fusion(f32[128]{0:T(128)S(1)} %copy-done.8, f32[513]{0:T(1024)S(1)} %fusion.39), kind=kLoop, calls=%fused_computation.77 | loop fusion | flops 65664 | bytes 527876 | tf_op jit(solution)/shard_map/cos | solution.py:217
  27.8 29.5 %all-to-all-done = bf16[128,2,8,128]{3,2,1,0:T(8,128)(2,1)S(1)} async-done(((bf16[128,2,8,128]{3,2,1,0:T(8,128)(2,1)}), bf16[128,2,8,128]{3,2,1,0:T(8,128)(2,1)S(1)}, u32[]{:S(2)}, u32[]{:S(2)}) %all-to-all-start) | async-done | bytes 524320 | tf_op jit(solution)/shard_map/all_to_all | solution.py:195
  57.3 0.0 copy-done.7
  57.3 0.4 convolution_bitcast_fusion.1
  57.8 0.0 copy-done
  57.8 0.0 copy-done.4
  57.8 0.4 subtract_convert_fusion.2
  58.1 0.1 maximum_bitcast_fusion
  58.2 0.0 copy-done.1
  58.2 0.3 fusion.1
  58.5 0.3 copy.81
  58.9 0.2 copy.51
  59.1 3.1 %collective-permute-start = (bf16[2,1024,31]{1,2,0:T(8,128)(2,1)S(1)}, bf16[2,1024,31]{1,2,0:T(8,128)(2,1)S(1)}, u32[]{:S(2)}, u32[]{:S(2)}) collective-permute-start(bf16[2,1024,31]{1,2,0:T(8,128)(2,1)S(1)} %slice.194), channel_id=1, source_target_pairs={{4,0},{8,4},{12,8},{16,12},{20,16},{24,20},{28,24},{32,28},{36,32}... | collective-permute-start | bytes 380936 | tf_op jit(solution)/shard_map/ppermute | solution.py:21
  62.2 4.3 %collective-permute-done = bf16[2,1024,31]{1,2,0:T(8,128)(2,1)S(1)} collective-permute-done((bf16[2,1024,31]{1,2,0:T(8,128)(2,1)S(1)}, bf16[2,1024,31]{1,2,0:T(8,128)(2,1)S(1)}, u32[]{:S(2)}, u32[]{:S(2)}) %collective-permute-start) | collective-permute-done | bytes 127008 | tf_op jit(solution)/shard_map/ppermute | solution.py:21
  66.6 1.3 %fusion.2 = bf16[2,1024,1024]{2,1,0:T(8,128)(2,1)S(1)} fusion(bf16[2,1024,31]{1,2,0:T(8,128)(2,1)S(1)} %collective-permute-done, bf16[2,1024,128]{1,2,0:T(8,128)(2,1)S(1)} %copy.51, s32[1024]{0:T(1024)S(1)} %add_bitcast_fusion), kind=kOutput, calls=%fused_computation.6 | convolution fusion | flops 668359680 | bytes 4849664 | tf_op jit(solution)/shard_map/xpc,cn->xpn/dot_general | solution.py:207
  67.9 0.8 slice_convert_fusion.7
  68.7 0.0 copy-start.6
  68.7 2.5 %subtract_convert_fusion.1 = (bf16[1,1024,128]{2,1,0:T(8,128)(2,1)S(1)}, f32[1,1024,128]{2,1,0:T(8,128)S(1)}, f32[1,1024,128]{2,1,0:T(8,128)S(1)}) fusion(f32[1,511,128]{2,1,0:T(8,128)S(1)} %bitcast.83, f32[1,513,128]{2,1,0:T(8,128)S(1)} %get-tuple-element.31, f32[1,511,128]{2,1,0:T(8,128)S(1)} %bitcast.81, f32[1,513,128]{2,1,0:T(8,128)S(1)} %get-tuple-element.30, ...), kind=kLoop, calls=%fused_computation.70 | loop fusion | flops 4718592 | bytes 10780672 | tf_op jit(solution)/shard_map/convert_element_type | solution.py:221
  71.2 0.0 copy-start.3
  71.2 0.0 copy-start.2
  71.2 0.2 add_convert_fusion.1
  71.4 0.2 copy.53
  71.6 0.2 copy.52
  71.8 0.0 copy-done.6
  71.8 0.3 convolution_bitcast_fusion
  72.1 0.0 copy-done.3
  72.1 0.4 subtract_convert_fusion
  72.5 0.1 pad_maximum_fusion.2
  72.5 0.0 copy-done.2
  72.6 0.3 convolution_bitcast_fusion.2
  72.9 0.1 fusion.9
  72.9 0.2 copy.55
  73.1 0.1 reshape.402
  73.2 0.9 %fusion.32 = f32[4,2,8192]{2,1,0:T(2,128)} fusion(bf16[16,8192,1]{1,0,2:T(8,128)(2,1)S(1)} %reshape.402, pred[4,1,16]{2,1,0:T(4,128)(4,1)S(1)} %copy.69), kind=kOutput, calls=%fused_computation.82 | convolution fusion | flops 2097152 | bytes 524352 | tf_op jit(solution)/shard_map/dot_general | solution.py:238
  74.2 4.0 %all-to-all-start.1 = ((f32[4,2,8192]{2,1,0:T(2,128)}), f32[4,2,8192]{2,1,0:T(2,128)S(1)}, u32[]{:S(2)}, u32[]{:S(2)}) async-start(f32[4,2,8192]{2,1,0:T(2,128)} %fusion.32), calls=%async_computation.1 | async-start | bytes 524288 | tf_op jit(solution)/shard_map/all_to_all | solution.py:239
  78.2 0.1 convert_reduce_fusion
  78.3 0.6 fusion.43
  79.6 4.1 %all-to-all-done.1 = f32[4,2,8192]{2,1,0:T(2,128)S(1)} async-done(((f32[4,2,8192]{2,1,0:T(2,128)}), f32[4,2,8192]{2,1,0:T(2,128)S(1)}, u32[]{:S(2)}, u32[]{:S(2)}) %all-to-all-start.1) | async-done | bytes 262176 | tf_op jit(solution)/shard_map/all_to_all | solution.py:239
  83.7 0.1 reduce_sum.27
  83.8 0.6 divide_bitcast_fusion
  (9 shorter events, 0.1 us)
Async XLA Ops:
  0.0 57.3 %copy-start.7 = (bf16[2,8,2,8,1]{3,1,2,4,0:T(8,128)(2,1)S(1)}, bf16[2,8,2,8,1]{3,1,2,4,0:T(8,128)(2,1)}, u32[]{:S(2)}) copy-start(bf16[2,8,2,8,1]{3,1,2,4,0:T(8,128)(2,1)} %constant.74) | copy-start | bytes 1540
  0.0 26.7 %copy-start.8 = (f32[128]{0:T(128)S(1)}, f32[128]{0:T(128)}, u32[]{:S(2)}) copy-start(f32[128]{0:T(128)} %param.24) | copy-start | bytes 1540
  0.0 26.6 %copy-start.9 = (s32[4,16]{1,0:T(4,128)S(1)}, s32[4,16]{1,0:T(4,128)}, u32[]{:S(2)}) copy-start(s32[4,16]{1,0:T(4,128)} %param.25) | copy-start | bytes 772
  0.0 26.7 %copy-start.10 = (s32[128]{0:T(128)S(1)}, s32[128]{0:T(128)}, u32[]{:S(2)}) copy-start(s32[128]{0:T(128)} %param.23) | copy-start | bytes 1540
  0.0 26.7 %copy-start.5 = (f32[8,1024]{1,0:T(8,128)S(1)}, f32[8,1024]{1,0:T(8,128)}, u32[]{:S(2)}) copy-start(f32[8,1024]{1,0:T(8,128)} %param.22) | copy-start | bytes 98308
  0.0 57.7 %copy-start = (f32[8,128]{0,1:T(8,128)S(1)}, f32[8,128]{0,1:T(8,128)}, u32[]{:S(2)}) copy-start(f32[8,128]{0,1:T(8,128)} %constant.64.clone) | copy-start | bytes 12292
  0.0 57.7 %copy-start.4 = (f32[8,128]{0,1:T(8,128)S(1)}, f32[8,128]{0,1:T(8,128)}, u32[]{:S(2)}) copy-start(f32[8,128]{0,1:T(8,128)} %constant.65.clone) | copy-start | bytes 12292
  3.5 53.8 %all-to-all-start = ((bf16[128,2,8,128]{3,2,1,0:T(8,128)(2,1)}), bf16[128,2,8,128]{3,2,1,0:T(8,128)(2,1)S(1)}, u32[]{:S(2)}, u32[]{:S(2)}) async-start(bf16[128,2,8,128]{3,2,1,0:T(8,128)(2,1)} %bitcast.89), calls=%async_computation | async-start | bytes 1048576 | tf_op jit(solution)/shard_map/all_to_all | solution.py:195
  24.1 34.1 %copy-start.1 = (bf16[2,128,2,128,1]{3,1,2,0,4:T(8,128)(2,1)S(1)}, bf16[2,128,2,128,1]{3,1,2,0,4:T(8,128)(2,1)}, u32[]{:S(2)}) copy-start(bf16[2,128,2,128,1]{3,1,2,0,4:T(8,128)(2,1)} %constant.75) | copy-start | bytes 393220
  59.1 7.4 %collective-permute-start = (bf16[2,1024,31]{1,2,0:T(8,128)(2,1)S(1)}, bf16[2,1024,31]{1,2,0:T(8,128)(2,1)S(1)}, u32[]{:S(2)}, u32[]{:S(2)}) collective-permute-start(bf16[2,1024,31]{1,2,0:T(8,128)(2,1)S(1)} %slice.194), channel_id=1, source_target_pairs={{4,0},{8,4},{12,8},{16,12},{20,16},{24,20},{28,24},{32,28},{36,32}... | collective-permute-start | bytes 380936 | tf_op jit(solution)/shard_map/ppermute | solution.py:21
  68.7 3.1 %copy-start.6 = (bf16[2,8,2,8,1]{3,1,2,4,0:T(8,128)(2,1)S(1)}, bf16[2,8,2,8,1]{3,1,2,4,0:T(8,128)(2,1)}, u32[]{:S(2)}) copy-start(bf16[2,8,2,8,1]{3,1,2,4,0:T(8,128)(2,1)} %constant.73) | copy-start | bytes 1540
  71.2 0.9 %copy-start.3 = (f32[8,128]{0,1:T(8,128)S(1)}, f32[8,128]{0,1:T(8,128)}, u32[]{:S(2)}) copy-start(f32[8,128]{0,1:T(8,128)} %constant.68.clone) | copy-start | bytes 12292
  71.2 1.3 %copy-start.2 = (bf16[2,128,2,128,1]{3,1,2,4,0:T(8,128)(2,1)S(1)}, bf16[2,128,2,128,1]{3,1,2,4,0:T(8,128)(2,1)}, u32[]{:S(2)}) copy-start(bf16[2,128,2,128,1]{3,1,2,4,0:T(8,128)(2,1)} %constant.72) | copy-start | bytes 393220
  74.2 9.5 %all-to-all-start.1 = ((f32[4,2,8192]{2,1,0:T(2,128)}), f32[4,2,8192]{2,1,0:T(2,128)S(1)}, u32[]{:S(2)}, u32[]{:S(2)}) async-start(f32[4,2,8192]{2,1,0:T(2,128)} %fusion.32), calls=%async_computation.1 | async-start | bytes 524288 | tf_op jit(solution)/shard_map/all_to_all | solution.py:239

commit v17 on v12

--- a/solution.py
+++ b/solution.py
@@ -13,6 +13,7 @@
 PUL_DEV = 8
 CAP = 8
 HALO = 31
+WIDE = ("y", "z", "c")
 
 
 def passed_along(shard, axis, by):
@@ -189,12 +190,18 @@
     echo = raw_echo[:, 0]
     length = echo.shape[2]
     compressed = range_compress(echo, range_replica)
-    devices = lax.axis_size("wide")
+    devices = lax.axis_size(WIDE)
     width = length // devices
     assert compressed.shape[0] == devices and compressed.shape[3] == width
-    turned = lax.all_to_all(compressed, "wide", split_axis=0, concat_axis=2, tiled=True)[0]
+    ys, zs, cores = lax.axis_size("y"), lax.axis_size("z"), lax.axis_size("c")
+    chunked = compressed.reshape(ys, zs, cores, 2, compressed.shape[2], width).transpose(2, 0, 1, 3, 4, 5)
+    turned = lax.all_to_all(
+        chunked.reshape(compressed.shape), ("c", "y", "z"), split_axis=0, concat_axis=2, tiled=True
+    )[0]
+    turned = turned.reshape(2, cores, ys, zs, -1, width).transpose(0, 2, 3, 1, 4, 5)
+    turned = turned.reshape(2, -1, width)
     doppler = pulse_transform(turned, PUL_DEV, -1).astype(jnp.bfloat16)
-    rim = passed_along(doppler[:, :, :HALO], "wide", -1)
+    rim = passed_along(doppler[:, :, :HALO], WIDE, -1)
     extended = jnp.concatenate([doppler, rim], axis=2)
     pulses = extended.shape[1]
     columns = jnp.arange(width + HALO, dtype=jnp.int32)
@@ -244,10 +251,13 @@
 
 
 def solution(mesh):
+    wide, narrow = mesh.devices.shape
+    parts = mesh.devices.reshape(4, wide // 8, 2, narrow)
+    split = jax.sharding.Mesh(parts, ("y", "z", "c", "narrow"))
     return jax.shard_map(
         per_device,
-        mesh=mesh,
-        in_specs=(P(None, "narrow", "wide", None), P(), P(), P("wide"), P("wide"), P()),
-        out_specs=P("narrow", None, "wide"),
+        mesh=split,
+        in_specs=(P(None, "narrow", WIDE, None), P(), P(), P(WIDE), P(WIDE), P()),
+        out_specs=P("narrow", None, WIDE),
         check_vma=False,
     )

time: 83.7 us -> 83.8 us (level)
  other arithmetic: 8.22 us -> 6.25 us
    another operation x0 -> x2, local copies, waits for them, and re-layouts: none -> 1.97 us  [the longest x1 1.88 us: per_device(): compressed.reshape(ys, zs, cores, 2, compressed.shape[2], width)]
    slice x1, local copies, waits for them, and re-layouts: 1.25 us -> 0.03 us  [per_device(): weight = interp_weight[tap_index][:, None]]
  transfers between devices with their start and end apart: 3 -> 3, of which waited for: 3 -> 3; matrix products, arithmetic and copies ran while one was open for 8% -> 4% of each run, Pallas kernels for 0% -> 0%
where the time goes in v17:
time: 83.8 us; the launch traced here: 83.4 us
  waiting for transfers between devices  35.4 us (42%)
  starting transfers between devices  28.6 us (34%)
  other arithmetic  6.25 us (7%)
  local copies, waits for them, and re-layouts  5.94 us (7%)
  Pallas kernels  3.45 us (4%)
  matrix products  2.83 us (3%)
  between operations  1.03 us (1%)
    all_to_all x1, waiting for transfers between devices, per_device(): lax.all_to_all(chunked.reshape(compressed.shape), ('c', 'y', 'z'), split_...  28.1 us
    all_to_all x1, starting transfers between devices, per_device(): lax.all_to_all(chunked.reshape(compressed.shape), ('c', 'y', 'z'), split_...  21 us
    all_to_all x1, starting transfers between devices, per_device(): lax.all_to_all(partial, 'narrow', split_axis=0, concat_axis=0, tiled=True)  4.02 us
    ppermute x1, waiting for transfers between devices, passed_along(): return lax.ppermute(shard, axis, pairs)  3.72 us
    all_to_all x1, waiting for transfers between devices, per_device(): lax.all_to_all(partial, 'narrow', split_axis=0, concat_axis=0, tiled=True)  3.54 us
    ppermute x1, starting transfers between devices, passed_along(): return lax.ppermute(shard, axis, pairs)  3.53 us
    pallas_call x1, Pallas kernels, range_compress(): pl.pallas_call(range_kernel, in_specs=[whole] * 8, out_specs=whole, out_s...  3.45 us
    convert_element_type x1, other arithmetic, per_device(): (moved_real * phase_cos - moved_imag * phase_sin).astype(jnp.bfloat16)  2.49 us
  transfers between devices with their start and end apart: 3, of which 3 were waited for; matrix products, arithmetic and copies ran while one was open for 4% of the time, Pallas kernels for 0%

profile of v17, /device:TPU:1, one launch (start us, length us, event | category | flops | bytes accessed | tf_op | source)
XLA Modules:
  0.0 83.4 jit_solution(8243610920861470977)
XLA Ops:
  0.0 0.0 copy-start.7
  0.0 0.0 copy-start.10
  0.0 0.0 copy-start.5
  0.0 0.0 copy-start.8
  0.0 0.0 copy-start
  0.0 0.0 copy-start.4
  0.0 3.4 %shard_map.190 = bf16[2048,128]{1,0:T(8,128)(2,1)} custom-call(bf16[2,1024,128]{2,1,0:T(8,128)(2,1)} %bitcast.116, bf16[2,4096]{1,0:T(2,128)(2,1)} %replica_ref.1, bf16[256,256]{1,0:T(8,128)(2,1)} %constant.55.clone.fwd_ref.inv_t_ref, bf16[256,256]{1,0:T(8,128)(2,1)} %constant.56.clone.fwd_t_ref.inv_ref, bf16[256,256]{1,0:T(8,128)(2,1)} %constant.56.clone.fwd_t_ref.inv_ref, ...), custom_call_target="tpu_custom_call" | custom-call | flops 603979776 | bytes 1048576 | tf_op jit(solution)/shard_map/pallas_call | solution.py:140
  3.5 1.9 %copy.64 = bf16[4,16,2,2,8,128]{5,4,3,1,0,2:T(8,128)(2,1)} copy(bf16[4,16,2,2,8,128]{5,4,3,2,1,0:T(8,128)(2,1)} %bitcast.107) | data formatting | bytes 1048576 | tf_op jit(solution)/shard_map/reshape;reshape | solution.py:197
  5.4 0.0 copy-start.1
  5.4 21.0 %all-to-all-start = ((bf16[128,2,8,128]{3,2,1,0:T(8,128)(2,1)}), bf16[128,2,8,128]{3,2,1,0:T(8,128)(2,1)S(1)}, u32[]{:S(2)}, u32[]{:S(2)}) async-start(bf16[128,2,8,128]{3,2,1,0:T(8,128)(2,1)} %bitcast.15), calls=%async_computation | async-start | bytes 1048576 | tf_op jit(solution)/shard_map/all_to_all | solution.py:198
  26.4 0.0 copy-done.10
  26.4 0.0 copy-done.5
  26.5 0.0 copy-done.8
  26.5 0.1 broadcast_divide_fusion
  26.6 1.0 %divide_cosine_fusion = (f32[1,513,128]{2,1,0:T(8,128)S(1)}, f32[1,513,128]{2,1,0:T(8,128)S(1)}) fusion(f32[128]{0:T(128)S(1)} %copy-done.8, f32[513]{0:T(1024)S(1)} %fusion.40), kind=kLoop, calls=%fused_computation.80 | loop fusion | flops 65664 | bytes 527876 | tf_op jit(solution)/shard_map/cos | solution.py:224
  27.6 1.0 %slice_cosine_fusion = (f32[511,128]{1,0:T(8,128)S(1)}, f32[511,128]{1,0:T(8,128)S(1)}) fusion(f32[513,128]{1,0:T(8,128)S(1)} %broadcast_divide_fusion), kind=kLoop, calls=%fused_computation.78 | loop fusion | bytes 784896 | tf_op jit(solution)/shard_map/cos | solution.py:224
  28.6 28.1 %all-to-all-done = bf16[128,2,8,128]{3,2,1,0:T(8,128)(2,1)S(1)} async-done(((bf16[128,2,8,128]{3,2,1,0:T(8,128)(2,1)}), bf16[128,2,8,128]{3,2,1,0:T(8,128)(2,1)S(1)}, u32[]{:S(2)}, u32[]{:S(2)}) %all-to-all-start) | async-done | bytes 524320 | tf_op jit(solution)/shard_map/all_to_all | solution.py:198
  56.8 0.1 copy.65
  56.9 0.0 copy-start.9
  56.9 0.0 copy-done.7
  56.9 0.4 convolution_bitcast_fusion.1
  57.3 0.0 copy-done
  57.3 0.0 copy-done.4
  57.3 0.4 subtract_convert_fusion.2
  57.7 0.1 maximum_bitcast_fusion
  57.7 0.0 copy-done.1
  57.8 0.3 fusion.1
  58.1 0.3 copy.104
  58.4 0.2 copy.70
  58.7 3.5 %collective-permute-start = (bf16[2,1024,31]{1,2,0:T(8,128)(2,1)S(1)}, bf16[2,1024,31]{1,2,0:T(8,128)(2,1)S(1)}, u32[]{:S(2)}, u32[]{:S(2)}) collective-permute-start(bf16[2,1024,31]{1,2,0:T(8,128)(2,1)S(1)} %slice.194), channel_id=1, source_target_pairs={{4,0},{8,4},{12,8},{16,12},{20,16},{24,20},{28,24},{32,28},{36,32}... | collective-permute-start | bytes 380936 | tf_op jit(solution)/shard_map/ppermute | solution.py:22
  62.2 0.0 copy-done.9
  62.2 0.3 rev.7
  62.6 0.3 rev.8
  62.9 0.1 convert_reduce_fusion
  63.0 3.7 %collective-permute-done = bf16[2,1024,31]{1,2,0:T(8,128)(2,1)S(1)} collective-permute-done((bf16[2,1024,31]{1,2,0:T(8,128)(2,1)S(1)}, bf16[2,1024,31]{1,2,0:T(8,128)(2,1)S(1)}, u32[]{:S(2)}, u32[]{:S(2)}) %collective-permute-start) | collective-permute-done | bytes 127008 | tf_op jit(solution)/shard_map/ppermute | solution.py:22
  66.8 1.3 %fusion.2 = bf16[2,1024,1024]{2,1,0:T(8,128)(2,1)S(1)} fusion(bf16[2,1024,31]{1,2,0:T(8,128)(2,1)S(1)} %collective-permute-done, bf16[2,1024,128]{1,2,0:T(8,128)(2,1)S(1)} %copy.70, s32[1024]{0:T(1024)S(1)} %add_bitcast_fusion), kind=kOutput, calls=%fused_computation.6 | convolution fusion | flops 668359680 | bytes 4849664 | tf_op jit(solution)/shard_map/xpc,cn->xpn/dot_general | solution.py:214
  68.1 0.8 slice_convert_fusion.7
  68.9 0.0 copy-start.6
  68.9 2.5 %subtract_convert_fusion.1 = (bf16[1,1024,128]{2,1,0:T(8,128)(2,1)S(1)}, f32[1,1024,128]{2,1,0:T(8,128)S(1)}, f32[1,1024,128]{2,1,0:T(8,128)S(1)}) fusion(f32[1,511,128]{2,1,0:T(8,128)S(1)} %bitcast.100, f32[1,513,128]{2,1,0:T(8,128)S(1)} %get-tuple-element.31, f32[1,511,128]{2,1,0:T(8,128)S(1)} %bitcast.98, f32[1,513,128]{2,1,0:T(8,128)S(1)} %get-tuple-element.30, ...), kind=kLoop, calls=%fused_computation.70 | loop fusion | flops 4718592 | bytes 10780672 | tf_op jit(solution)/shard_map/convert_element_type | solution.py:228
  71.4 0.0 copy-start.3
  71.4 0.0 copy-start.2
  71.4 0.1 add_convert_fusion.1
  71.6 0.2 copy.72
  71.8 0.2 copy.71
  71.9 0.0 copy-done.6
  71.9 0.3 convolution_bitcast_fusion
  72.3 0.0 copy-done.3
  72.3 0.4 subtract_convert_fusion
  72.7 0.1 pad_maximum_fusion.2
  72.7 0.0 copy-done.2
  72.7 0.3 convolution_bitcast_fusion.2
  73.0 0.1 fusion.32
  73.1 0.2 fusion.33
  73.3 0.7 copy.75
  73.9 4.0 %all-to-all-start.1 = ((f32[4,8,8,128]{3,2,1,0:T(8,128)}), f32[4,8,8,128]{3,2,1,0:T(8,128)S(1)}, u32[]{:S(2)}, u32[]{:S(2)}) async-start(f32[4,8,8,128]{3,2,1,0:T(8,128)} %copy.75), calls=%async_computation.1 | async-start | bytes 262144 | tf_op jit(solution)/shard_map/all_to_all | solution.py:248
  78.0 0.6 fusion.47
  79.2 3.5 %all-to-all-done.1 = f32[4,8,8,128]{3,2,1,0:T(8,128)S(1)} async-done(((f32[4,8,8,128]{3,2,1,0:T(8,128)}), f32[4,8,8,128]{3,2,1,0:T(8,128)S(1)}, u32[]{:S(2)}, u32[]{:S(2)}) %all-to-all-start.1) | async-done | bytes 131104 | tf_op jit(solution)/shard_map/all_to_all | solution.py:248
  82.8 0.6 copy.105
  (8 shorter events, 0.1 us)
Async XLA Ops:
  0.0 56.9 %copy-start.7 = (bf16[2,8,2,8,1]{3,1,2,4,0:T(8,128)(2,1)S(1)}, bf16[2,8,2,8,1]{3,1,2,4,0:T(8,128)(2,1)}, u32[]{:S(2)}) copy-start(bf16[2,8,2,8,1]{3,1,2,4,0:T(8,128)(2,1)} %constant.69) | copy-start | bytes 1540
  0.0 26.4 %copy-start.10 = (s32[128]{0:T(128)S(1)}, s32[128]{0:T(128)}, u32[]{:S(2)}) copy-start(s32[128]{0:T(128)} %param.23) | copy-start | bytes 1540
  0.0 26.4 %copy-start.5 = (f32[8,1024]{1,0:T(8,128)S(1)}, f32[8,1024]{1,0:T(8,128)}, u32[]{:S(2)}) copy-start(f32[8,1024]{1,0:T(8,128)} %param.22) | copy-start | bytes 98308
  0.0 26.5 %copy-start.8 = (f32[128]{0:T(128)S(1)}, f32[128]{0:T(128)}, u32[]{:S(2)}) copy-start(f32[128]{0:T(128)} %param.24) | copy-start | bytes 1540
  0.0 57.3 %copy-start = (f32[8,128]{0,1:T(8,128)S(1)}, f32[8,128]{0,1:T(8,128)}, u32[]{:S(2)}) copy-start(f32[8,128]{0,1:T(8,128)} %constant.61.clone) | copy-start | bytes 12292
  0.0 57.3 %copy-start.4 = (f32[8,128]{0,1:T(8,128)S(1)}, f32[8,128]{0,1:T(8,128)}, u32[]{:S(2)}) copy-start(f32[8,128]{0,1:T(8,128)} %constant.62.clone) | copy-start | bytes 12292
  5.4 52.4 %copy-start.1 = (bf16[2,128,2,128,1]{3,1,2,0,4:T(8,128)(2,1)S(1)}, bf16[2,128,2,128,1]{3,1,2,0,4:T(8,128)(2,1)}, u32[]{:S(2)}) copy-start(bf16[2,128,2,128,1]{3,1,2,0,4:T(8,128)(2,1)} %constant.70) | copy-start | bytes 393220
  5.4 51.4 %all-to-all-start = ((bf16[128,2,8,128]{3,2,1,0:T(8,128)(2,1)}), bf16[128,2,8,128]{3,2,1,0:T(8,128)(2,1)S(1)}, u32[]{:S(2)}, u32[]{:S(2)}) async-start(bf16[128,2,8,128]{3,2,1,0:T(8,128)(2,1)} %bitcast.15), calls=%async_computation | async-start | bytes 1048576 | tf_op jit(solution)/shard_map/all_to_all | solution.py:198
  56.9 5.3 %copy-start.9 = (s32[4,16]{1,0:T(4,128)S(1)}, s32[4,16]{1,0:T(4,128)}, u32[]{:S(2)}) copy-start(s32[4,16]{1,0:T(4,128)} %param.25) | copy-start | bytes 772
  58.7 8.1 %collective-permute-start = (bf16[2,1024,31]{1,2,0:T(8,128)(2,1)S(1)}, bf16[2,1024,31]{1,2,0:T(8,128)(2,1)S(1)}, u32[]{:S(2)}, u32[]{:S(2)}) collective-permute-start(bf16[2,1024,31]{1,2,0:T(8,128)(2,1)S(1)} %slice.194), channel_id=1, source_target_pairs={{4,0},{8,4},{12,8},{16,12},{20,16},{24,20},{28,24},{32,28},{36,32}... | collective-permute-start | bytes 380936 | tf_op jit(solution)/shard_map/ppermute | solution.py:22
  68.9 3.0 %copy-start.6 = (bf16[2,8,2,8,1]{3,1,2,4,0:T(8,128)(2,1)S(1)}, bf16[2,8,2,8,1]{3,1,2,4,0:T(8,128)(2,1)}, u32[]{:S(2)}) copy-start(bf16[2,8,2,8,1]{3,1,2,4,0:T(8,128)(2,1)} %constant.68) | copy-start | bytes 1540
  71.4 0.9 %copy-start.3 = (f32[8,128]{0,1:T(8,128)S(1)}, f32[8,128]{0,1:T(8,128)}, u32[]{:S(2)}) copy-start(f32[8,128]{0,1:T(8,128)} %constant.65.clone) | copy-start | bytes 12292
  71.4 1.3 %copy-start.2 = (bf16[2,128,2,128,1]{3,1,2,4,0:T(8,128)(2,1)S(1)}, bf16[2,128,2,128,1]{3,1,2,4,0:T(8,128)(2,1)}, u32[]{:S(2)}) copy-start(bf16[2,128,2,128,1]{3,1,2,4,0:T(8,128)(2,1)} %constant.67) | copy-start | bytes 393220
  73.9 8.8 %all-to-all-start.1 = ((f32[4,8,8,128]{3,2,1,0:T(8,128)}), f32[4,8,8,128]{3,2,1,0:T(8,128)S(1)}, u32[]{:S(2)}, u32[]{:S(2)}) async-start(f32[4,8,8,128]{3,2,1,0:T(8,128)} %copy.75), calls=%async_computation.1 | async-start | bytes 262144 | tf_op jit(solution)/shard_map/all_to_all | solution.py:248

commit v18 on v14

--- a/solution.py
+++ b/solution.py
@@ -79,12 +79,10 @@
     fwd_tw, inv_tw = fwd_tw_ref[...], inv_tw_ref[...]
     taps = replica_ref[...].astype(jnp.float32)
     filled = taps.shape[1] // side
+    rows = pltpu.einshape("r(nb)->(rn)b", taps, b=side)
     blank = jnp.zeros((side - filled, side), jnp.float32)
-    pieces = []
-    for part in range(2):
-        pieces += [taps[part : part + 1, n * side : (n + 1) * side] for n in range(filled)]
-        pieces.append(blank)
-    replica = jnp.concatenate(pieces, axis=0).astype(jnp.bfloat16)
+    replica = jnp.concatenate([rows[:filled], blank, rows[filled:], blank], axis=0)
+    replica = replica.astype(jnp.bfloat16)
     rep_real, rep_imag = forward_transposed(replica, fwd, fwd_t, fwd_tw)
     rep_real = rep_real * 128.0
     rep_imag = rep_imag * 128.0

time: 84 us -> 84 us (level)
  no operation moved by 1% of the time
where the time goes in v18:
time: 84 us; the launch traced here: 83.6 us
  waiting for transfers between devices  34.8 us (41%)
  starting transfers between devices  27.8 us (33%)
  other arithmetic  8.84 us (11%)
  local copies, waits for them, and re-layouts  4.87 us (6%)
  Pallas kernels  3.4 us (4%)
  matrix products  2.84 us (3%)
  between operations  0.96 us (1%)
    all_to_all x1, waiting for transfers between devices, per_device(): lax.all_to_all(compressed, 'wide', split_axis=0, concat_axis=2, tiled=True)  27.8 us
    all_to_all x1, starting transfers between devices, per_device(): lax.all_to_all(compressed, 'wide', split_axis=0, concat_axis=2, tiled=True)  20.7 us
    all_to_all x1, starting transfers between devices, per_device(): lax.all_to_all(partial, 'narrow', split_axis=0, concat_axis=0, tiled=True)  4.01 us
    all_to_all x1, waiting for transfers between devices, per_device(): lax.all_to_all(partial, 'narrow', split_axis=0, concat_axis=0, tiled=True)  3.54 us
    ppermute x1, waiting for transfers between devices, passed_along(): return lax.ppermute(shard, axis, pairs)  3.48 us
    pallas_call x1, Pallas kernels, range_compress(): pl.pallas_call(range_kernel, in_specs=[whole] * 8, out_specs=whole, out_s...  3.4 us
    ppermute x1, starting transfers between devices, passed_along(): return lax.ppermute(shard, axis, pairs)  3.11 us
    convert_element_type x1, other arithmetic, per_device(): (moved_real * phase_cos - moved_imag * phase_sin).astype(jnp.bfloat16)  2.49 us
  transfers between devices with their start and end apart: 3, of which 3 were waited for; matrix products, arithmetic and copies ran while one was open for 8% of the time, Pallas kernels for 0%

profile of v18, /device:TPU:1, one launch (start us, length us, event | category | flops | bytes accessed | tf_op | source)
XLA Modules:
  0.0 83.6 jit_solution(6675983146321238124)
XLA Ops:
  0.0 0.0 copy-start.6
  0.0 0.0 copy-start
  0.0 0.0 copy-start.4
  0.0 3.4 %shard_map.190 = bf16[2048,128]{1,0:T(8,128)(2,1)} custom-call(bf16[2,1024,128]{2,1,0:T(8,128)(2,1)} %bitcast.108, bf16[2,4096]{1,0:T(2,128)(2,1)} %replica_ref.1, bf16[256,256]{1,0:T(8,128)(2,1)} %constant.55.clone.fwd_ref.inv_t_ref, bf16[256,256]{1,0:T(8,128)(2,1)} %constant.56.clone.fwd_t_ref.inv_ref, bf16[256,256]{1,0:T(8,128)(2,1)} %constant.56.clone.fwd_t_ref.inv_ref, ...), custom_call_target="tpu_custom_call" | custom-call | flops 603979776 | bytes 1048576 | tf_op jit(solution)/shard_map/pallas_call | solution.py:137
  3.4 0.0 copy-start.1
  3.4 20.7 %all-to-all-start = ((bf16[128,2,8,128]{3,2,1,0:T(8,128)(2,1)}), bf16[128,2,8,128]{3,2,1,0:T(8,128)(2,1)S(1)}, u32[]{:S(2)}, u32[]{:S(2)}) async-start(bf16[128,2,8,128]{3,2,1,0:T(8,128)(2,1)} %bitcast.99), calls=%async_computation | async-start | bytes 1048576 | tf_op jit(solution)/shard_map/all_to_all | solution.py:193
  24.1 0.7 iota_add_fusion
  24.8 1.2 %fusion.52 = (f32[1,1024]{1,0:T(1,128)S(1)}, f32[1,1024]{1,0:T(1,128)S(1)}, f32[1,1024]{1,0:T(1,128)S(1)}, f32[1,1024]{1,0:T(1,128)S(1)}, f32[1,1024]{1,0:T(1,12...) fusion(f32[8,1024]{1,0:T(8,128)} %param.22), kind=kLoop, calls=%fused_computation.107 | loop fusion | bytes 65536 | tf_op jit(solution)/shard_map/slice | solution.py:207
  26.1 0.8 broadcast_divide_fusion
  26.8 1.7 %divide_cosine_fusion = (f32[1,513,128]{2,1,0:T(8,128)S(1)}, f32[1,513,128]{2,1,0:T(8,128)S(1)}) fusion(f32[128]{0:T(128)} %param.24, f32[513]{0:T(1024)S(1)} %fusion.40), kind=kLoop, calls=%fused_computation.80 | loop fusion | flops 65664 | bytes 527876 | tf_op jit(solution)/shard_map/cos | solution.py:215
  28.5 1.0 %slice_cosine_fusion = (f32[511,128]{1,0:T(8,128)S(1)}, f32[511,128]{1,0:T(8,128)S(1)}) fusion(f32[513,128]{1,0:T(8,128)S(1)} %broadcast_divide_fusion), kind=kLoop, calls=%fused_computation.78 | loop fusion | bytes 784896 | tf_op jit(solution)/shard_map/cos | solution.py:215
  29.5 27.8 %all-to-all-done = bf16[128,2,8,128]{3,2,1,0:T(8,128)(2,1)S(1)} async-done(((bf16[128,2,8,128]{3,2,1,0:T(8,128)(2,1)}), bf16[128,2,8,128]{3,2,1,0:T(8,128)(2,1)S(1)}, u32[]{:S(2)}, u32[]{:S(2)}) %all-to-all-start) | async-done | bytes 524320 | tf_op jit(solution)/shard_map/all_to_all | solution.py:193
  57.4 0.0 copy-start.7
  57.4 0.0 copy-done.6
  57.4 0.4 convolution_bitcast_fusion.1
  57.8 0.0 copy-done
  57.8 0.0 copy-done.4
  57.8 0.4 subtract_convert_fusion.2
  58.2 0.1 maximum_bitcast_fusion
  58.3 0.0 copy-done.1
  58.3 0.3 fusion.1
  58.6 0.3 copy.86
  58.9 0.2 copy.53
  59.2 3.1 %collective-permute-start = (bf16[2,1024,31]{1,2,0:T(8,128)(2,1)S(1)}, bf16[2,1024,31]{1,2,0:T(8,128)(2,1)S(1)}, u32[]{:S(2)}, u32[]{:S(2)}) collective-permute-start(bf16[2,1024,31]{1,2,0:T(8,128)(2,1)S(1)} %slice.194), channel_id=1, source_target_pairs={{4,0},{8,4},{12,8},{16,12},{20,16},{24,20},{28,24},{32,28},{36,32}... | collective-permute-start | bytes 380936 | tf_op jit(solution)/shard_map/ppermute | solution.py:21
  62.3 0.0 copy-done.7
  62.3 0.3 rev.7
  62.7 0.3 rev.8
  63.0 0.1 convert_reduce_fusion
  63.1 3.5 %collective-permute-done = bf16[2,1024,31]{1,2,0:T(8,128)(2,1)S(1)} collective-permute-done((bf16[2,1024,31]{1,2,0:T(8,128)(2,1)S(1)}, bf16[2,1024,31]{1,2,0:T(8,128)(2,1)S(1)}, u32[]{:S(2)}, u32[]{:S(2)}) %collective-permute-start) | collective-permute-done | bytes 127008 | tf_op jit(solution)/shard_map/ppermute | solution.py:21
  66.6 1.3 %fusion.2 = bf16[2,1024,1024]{2,1,0:T(8,128)(2,1)S(1)} fusion(bf16[2,1024,31]{1,2,0:T(8,128)(2,1)S(1)} %collective-permute-done, bf16[2,1024,128]{1,2,0:T(8,128)(2,1)S(1)} %copy.53, s32[1024]{0:T(1024)S(1)} %add_bitcast_fusion), kind=kOutput, calls=%fused_computation.6 | convolution fusion | flops 668359680 | bytes 4849664 | tf_op jit(solution)/shard_map/xpc,cn->xpn/dot_general | solution.py:205
  67.9 0.8 slice_convert_fusion.7
  68.7 0.0 copy-start.5
  68.8 2.5 %subtract_convert_fusion.1 = (bf16[1,1024,128]{2,1,0:T(8,128)(2,1)S(1)}, f32[1,1024,128]{2,1,0:T(8,128)S(1)}, f32[1,1024,128]{2,1,0:T(8,128)S(1)}) fusion(f32[1,511,128]{2,1,0:T(8,128)S(1)} %bitcast.93, f32[1,513,128]{2,1,0:T(8,128)S(1)} %get-tuple-element.31, f32[1,511,128]{2,1,0:T(8,128)S(1)} %bitcast.91, f32[1,513,128]{2,1,0:T(8,128)S(1)} %get-tuple-element.30, ...), kind=kLoop, calls=%fused_computation.70 | loop fusion | flops 4718592 | bytes 10780672 | tf_op jit(solution)/shard_map/convert_element_type | solution.py:219
  71.3 0.0 copy-start.3
  71.3 0.0 copy-start.2
  71.3 0.1 add_convert_fusion.1
  71.4 0.2 copy.55
  71.6 0.2 copy.54
  71.8 0.0 copy-done.5
  71.8 0.3 convolution_bitcast_fusion
  72.2 0.0 copy-done.3
  72.2 0.4 subtract_convert_fusion
  72.5 0.1 pad_maximum_fusion.2
  72.6 0.0 copy-done.2
  72.6 0.3 convolution_bitcast_fusion.2
  72.9 0.1 fusion.9
  73.0 0.2 copy.57
  73.2 0.1 convert_element_type.82
  73.3 0.2 fusion.32
  73.4 0.6 copy.59
  74.1 4.0 %all-to-all-start.1 = ((f32[4,64,128]{2,1,0:T(8,128)}), f32[4,64,128]{2,1,0:T(8,128)S(1)}, u32[]{:S(2)}, u32[]{:S(2)}) async-start(f32[4,64,128]{2,1,0:T(8,128)} %copy.59), calls=%async_computation.1 | async-start | bytes 262144 | tf_op jit(solution)/shard_map/all_to_all | solution.py:237
  78.1 0.6 fusion.47
  79.4 3.5 %all-to-all-done.1 = f32[4,64,128]{2,1,0:T(8,128)S(1)} async-done(((f32[4,64,128]{2,1,0:T(8,128)}), f32[4,64,128]{2,1,0:T(8,128)S(1)}, u32[]{:S(2)}, u32[]{:S(2)}) %all-to-all-start.1) | async-done | bytes 131104 | tf_op jit(solution)/shard_map/all_to_all | solution.py:237
  82.9 0.6 divide_bitcast_fusion
  (6 shorter events, 0.1 us)
Async XLA Ops:
  0.0 57.4 %copy-start.6 = (bf16[2,8,2,8,1]{3,1,2,4,0:T(8,128)(2,1)S(1)}, bf16[2,8,2,8,1]{3,1,2,4,0:T(8,128)(2,1)}, u32[]{:S(2)}) copy-start(bf16[2,8,2,8,1]{3,1,2,4,0:T(8,128)(2,1)} %constant.69) | copy-start | bytes 1540
  0.0 57.8 %copy-start = (f32[8,128]{0,1:T(8,128)S(1)}, f32[8,128]{0,1:T(8,128)}, u32[]{:S(2)}) copy-start(f32[8,128]{0,1:T(8,128)} %constant.61.clone) | copy-start | bytes 12292
  0.0 57.8 %copy-start.4 = (f32[8,128]{0,1:T(8,128)S(1)}, f32[8,128]{0,1:T(8,128)}, u32[]{:S(2)}) copy-start(f32[8,128]{0,1:T(8,128)} %constant.62.clone) | copy-start | bytes 12292
  3.4 54.8 %copy-start.1 = (bf16[2,128,2,128,1]{3,1,2,0,4:T(8,128)(2,1)S(1)}, bf16[2,128,2,128,1]{3,1,2,0,4:T(8,128)(2,1)}, u32[]{:S(2)}) copy-start(bf16[2,128,2,128,1]{3,1,2,0,4:T(8,128)(2,1)} %constant.70) | copy-start | bytes 393220
  3.4 53.9 %all-to-all-start = ((bf16[128,2,8,128]{3,2,1,0:T(8,128)(2,1)}), bf16[128,2,8,128]{3,2,1,0:T(8,128)(2,1)S(1)}, u32[]{:S(2)}, u32[]{:S(2)}) async-start(bf16[128,2,8,128]{3,2,1,0:T(8,128)(2,1)} %bitcast.99), calls=%async_computation | async-start | bytes 1048576 | tf_op jit(solution)/shard_map/all_to_all | solution.py:193
  57.4 4.9 %copy-start.7 = (s32[4,16]{1,0:T(4,128)S(1)}, s32[4,16]{1,0:T(4,128)}, u32[]{:S(2)}) copy-start(s32[4,16]{1,0:T(4,128)} %param.25) | copy-start | bytes 772
  59.2 7.4 %collective-permute-start = (bf16[2,1024,31]{1,2,0:T(8,128)(2,1)S(1)}, bf16[2,1024,31]{1,2,0:T(8,128)(2,1)S(1)}, u32[]{:S(2)}, u32[]{:S(2)}) collective-permute-start(bf16[2,1024,31]{1,2,0:T(8,128)(2,1)S(1)} %slice.194), channel_id=1, source_target_pairs={{4,0},{8,4},{12,8},{16,12},{20,16},{24,20},{28,24},{32,28},{36,32}... | collective-permute-start | bytes 380936 | tf_op jit(solution)/shard_map/ppermute | solution.py:21
  68.7 3.0 %copy-start.5 = (bf16[2,8,2,8,1]{3,1,2,4,0:T(8,128)(2,1)S(1)}, bf16[2,8,2,8,1]{3,1,2,4,0:T(8,128)(2,1)}, u32[]{:S(2)}) copy-start(bf16[2,8,2,8,1]{3,1,2,4,0:T(8,128)(2,1)} %constant.68) | copy-start | bytes 1540
  71.3 0.9 %copy-start.3 = (f32[8,128]{0,1:T(8,128)S(1)}, f32[8,128]{0,1:T(8,128)}, u32[]{:S(2)}) copy-start(f32[8,128]{0,1:T(8,128)} %constant.65.clone) | copy-start | bytes 12292
  71.3 1.3 %copy-start.2 = (bf16[2,128,2,128,1]{3,1,2,4,0:T(8,128)(2,1)S(1)}, bf16[2,128,2,128,1]{3,1,2,4,0:T(8,128)(2,1)}, u32[]{:S(2)}) copy-start(bf16[2,128,2,128,1]{3,1,2,4,0:T(8,128)(2,1)} %constant.67) | copy-start | bytes 393220
  74.1 8.8 %all-to-all-start.1 = ((f32[4,64,128]{2,1,0:T(8,128)}), f32[4,64,128]{2,1,0:T(8,128)S(1)}, u32[]{:S(2)}, u32[]{:S(2)}) async-start(f32[4,64,128]{2,1,0:T(8,128)} %copy.59), calls=%async_computation.1 | async-start | bytes 262144 | tf_op jit(solution)/shard_map/all_to_all | solution.py:237

commit v19 on v12

--- a/solution.py
+++ b/solution.py
@@ -193,8 +193,9 @@
     width = length // devices
     assert compressed.shape[0] == devices and compressed.shape[3] == width
     turned = lax.all_to_all(compressed, "wide", split_axis=0, concat_axis=2, tiled=True)[0]
-    doppler = pulse_transform(turned, PUL_DEV, -1).astype(jnp.bfloat16)
-    rim = passed_along(doppler[:, :, :HALO], "wide", -1)
+    spectra = pulse_transform(turned, PUL_DEV, -1)
+    doppler = spectra.astype(jnp.bfloat16)
+    rim = passed_along(spectra[:, :, :HALO].astype(jnp.bfloat16), "wide", -1)
     extended = jnp.concatenate([doppler, rim], axis=2)
     pulses = extended.shape[1]
     columns = jnp.arange(width + HALO, dtype=jnp.int32)

time: 83.7 us -> 83.7 us (level)
  no operation moved by 1% of the time
where the time goes in v19:
time: 83.7 us; the launch traced here: 83.3 us
  waiting for transfers between devices  34.8 us (42%)
  starting transfers between devices  27.8 us (33%)
  other arithmetic  8.22 us (10%)
  local copies, waits for them, and re-layouts  5.2 us (6%)
  Pallas kernels  3.41 us (4%)
  matrix products  2.83 us (3%)
  between operations  0.96 us (1%)
    all_to_all x1, waiting for transfers between devices, per_device(): lax.all_to_all(compressed, 'wide', split_axis=0, concat_axis=2, tiled=True)  27.8 us
    all_to_all x1, starting transfers between devices, per_device(): lax.all_to_all(compressed, 'wide', split_axis=0, concat_axis=2, tiled=True)  20.7 us
    all_to_all x1, starting transfers between devices, per_device(): lax.all_to_all(partial, 'narrow', split_axis=0, concat_axis=0, tiled=True)  4.02 us
    all_to_all x1, waiting for transfers between devices, per_device(): lax.all_to_all(partial, 'narrow', split_axis=0, concat_axis=0, tiled=True)  3.54 us
    ppermute x1, waiting for transfers between devices, passed_along(): return lax.ppermute(shard, axis, pairs)  3.48 us
    pallas_call x1, Pallas kernels, range_compress(): pl.pallas_call(range_kernel, in_specs=[whole] * 8, out_specs=whole, out_s...  3.41 us
    ppermute x1, starting transfers between devices, passed_along(): return lax.ppermute(shard, axis, pairs)  3.11 us
    convert_element_type x1, other arithmetic, per_device(): (moved_real * phase_cos - moved_imag * phase_sin).astype(jnp.bfloat16)  2.49 us
  transfers between devices with their start and end apart: 3, of which 3 were waited for; matrix products, arithmetic and copies ran while one was open for 8% of the time, Pallas kernels for 0%

profile of v19, /device:TPU:1, one launch (start us, length us, event | category | flops | bytes accessed | tf_op | source)
XLA Modules:
  0.0 83.3 jit_solution(8714679565631387363)
XLA Ops:
  0.0 0.0 copy-start.6
  0.0 0.0 copy-start
  0.0 0.0 copy-start.4
  0.0 3.4 %shard_map.190 = bf16[2048,128]{1,0:T(8,128)(2,1)} custom-call(bf16[2,1024,128]{2,1,0:T(8,128)(2,1)} %bitcast.108, bf16[2,4096]{1,0:T(2,128)(2,1)} %replica_ref.1, bf16[256,256]{1,0:T(8,128)(2,1)} %constant.55.clone.fwd_ref.inv_t_ref, bf16[256,256]{1,0:T(8,128)(2,1)} %constant.56.clone.fwd_t_ref.inv_ref, bf16[256,256]{1,0:T(8,128)(2,1)} %constant.56.clone.fwd_t_ref.inv_ref, ...), custom_call_target="tpu_custom_call" | custom-call | flops 603979776 | bytes 1048576 | tf_op jit(solution)/shard_map/pallas_call | solution.py:139
  3.4 0.0 copy-start.1
  3.4 20.7 %all-to-all-start = ((bf16[128,2,8,128]{3,2,1,0:T(8,128)(2,1)}), bf16[128,2,8,128]{3,2,1,0:T(8,128)(2,1)S(1)}, u32[]{:S(2)}, u32[]{:S(2)}) async-start(bf16[128,2,8,128]{3,2,1,0:T(8,128)(2,1)} %bitcast.99), calls=%async_computation | async-start | bytes 1048576 | tf_op jit(solution)/shard_map/all_to_all | solution.py:195
  24.1 0.7 iota_add_fusion
  24.8 1.2 %fusion.52 = (f32[1,1024]{1,0:T(1,128)S(1)}, f32[1,1024]{1,0:T(1,128)S(1)}, f32[1,1024]{1,0:T(1,128)S(1)}, f32[1,1024]{1,0:T(1,128)S(1)}, f32[1,1024]{1,0:T(1,12...) fusion(f32[8,1024]{1,0:T(8,128)} %param.22), kind=kLoop, calls=%fused_computation.108 | loop fusion | bytes 65536 | tf_op jit(solution)/shard_map/slice | solution.py:210
  26.1 0.8 broadcast_divide_fusion
  26.9 1.7 %divide_cosine_fusion = (f32[1,513,128]{2,1,0:T(8,128)S(1)}, f32[1,513,128]{2,1,0:T(8,128)S(1)}) fusion(f32[128]{0:T(128)} %param.24, f32[513]{0:T(1024)S(1)} %fusion.40), kind=kLoop, calls=%fused_computation.80 | loop fusion | flops 65664 | bytes 527876 | tf_op jit(solution)/shard_map/cos | solution.py:218
  28.5 1.0 %slice_cosine_fusion = (f32[511,128]{1,0:T(8,128)S(1)}, f32[511,128]{1,0:T(8,128)S(1)}) fusion(f32[513,128]{1,0:T(8,128)S(1)} %broadcast_divide_fusion), kind=kLoop, calls=%fused_computation.78 | loop fusion | bytes 784896 | tf_op jit(solution)/shard_map/cos | solution.py:218
  29.5 27.8 %all-to-all-done = bf16[128,2,8,128]{3,2,1,0:T(8,128)(2,1)S(1)} async-done(((bf16[128,2,8,128]{3,2,1,0:T(8,128)(2,1)}), bf16[128,2,8,128]{3,2,1,0:T(8,128)(2,1)S(1)}, u32[]{:S(2)}, u32[]{:S(2)}) %all-to-all-start) | async-done | bytes 524320 | tf_op jit(solution)/shard_map/all_to_all | solution.py:195
  57.4 0.0 copy-start.7
  57.4 0.0 copy-done.6
  57.4 0.4 convolution_bitcast_fusion.1
  57.8 0.0 copy-done
  57.8 0.0 copy-done.4
  57.8 0.4 subtract_convert_fusion.2
  58.2 0.1 pad_maximum_fusion
  58.3 0.0 copy-done.1
  58.3 0.3 fusion
  58.6 0.3 copy.100
  58.9 0.2 copy.66
  59.2 3.1 %collective-permute-start = (bf16[2,1024,31]{1,2,0:T(8,128)(2,1)S(1)}, bf16[2,1024,31]{1,2,0:T(8,128)(2,1)S(1)}, u32[]{:S(2)}, u32[]{:S(2)}) collective-permute-start(bf16[2,1024,31]{1,2,0:T(8,128)(2,1)S(1)} %slice.195), channel_id=1, source_target_pairs={{4,0},{8,4},{12,8},{16,12},{20,16},{24,20},{28,24},{32,28},{36,32}... | collective-permute-start | bytes 380936 | tf_op jit(solution)/shard_map/ppermute | solution.py:21
  62.3 0.0 copy-done.7
  62.3 0.3 rev.7
  62.7 0.3 rev.8
  63.0 0.1 convert_reduce_fusion
  63.1 3.5 %collective-permute-done = bf16[2,1024,31]{1,2,0:T(8,128)(2,1)S(1)} collective-permute-done((bf16[2,1024,31]{1,2,0:T(8,128)(2,1)S(1)}, bf16[2,1024,31]{1,2,0:T(8,128)(2,1)S(1)}, u32[]{:S(2)}, u32[]{:S(2)}) %collective-permute-start) | collective-permute-done | bytes 127008 | tf_op jit(solution)/shard_map/ppermute | solution.py:21
  66.6 1.3 %fusion.1 = bf16[2,1024,1024]{2,1,0:T(8,128)(2,1)S(1)} fusion(bf16[2,1024,31]{1,2,0:T(8,128)(2,1)S(1)} %collective-permute-done, bf16[2,1024,128]{1,2,0:T(8,128)(2,1)S(1)} %copy.66, s32[1024]{0:T(1024)S(1)} %add_bitcast_fusion), kind=kOutput, calls=%fused_computation.5 | convolution fusion | flops 668359680 | bytes 4849664 | tf_op jit(solution)/shard_map/xpc,cn->xpn/dot_general | solution.py:208
  67.9 0.8 slice_convert_fusion.7
  68.8 0.0 copy-start.5
  68.8 2.5 %subtract_convert_fusion.1 = (bf16[1,1024,128]{2,1,0:T(8,128)(2,1)S(1)}, f32[1,1024,128]{2,1,0:T(8,128)S(1)}, f32[1,1024,128]{2,1,0:T(8,128)S(1)}) fusion(f32[1,511,128]{2,1,0:T(8,128)S(1)} %bitcast.93, f32[1,513,128]{2,1,0:T(8,128)S(1)} %get-tuple-element.31, f32[1,511,128]{2,1,0:T(8,128)S(1)} %bitcast.91, f32[1,513,128]{2,1,0:T(8,128)S(1)} %get-tuple-element.30, ...), kind=kLoop, calls=%fused_computation.70 | loop fusion | flops 4718592 | bytes 10780672 | tf_op jit(solution)/shard_map/convert_element_type | solution.py:222
  71.3 0.0 copy-start.3
  71.3 0.0 copy-start.2
  71.3 0.1 add_convert_fusion.1
  71.4 0.2 copy.68
  71.6 0.2 copy.67
  71.8 0.0 copy-done.5
  71.8 0.3 convolution_bitcast_fusion
  72.2 0.0 copy-done.3
  72.2 0.4 subtract_convert_fusion
  72.5 0.1 pad_maximum_fusion.3
  72.6 0.0 copy-done.2
  72.6 0.3 convolution_bitcast_fusion.2
  72.9 0.1 fusion.32
  73.0 0.2 fusion.33
  73.1 0.6 copy.71
  73.8 4.0 %all-to-all-start.1 = ((f32[4,8,8,128]{3,2,1,0:T(8,128)}), f32[4,8,8,128]{3,2,1,0:T(8,128)S(1)}, u32[]{:S(2)}, u32[]{:S(2)}) async-start(f32[4,8,8,128]{3,2,1,0:T(8,128)} %copy.71), calls=%async_computation.1 | async-start | bytes 262144 | tf_op jit(solution)/shard_map/all_to_all | solution.py:242
  77.8 0.6 fusion.47
  79.1 3.5 %all-to-all-done.1 = f32[4,8,8,128]{3,2,1,0:T(8,128)S(1)} async-done(((f32[4,8,8,128]{3,2,1,0:T(8,128)}), f32[4,8,8,128]{3,2,1,0:T(8,128)S(1)}, u32[]{:S(2)}, u32[]{:S(2)}) %all-to-all-start.1) | async-done | bytes 131104 | tf_op jit(solution)/shard_map/all_to_all | solution.py:242
  82.7 0.6 copy.101
  (7 shorter events, 0.1 us)
Async XLA Ops:
  0.0 57.4 %copy-start.6 = (bf16[2,8,2,8,1]{3,1,2,4,0:T(8,128)(2,1)S(1)}, bf16[2,8,2,8,1]{3,1,2,4,0:T(8,128)(2,1)}, u32[]{:S(2)}) copy-start(bf16[2,8,2,8,1]{3,1,2,4,0:T(8,128)(2,1)} %constant.70) | copy-start | bytes 1540
  0.0 57.8 %copy-start = (f32[8,128]{0,1:T(8,128)S(1)}, f32[8,128]{0,1:T(8,128)}, u32[]{:S(2)}) copy-start(f32[8,128]{0,1:T(8,128)} %constant.61.clone) | copy-start | bytes 12292
  0.0 57.8 %copy-start.4 = (f32[8,128]{0,1:T(8,128)S(1)}, f32[8,128]{0,1:T(8,128)}, u32[]{:S(2)}) copy-start(f32[8,128]{0,1:T(8,128)} %constant.62.clone) | copy-start | bytes 12292
  3.4 54.8 %copy-start.1 = (bf16[2,128,2,128,1]{3,1,2,4,0:T(8,128)(2,1)S(1)}, bf16[2,128,2,128,1]{3,1,2,4,0:T(8,128)(2,1)}, u32[]{:S(2)}) copy-start(bf16[2,128,2,128,1]{3,1,2,4,0:T(8,128)(2,1)} %constant.69) | copy-start | bytes 393220
  3.4 53.9 %all-to-all-start = ((bf16[128,2,8,128]{3,2,1,0:T(8,128)(2,1)}), bf16[128,2,8,128]{3,2,1,0:T(8,128)(2,1)S(1)}, u32[]{:S(2)}, u32[]{:S(2)}) async-start(bf16[128,2,8,128]{3,2,1,0:T(8,128)(2,1)} %bitcast.99), calls=%async_computation | async-start | bytes 1048576 | tf_op jit(solution)/shard_map/all_to_all | solution.py:195
  57.4 4.9 %copy-start.7 = (s32[4,16]{1,0:T(4,128)S(1)}, s32[4,16]{1,0:T(4,128)}, u32[]{:S(2)}) copy-start(s32[4,16]{1,0:T(4,128)} %param.25) | copy-start | bytes 772
  59.2 7.4 %collective-permute-start = (bf16[2,1024,31]{1,2,0:T(8,128)(2,1)S(1)}, bf16[2,1024,31]{1,2,0:T(8,128)(2,1)S(1)}, u32[]{:S(2)}, u32[]{:S(2)}) collective-permute-start(bf16[2,1024,31]{1,2,0:T(8,128)(2,1)S(1)} %slice.195), channel_id=1, source_target_pairs={{4,0},{8,4},{12,8},{16,12},{20,16},{24,20},{28,24},{32,28},{36,32}... | collective-permute-start | bytes 380936 | tf_op jit(solution)/shard_map/ppermute | solution.py:21
  68.8 3.0 %copy-start.5 = (bf16[2,8,2,8,1]{3,1,2,4,0:T(8,128)(2,1)S(1)}, bf16[2,8,2,8,1]{3,1,2,4,0:T(8,128)(2,1)}, u32[]{:S(2)}) copy-start(bf16[2,8,2,8,1]{3,1,2,4,0:T(8,128)(2,1)} %constant.68) | copy-start | bytes 1540
  71.3 0.9 %copy-start.3 = (f32[8,128]{0,1:T(8,128)S(1)}, f32[8,128]{0,1:T(8,128)}, u32[]{:S(2)}) copy-start(f32[8,128]{0,1:T(8,128)} %constant.65.clone) | copy-start | bytes 12292
  71.3 1.3 %copy-start.2 = (bf16[2,128,2,128,1]{3,1,2,4,0:T(8,128)(2,1)S(1)}, bf16[2,128,2,128,1]{3,1,2,4,0:T(8,128)(2,1)}, u32[]{:S(2)}) copy-start(bf16[2,128,2,128,1]{3,1,2,4,0:T(8,128)(2,1)} %constant.67) | copy-start | bytes 393220
  73.8 8.8 %all-to-all-start.1 = ((f32[4,8,8,128]{3,2,1,0:T(8,128)}), f32[4,8,8,128]{3,2,1,0:T(8,128)S(1)}, u32[]{:S(2)}, u32[]{:S(2)}) async-start(f32[4,8,8,128]{3,2,1,0:T(8,128)} %copy.71), calls=%async_computation.1 | async-start | bytes 262144 | tf_op jit(solution)/shard_map/all_to_all | solution.py:242

commit v20 on v15

--- a/solution.py
+++ b/solution.py
@@ -191,8 +191,9 @@
     width = length // devices
     assert compressed.shape[0] == devices and compressed.shape[3] == width
     turned = lax.all_to_all(compressed, "wide", split_axis=0, concat_axis=2, tiled=True)[0]
-    doppler = pulse_transform(turned, PUL_DEV, -1).astype(jnp.bfloat16)
-    rim = passed_along(doppler[:, :, :HALO], "wide", -1)
+    spectra = pulse_transform(turned, PUL_DEV, -1)
+    doppler = spectra.astype(jnp.bfloat16)
+    rim = passed_along(spectra[:, :, :HALO].astype(jnp.bfloat16), "wide", -1)
     extended = jnp.concatenate([doppler, rim], axis=2)
     pulses = extended.shape[1]
     columns = jnp.arange(width + HALO, dtype=jnp.int32)

time: 83.7 us -> 83.7 us (level)
  no operation moved by 1% of the time
where the time goes in v20:
time: 83.7 us; the launch traced here: 83.3 us
  waiting for transfers between devices  34.8 us (42%)
  starting transfers between devices  27.8 us (33%)
  other arithmetic  8.22 us (10%)
  local copies, waits for them, and re-layouts  5.2 us (6%)
  Pallas kernels  3.4 us (4%)
  matrix products  2.84 us (3%)
  between operations  0.96 us (1%)
    all_to_all x1, waiting for transfers between devices, per_device(): lax.all_to_all(compressed, 'wide', split_axis=0, concat_axis=2, tiled=True)  27.8 us
    all_to_all x1, starting transfers between devices, per_device(): lax.all_to_all(compressed, 'wide', split_axis=0, concat_axis=2, tiled=True)  20.7 us
    all_to_all x1, starting transfers between devices, per_device(): lax.all_to_all(partial, 'narrow', split_axis=0, concat_axis=0, tiled=True)  4.01 us
    all_to_all x1, waiting for transfers between devices, per_device(): lax.all_to_all(partial, 'narrow', split_axis=0, concat_axis=0, tiled=True)  3.54 us
    ppermute x1, waiting for transfers between devices, passed_along(): return lax.ppermute(shard, axis, pairs)  3.48 us
    pallas_call x1, Pallas kernels, range_compress(): pl.pallas_call(range_kernel, in_specs=[whole] * 8, out_specs=whole, out_s...  3.4 us
    ppermute x1, starting transfers between devices, passed_along(): return lax.ppermute(shard, axis, pairs)  3.11 us
    convert_element_type x1, other arithmetic, per_device(): (moved_real * phase_cos - moved_imag * phase_sin).astype(jnp.bfloat16)  2.49 us
  transfers between devices with their start and end apart: 3, of which 3 were waited for; matrix products, arithmetic and copies ran while one was open for 8% of the time, Pallas kernels for 0%

profile of v20, /device:TPU:1, one launch (start us, length us, event | category | flops | bytes accessed | tf_op | source)
XLA Modules:
  0.0 83.3 jit_solution(621996414532472941)
XLA Ops:
  0.0 0.0 copy-start.6
  0.0 0.0 copy-start
  0.0 0.0 copy-start.4
  0.0 3.4 %shard_map.190 = bf16[2048,128]{1,0:T(8,128)(2,1)} custom-call(bf16[2,1024,128]{2,1,0:T(8,128)(2,1)} %bitcast.108, bf16[2,4096]{1,0:T(2,128)(2,1)} %replica_ref.1, bf16[256,256]{1,0:T(8,128)(2,1)} %constant.55.clone.fwd_ref.inv_t_ref, bf16[256,256]{1,0:T(8,128)(2,1)} %constant.56.clone.fwd_t_ref.inv_ref, bf16[256,256]{1,0:T(8,128)(2,1)} %constant.56.clone.fwd_t_ref.inv_ref, ...), custom_call_target="tpu_custom_call" | custom-call | flops 603979776 | bytes 1048576 | tf_op jit(solution)/shard_map/pallas_call | solution.py:137
  3.4 0.0 copy-start.1
  3.4 20.7 %all-to-all-start = ((bf16[128,2,8,128]{3,2,1,0:T(8,128)(2,1)}), bf16[128,2,8,128]{3,2,1,0:T(8,128)(2,1)S(1)}, u32[]{:S(2)}, u32[]{:S(2)}) async-start(bf16[128,2,8,128]{3,2,1,0:T(8,128)(2,1)} %bitcast.99), calls=%async_computation | async-start | bytes 1048576 | tf_op jit(solution)/shard_map/all_to_all | solution.py:193
  24.1 0.7 iota_add_fusion
  24.8 1.2 %fusion.52 = (f32[1,1024]{1,0:T(1,128)S(1)}, f32[1,1024]{1,0:T(1,128)S(1)}, f32[1,1024]{1,0:T(1,128)S(1)}, f32[1,1024]{1,0:T(1,128)S(1)}, f32[1,1024]{1,0:T(1,12...) fusion(f32[8,1024]{1,0:T(8,128)} %param.22), kind=kLoop, calls=%fused_computation.108 | loop fusion | bytes 65536 | tf_op jit(solution)/shard_map/slice | solution.py:208
  26.1 0.8 broadcast_divide_fusion
  26.8 1.7 %divide_cosine_fusion = (f32[1,513,128]{2,1,0:T(8,128)S(1)}, f32[1,513,128]{2,1,0:T(8,128)S(1)}) fusion(f32[128]{0:T(128)} %param.24, f32[513]{0:T(1024)S(1)} %fusion.40), kind=kLoop, calls=%fused_computation.80 | loop fusion | flops 65664 | bytes 527876 | tf_op jit(solution)/shard_map/cos | solution.py:216
  28.5 1.0 %slice_cosine_fusion = (f32[511,128]{1,0:T(8,128)S(1)}, f32[511,128]{1,0:T(8,128)S(1)}) fusion(f32[513,128]{1,0:T(8,128)S(1)} %broadcast_divide_fusion), kind=kLoop, calls=%fused_computation.78 | loop fusion | bytes 784896 | tf_op jit(solution)/shard_map/cos | solution.py:216
  29.5 27.8 %all-to-all-done = bf16[128,2,8,128]{3,2,1,0:T(8,128)(2,1)S(1)} async-done(((bf16[128,2,8,128]{3,2,1,0:T(8,128)(2,1)}), bf16[128,2,8,128]{3,2,1,0:T(8,128)(2,1)S(1)}, u32[]{:S(2)}, u32[]{:S(2)}) %all-to-all-start) | async-done | bytes 524320 | tf_op jit(solution)/shard_map/all_to_all | solution.py:193
  57.4 0.0 copy-start.7
  57.4 0.0 copy-done.6
  57.4 0.4 convolution_bitcast_fusion.1
  57.8 0.0 copy-done
  57.8 0.0 copy-done.4
  57.8 0.4 subtract_convert_fusion.2
  58.2 0.1 pad_maximum_fusion
  58.3 0.0 copy-done.1
  58.3 0.3 fusion
  58.6 0.3 copy.100
  58.9 0.2 copy.66
  59.2 3.1 %collective-permute-start = (bf16[2,1024,31]{1,2,0:T(8,128)(2,1)S(1)}, bf16[2,1024,31]{1,2,0:T(8,128)(2,1)S(1)}, u32[]{:S(2)}, u32[]{:S(2)}) collective-permute-start(bf16[2,1024,31]{1,2,0:T(8,128)(2,1)S(1)} %slice.195), channel_id=1, source_target_pairs={{4,0},{8,4},{12,8},{16,12},{20,16},{24,20},{28,24},{32,28},{36,32}... | collective-permute-start | bytes 380936 | tf_op jit(solution)/shard_map/ppermute | solution.py:21
  62.3 0.0 copy-done.7
  62.3 0.3 rev.7
  62.7 0.3 rev.8
  63.0 0.1 convert_reduce_fusion
  63.1 3.5 %collective-permute-done = bf16[2,1024,31]{1,2,0:T(8,128)(2,1)S(1)} collective-permute-done((bf16[2,1024,31]{1,2,0:T(8,128)(2,1)S(1)}, bf16[2,1024,31]{1,2,0:T(8,128)(2,1)S(1)}, u32[]{:S(2)}, u32[]{:S(2)}) %collective-permute-start) | collective-permute-done | bytes 127008 | tf_op jit(solution)/shard_map/ppermute | solution.py:21
  66.6 1.3 %fusion.1 = bf16[2,1024,1024]{2,1,0:T(8,128)(2,1)S(1)} fusion(bf16[2,1024,31]{1,2,0:T(8,128)(2,1)S(1)} %collective-permute-done, bf16[2,1024,128]{1,2,0:T(8,128)(2,1)S(1)} %copy.66, s32[1024]{0:T(1024)S(1)} %add_bitcast_fusion), kind=kOutput, calls=%fused_computation.5 | convolution fusion | flops 668359680 | bytes 4849664 | tf_op jit(solution)/shard_map/xpc,cn->xpn/dot_general | solution.py:206
  67.9 0.8 slice_convert_fusion.7
  68.7 0.0 copy-start.5
  68.8 2.5 %subtract_convert_fusion.1 = (bf16[1,1024,128]{2,1,0:T(8,128)(2,1)S(1)}, f32[1,1024,128]{2,1,0:T(8,128)S(1)}, f32[1,1024,128]{2,1,0:T(8,128)S(1)}) fusion(f32[1,511,128]{2,1,0:T(8,128)S(1)} %bitcast.93, f32[1,513,128]{2,1,0:T(8,128)S(1)} %get-tuple-element.31, f32[1,511,128]{2,1,0:T(8,128)S(1)} %bitcast.91, f32[1,513,128]{2,1,0:T(8,128)S(1)} %get-tuple-element.30, ...), kind=kLoop, calls=%fused_computation.70 | loop fusion | flops 4718592 | bytes 10780672 | tf_op jit(solution)/shard_map/convert_element_type | solution.py:220
  71.3 0.0 copy-start.3
  71.3 0.0 copy-start.2
  71.3 0.1 add_convert_fusion.1
  71.4 0.2 copy.68
  71.6 0.2 copy.67
  71.8 0.0 copy-done.5
  71.8 0.3 convolution_bitcast_fusion
  72.1 0.0 copy-done.3
  72.2 0.4 subtract_convert_fusion
  72.5 0.1 pad_maximum_fusion.3
  72.6 0.0 copy-done.2
  72.6 0.3 convolution_bitcast_fusion.2
  72.9 0.1 fusion.32
  73.0 0.2 fusion.33
  73.1 0.6 copy.71
  73.8 4.0 %all-to-all-start.1 = ((f32[4,8,8,128]{3,2,1,0:T(8,128)}), f32[4,8,8,128]{3,2,1,0:T(8,128)S(1)}, u32[]{:S(2)}, u32[]{:S(2)}) async-start(f32[4,8,8,128]{3,2,1,0:T(8,128)} %copy.71), calls=%async_computation.1 | async-start | bytes 262144 | tf_op jit(solution)/shard_map/all_to_all | solution.py:240
  77.8 0.6 fusion.47
  79.1 3.5 %all-to-all-done.1 = f32[4,8,8,128]{3,2,1,0:T(8,128)S(1)} async-done(((f32[4,8,8,128]{3,2,1,0:T(8,128)}), f32[4,8,8,128]{3,2,1,0:T(8,128)S(1)}, u32[]{:S(2)}, u32[]{:S(2)}) %all-to-all-start.1) | async-done | bytes 131104 | tf_op jit(solution)/shard_map/all_to_all | solution.py:240
  82.7 0.6 copy.101
  (7 shorter events, 0.1 us)
Async XLA Ops:
  0.0 57.4 %copy-start.6 = (bf16[2,8,2,8,1]{3,1,2,4,0:T(8,128)(2,1)S(1)}, bf16[2,8,2,8,1]{3,1,2,4,0:T(8,128)(2,1)}, u32[]{:S(2)}) copy-start(bf16[2,8,2,8,1]{3,1,2,4,0:T(8,128)(2,1)} %constant.70) | copy-start | bytes 1540
  0.0 57.8 %copy-start = (f32[8,128]{0,1:T(8,128)S(1)}, f32[8,128]{0,1:T(8,128)}, u32[]{:S(2)}) copy-start(f32[8,128]{0,1:T(8,128)} %constant.61.clone) | copy-start | bytes 12292
  0.0 57.8 %copy-start.4 = (f32[8,128]{0,1:T(8,128)S(1)}, f32[8,128]{0,1:T(8,128)}, u32[]{:S(2)}) copy-start(f32[8,128]{0,1:T(8,128)} %constant.62.clone) | copy-start | bytes 12292
  3.4 54.8 %copy-start.1 = (bf16[2,128,2,128,1]{3,1,2,4,0:T(8,128)(2,1)S(1)}, bf16[2,128,2,128,1]{3,1,2,4,0:T(8,128)(2,1)}, u32[]{:S(2)}) copy-start(bf16[2,128,2,128,1]{3,1,2,4,0:T(8,128)(2,1)} %constant.69) | copy-start | bytes 393220
  3.4 53.9 %all-to-all-start = ((bf16[128,2,8,128]{3,2,1,0:T(8,128)(2,1)}), bf16[128,2,8,128]{3,2,1,0:T(8,128)(2,1)S(1)}, u32[]{:S(2)}, u32[]{:S(2)}) async-start(bf16[128,2,8,128]{3,2,1,0:T(8,128)(2,1)} %bitcast.99), calls=%async_computation | async-start | bytes 1048576 | tf_op jit(solution)/shard_map/all_to_all | solution.py:193
  57.4 4.9 %copy-start.7 = (s32[4,16]{1,0:T(4,128)S(1)}, s32[4,16]{1,0:T(4,128)}, u32[]{:S(2)}) copy-start(s32[4,16]{1,0:T(4,128)} %param.25) | copy-start | bytes 772
  59.2 7.4 %collective-permute-start = (bf16[2,1024,31]{1,2,0:T(8,128)(2,1)S(1)}, bf16[2,1024,31]{1,2,0:T(8,128)(2,1)S(1)}, u32[]{:S(2)}, u32[]{:S(2)}) collective-permute-start(bf16[2,1024,31]{1,2,0:T(8,128)(2,1)S(1)} %slice.195), channel_id=1, source_target_pairs={{4,0},{8,4},{12,8},{16,12},{20,16},{24,20},{28,24},{32,28},{36,32}... | collective-permute-start | bytes 380936 | tf_op jit(solution)/shard_map/ppermute | solution.py:21
  68.7 3.0 %copy-start.5 = (bf16[2,8,2,8,1]{3,1,2,4,0:T(8,128)(2,1)S(1)}, bf16[2,8,2,8,1]{3,1,2,4,0:T(8,128)(2,1)}, u32[]{:S(2)}) copy-start(bf16[2,8,2,8,1]{3,1,2,4,0:T(8,128)(2,1)} %constant.68) | copy-start | bytes 1540
  71.3 0.9 %copy-start.3 = (f32[8,128]{0,1:T(8,128)S(1)}, f32[8,128]{0,1:T(8,128)}, u32[]{:S(2)}) copy-start(f32[8,128]{0,1:T(8,128)} %constant.65.clone) | copy-start | bytes 12292
  71.3 1.3 %copy-start.2 = (bf16[2,128,2,128,1]{3,1,2,4,0:T(8,128)(2,1)S(1)}, bf16[2,128,2,128,1]{3,1,2,4,0:T(8,128)(2,1)}, u32[]{:S(2)}) copy-start(bf16[2,128,2,128,1]{3,1,2,4,0:T(8,128)(2,1)} %constant.67) | copy-start | bytes 393220
  73.8 8.8 %all-to-all-start.1 = ((f32[4,8,8,128]{3,2,1,0:T(8,128)}), f32[4,8,8,128]{3,2,1,0:T(8,128)S(1)}, u32[]{:S(2)}, u32[]{:S(2)}) async-start(f32[4,8,8,128]{3,2,1,0:T(8,128)} %copy.71), calls=%async_computation.1 | async-start | bytes 262144 | tf_op jit(solution)/shard_map/all_to_all | solution.py:240

commit v21 on v18

--- a/solution.py
+++ b/solution.py
@@ -191,8 +191,9 @@
     width = length // devices
     assert compressed.shape[0] == devices and compressed.shape[3] == width
     turned = lax.all_to_all(compressed, "wide", split_axis=0, concat_axis=2, tiled=True)[0]
-    doppler = pulse_transform(turned, PUL_DEV, -1).astype(jnp.bfloat16)
-    rim = passed_along(doppler[:, :, :HALO], "wide", -1)
+    spectra = pulse_transform(turned, PUL_DEV, -1)
+    doppler = spectra.astype(jnp.bfloat16)
+    rim = passed_along(spectra[:, :, :HALO].astype(jnp.bfloat16), "wide", -1)
     extended = jnp.concatenate([doppler, rim], axis=2)
     pulses = extended.shape[1]
     columns = jnp.arange(width + HALO, dtype=jnp.int32)

time: 84 us -> 84 us (level)
  no operation moved by 1% of the time
where the time goes in v21:
time: 84 us; the launch traced here: 83.6 us
  waiting for transfers between devices  34.8 us (41%)
  starting transfers between devices  27.8 us (33%)
  other arithmetic  8.84 us (11%)
  local copies, waits for them, and re-layouts  4.87 us (6%)
  Pallas kernels  3.4 us (4%)
  matrix products  2.84 us (3%)
  between operations  0.96 us (1%)
    all_to_all x1, waiting for transfers between devices, per_device(): lax.all_to_all(compressed, 'wide', split_axis=0, concat_axis=2, tiled=True)  27.8 us
    all_to_all x1, starting transfers between devices, per_device(): lax.all_to_all(compressed, 'wide', split_axis=0, concat_axis=2, tiled=True)  20.7 us
    all_to_all x1, starting transfers between devices, per_device(): lax.all_to_all(partial, 'narrow', split_axis=0, concat_axis=0, tiled=True)  4.01 us
    all_to_all x1, waiting for transfers between devices, per_device(): lax.all_to_all(partial, 'narrow', split_axis=0, concat_axis=0, tiled=True)  3.54 us
    ppermute x1, waiting for transfers between devices, passed_along(): return lax.ppermute(shard, axis, pairs)  3.48 us
    pallas_call x1, Pallas kernels, range_compress(): pl.pallas_call(range_kernel, in_specs=[whole] * 8, out_specs=whole, out_s...  3.4 us
    ppermute x1, starting transfers between devices, passed_along(): return lax.ppermute(shard, axis, pairs)  3.11 us
    convert_element_type x1, other arithmetic, per_device(): (moved_real * phase_cos - moved_imag * phase_sin).astype(jnp.bfloat16)  2.49 us
  transfers between devices with their start and end apart: 3, of which 3 were waited for; matrix products, arithmetic and copies ran while one was open for 8% of the time, Pallas kernels for 0%

profile of v21, /device:TPU:1, one launch (start us, length us, event | category | flops | bytes accessed | tf_op | source)
XLA Modules:
  0.0 83.6 jit_solution(183634161887050344)
XLA Ops:
  0.0 0.0 copy-start.6
  0.0 0.0 copy-start
  0.0 0.0 copy-start.4
  0.0 3.4 %shard_map.190 = bf16[2048,128]{1,0:T(8,128)(2,1)} custom-call(bf16[2,1024,128]{2,1,0:T(8,128)(2,1)} %bitcast.107, bf16[2,4096]{1,0:T(2,128)(2,1)} %replica_ref.1, bf16[256,256]{1,0:T(8,128)(2,1)} %constant.55.clone.fwd_ref.inv_t_ref, bf16[256,256]{1,0:T(8,128)(2,1)} %constant.56.clone.fwd_t_ref.inv_ref, bf16[256,256]{1,0:T(8,128)(2,1)} %constant.56.clone.fwd_t_ref.inv_ref, ...), custom_call_target="tpu_custom_call" | custom-call | flops 603979776 | bytes 1048576 | tf_op jit(solution)/shard_map/pallas_call | solution.py:137
  3.4 0.0 copy-start.1
  3.4 20.7 %all-to-all-start = ((bf16[128,2,8,128]{3,2,1,0:T(8,128)(2,1)}), bf16[128,2,8,128]{3,2,1,0:T(8,128)(2,1)S(1)}, u32[]{:S(2)}, u32[]{:S(2)}) async-start(bf16[128,2,8,128]{3,2,1,0:T(8,128)(2,1)} %bitcast.98), calls=%async_computation | async-start | bytes 1048576 | tf_op jit(solution)/shard_map/all_to_all | solution.py:193
  24.1 0.7 iota_add_fusion
  24.8 1.2 %fusion.52 = (f32[1,1024]{1,0:T(1,128)S(1)}, f32[1,1024]{1,0:T(1,128)S(1)}, f32[1,1024]{1,0:T(1,128)S(1)}, f32[1,1024]{1,0:T(1,128)S(1)}, f32[1,1024]{1,0:T(1,12...) fusion(f32[8,1024]{1,0:T(8,128)} %param.22), kind=kLoop, calls=%fused_computation.107 | loop fusion | bytes 65536 | tf_op jit(solution)/shard_map/slice | solution.py:208
  26.1 0.8 broadcast_divide_fusion
  26.8 1.7 %divide_cosine_fusion = (f32[1,513,128]{2,1,0:T(8,128)S(1)}, f32[1,513,128]{2,1,0:T(8,128)S(1)}) fusion(f32[128]{0:T(128)} %param.24, f32[513]{0:T(1024)S(1)} %fusion.40), kind=kLoop, calls=%fused_computation.80 | loop fusion | flops 65664 | bytes 527876 | tf_op jit(solution)/shard_map/cos | solution.py:216
  28.5 1.0 %slice_cosine_fusion = (f32[511,128]{1,0:T(8,128)S(1)}, f32[511,128]{1,0:T(8,128)S(1)}) fusion(f32[513,128]{1,0:T(8,128)S(1)} %broadcast_divide_fusion), kind=kLoop, calls=%fused_computation.78 | loop fusion | bytes 784896 | tf_op jit(solution)/shard_map/cos | solution.py:216
  29.5 27.8 %all-to-all-done = bf16[128,2,8,128]{3,2,1,0:T(8,128)(2,1)S(1)} async-done(((bf16[128,2,8,128]{3,2,1,0:T(8,128)(2,1)}), bf16[128,2,8,128]{3,2,1,0:T(8,128)(2,1)S(1)}, u32[]{:S(2)}, u32[]{:S(2)}) %all-to-all-start) | async-done | bytes 524320 | tf_op jit(solution)/shard_map/all_to_all | solution.py:193
  57.4 0.0 copy-start.7
  57.4 0.0 copy-done.6
  57.4 0.4 convolution_bitcast_fusion.1
  57.8 0.0 copy-done
  57.8 0.0 copy-done.4
  57.8 0.4 subtract_convert_fusion.2
  58.2 0.1 pad_maximum_fusion
  58.3 0.0 copy-done.1
  58.3 0.3 fusion
  58.6 0.3 copy.86
  58.9 0.2 copy.53
  59.2 3.1 %collective-permute-start = (bf16[2,1024,31]{1,2,0:T(8,128)(2,1)S(1)}, bf16[2,1024,31]{1,2,0:T(8,128)(2,1)S(1)}, u32[]{:S(2)}, u32[]{:S(2)}) collective-permute-start(bf16[2,1024,31]{1,2,0:T(8,128)(2,1)S(1)} %slice.195), channel_id=1, source_target_pairs={{4,0},{8,4},{12,8},{16,12},{20,16},{24,20},{28,24},{32,28},{36,32}... | collective-permute-start | bytes 380936 | tf_op jit(solution)/shard_map/ppermute | solution.py:21
  62.3 0.0 copy-done.7
  62.3 0.3 rev.7
  62.7 0.3 rev.8
  63.0 0.1 convert_reduce_fusion
  63.1 3.5 %collective-permute-done = bf16[2,1024,31]{1,2,0:T(8,128)(2,1)S(1)} collective-permute-done((bf16[2,1024,31]{1,2,0:T(8,128)(2,1)S(1)}, bf16[2,1024,31]{1,2,0:T(8,128)(2,1)S(1)}, u32[]{:S(2)}, u32[]{:S(2)}) %collective-permute-start) | collective-permute-done | bytes 127008 | tf_op jit(solution)/shard_map/ppermute | solution.py:21
  66.6 1.3 %fusion.1 = bf16[2,1024,1024]{2,1,0:T(8,128)(2,1)S(1)} fusion(bf16[2,1024,31]{1,2,0:T(8,128)(2,1)S(1)} %collective-permute-done, bf16[2,1024,128]{1,2,0:T(8,128)(2,1)S(1)} %copy.53, s32[1024]{0:T(1024)S(1)} %add_bitcast_fusion), kind=kOutput, calls=%fused_computation.5 | convolution fusion | flops 668359680 | bytes 4849664 | tf_op jit(solution)/shard_map/xpc,cn->xpn/dot_general | solution.py:206
  67.9 0.8 slice_convert_fusion.7
  68.7 0.0 copy-start.5
  68.8 2.5 %subtract_convert_fusion.1 = (bf16[1,1024,128]{2,1,0:T(8,128)(2,1)S(1)}, f32[1,1024,128]{2,1,0:T(8,128)S(1)}, f32[1,1024,128]{2,1,0:T(8,128)S(1)}) fusion(f32[1,511,128]{2,1,0:T(8,128)S(1)} %bitcast.92, f32[1,513,128]{2,1,0:T(8,128)S(1)} %get-tuple-element.31, f32[1,511,128]{2,1,0:T(8,128)S(1)} %bitcast.90, f32[1,513,128]{2,1,0:T(8,128)S(1)} %get-tuple-element.30, ...), kind=kLoop, calls=%fused_computation.70 | loop fusion | flops 4718592 | bytes 10780672 | tf_op jit(solution)/shard_map/convert_element_type | solution.py:220
  71.3 0.0 copy-start.3
  71.3 0.0 copy-start.2
  71.3 0.1 add_convert_fusion.1
  71.4 0.2 copy.55
  71.6 0.2 copy.54
  71.8 0.0 copy-done.5
  71.8 0.3 convolution_bitcast_fusion
  72.1 0.0 copy-done.3
  72.2 0.4 subtract_convert_fusion
  72.5 0.1 pad_maximum_fusion.3
  72.6 0.0 copy-done.2
  72.6 0.3 convolution_bitcast_fusion.2
  72.9 0.1 fusion.8
  73.0 0.2 copy.57
  73.1 0.1 convert_element_type.75
  73.3 0.2 fusion.32
  73.4 0.6 copy.59
  74.1 4.0 %all-to-all-start.1 = ((f32[4,64,128]{2,1,0:T(8,128)}), f32[4,64,128]{2,1,0:T(8,128)S(1)}, u32[]{:S(2)}, u32[]{:S(2)}) async-start(f32[4,64,128]{2,1,0:T(8,128)} %copy.59), calls=%async_computation.1 | async-start | bytes 262144 | tf_op jit(solution)/shard_map/all_to_all | solution.py:238
  78.1 0.6 fusion.47
  79.4 3.5 %all-to-all-done.1 = f32[4,64,128]{2,1,0:T(8,128)S(1)} async-done(((f32[4,64,128]{2,1,0:T(8,128)}), f32[4,64,128]{2,1,0:T(8,128)S(1)}, u32[]{:S(2)}, u32[]{:S(2)}) %all-to-all-start.1) | async-done | bytes 131104 | tf_op jit(solution)/shard_map/all_to_all | solution.py:238
  82.9 0.6 divide_bitcast_fusion
  (6 shorter events, 0.1 us)
Async XLA Ops:
  0.0 57.4 %copy-start.6 = (bf16[2,8,2,8,1]{3,1,2,4,0:T(8,128)(2,1)S(1)}, bf16[2,8,2,8,1]{3,1,2,4,0:T(8,128)(2,1)}, u32[]{:S(2)}) copy-start(bf16[2,8,2,8,1]{3,1,2,4,0:T(8,128)(2,1)} %constant.70) | copy-start | bytes 1540
  0.0 57.8 %copy-start = (f32[8,128]{0,1:T(8,128)S(1)}, f32[8,128]{0,1:T(8,128)}, u32[]{:S(2)}) copy-start(f32[8,128]{0,1:T(8,128)} %constant.61.clone) | copy-start | bytes 12292
  0.0 57.8 %copy-start.4 = (f32[8,128]{0,1:T(8,128)S(1)}, f32[8,128]{0,1:T(8,128)}, u32[]{:S(2)}) copy-start(f32[8,128]{0,1:T(8,128)} %constant.62.clone) | copy-start | bytes 12292
  3.4 54.8 %copy-start.1 = (bf16[2,128,2,128,1]{3,1,2,4,0:T(8,128)(2,1)S(1)}, bf16[2,128,2,128,1]{3,1,2,4,0:T(8,128)(2,1)}, u32[]{:S(2)}) copy-start(bf16[2,128,2,128,1]{3,1,2,4,0:T(8,128)(2,1)} %constant.69) | copy-start | bytes 393220
  3.4 53.9 %all-to-all-start = ((bf16[128,2,8,128]{3,2,1,0:T(8,128)(2,1)}), bf16[128,2,8,128]{3,2,1,0:T(8,128)(2,1)S(1)}, u32[]{:S(2)}, u32[]{:S(2)}) async-start(bf16[128,2,8,128]{3,2,1,0:T(8,128)(2,1)} %bitcast.98), calls=%async_computation | async-start | bytes 1048576 | tf_op jit(solution)/shard_map/all_to_all | solution.py:193
  57.4 4.9 %copy-start.7 = (s32[4,16]{1,0:T(4,128)S(1)}, s32[4,16]{1,0:T(4,128)}, u32[]{:S(2)}) copy-start(s32[4,16]{1,0:T(4,128)} %param.25) | copy-start | bytes 772
  59.2 7.4 %collective-permute-start = (bf16[2,1024,31]{1,2,0:T(8,128)(2,1)S(1)}, bf16[2,1024,31]{1,2,0:T(8,128)(2,1)S(1)}, u32[]{:S(2)}, u32[]{:S(2)}) collective-permute-start(bf16[2,1024,31]{1,2,0:T(8,128)(2,1)S(1)} %slice.195), channel_id=1, source_target_pairs={{4,0},{8,4},{12,8},{16,12},{20,16},{24,20},{28,24},{32,28},{36,32}... | collective-permute-start | bytes 380936 | tf_op jit(solution)/shard_map/ppermute | solution.py:21
  68.7 3.0 %copy-start.5 = (bf16[2,8,2,8,1]{3,1,2,4,0:T(8,128)(2,1)S(1)}, bf16[2,8,2,8,1]{3,1,2,4,0:T(8,128)(2,1)}, u32[]{:S(2)}) copy-start(bf16[2,8,2,8,1]{3,1,2,4,0:T(8,128)(2,1)} %constant.68) | copy-start | bytes 1540
  71.3 0.9 %copy-start.3 = (f32[8,128]{0,1:T(8,128)S(1)}, f32[8,128]{0,1:T(8,128)}, u32[]{:S(2)}) copy-start(f32[8,128]{0,1:T(8,128)} %constant.65.clone) | copy-start | bytes 12292
  71.3 1.3 %copy-start.2 = (bf16[2,128,2,128,1]{3,1,2,4,0:T(8,128)(2,1)S(1)}, bf16[2,128,2,128,1]{3,1,2,4,0:T(8,128)(2,1)}, u32[]{:S(2)}) copy-start(bf16[2,128,2,128,1]{3,1,2,4,0:T(8,128)(2,1)} %constant.67) | copy-start | bytes 393220
  74.1 8.8 %all-to-all-start.1 = ((f32[4,64,128]{2,1,0:T(8,128)}), f32[4,64,128]{2,1,0:T(8,128)S(1)}, u32[]{:S(2)}, u32[]{:S(2)}) async-start(f32[4,64,128]{2,1,0:T(8,128)} %copy.59), calls=%async_computation.1 | async-start | bytes 262144 | tf_op jit(solution)/shard_map/all_to_all | solution.py:238
